TPU v7x, 256 devices: a whole 4x4x8 slice. The times are simulated.
256 devices in a mesh: agent: 4 (over y), tile: 64 (over x, z, core).
Axes of the slice: x: 4, y: 4, z: 8, core: 2. Of those that a mesh axis runs over, the one named last changes fastest.
Arguments:
- feats: bfloat16 [32, 256, 24, 256], P('agent', 'tile'), may hold values from -18 to 18
- types: int32 [32], replicated, may hold values from 0 to 1
- valid: int32 [32], replicated, may hold values 0 or 1
- offsets: int32 [32, 2], replicated, may hold values from -2 to 2
- w_qkv: bfloat16 [2, 256, 768], replicated, may hold values from -0.375 to 0.375
- w_out: bfloat16 [2, 256, 256], replicated, may hold values from -0.375 to 0.375
- d_out: bfloat16 [32, 256, 24, 256], P('agent', 'tile'), may hold values from -6 to 6
Outputs:
- d_feats: bfloat16 [32, 256, 24, 256], P('agent', 'tile')
- g_qkv: float32 [2, 256, 768], P(None, 'tile')
- g_out: float32 [2, 256, 256], P(None, 'tile')
All inputs are finite; a program needn't handle non-finite values.
Results may differ from a plain program's by a relative error of at most 0.012.
The roundings to bfloat16 on the way count: a program that leaves them out, or rounds other values in their place, can miss the bound.
Values may be sent and summed in bfloat16 or wider, within the bound.
No kernel may reach another device: no remote copies, remote signals or barrier semaphores. Data moves between devices by JAX's collectives and lax.ppermute only.
A program may use at most 128 MiB of HBM per device.

v0:
```python
import math

import jax
import jax.numpy as jnp
from jax import lax
from jax.sharding import PartitionSpec as P

HEADS = 8
MAXOFF = 2


def with_halo(cells, sides, width):
    for axis, dim in sides:
        count = lax.axis_size(axis)
        ends = count - 1
        head = lax.slice_in_dim(cells, 0, width, axis=dim)
        tail = lax.slice_in_dim(cells, cells.shape[dim] - width, cells.shape[dim], axis=dim)
        cells = jnp.concatenate(
            [
                lax.ppermute(tail, axis, [(i, (i + 1) % count) for i in range(ends)]),
                cells,
                lax.ppermute(head, axis, [((i + 1) % count, i) for i in range(ends)]),
            ],
            axis=dim,
        )
    return cells


def relocate(rimmed, offsets, direction):
    padded = jnp.pad(rimmed, ((0, 0), (0, 0), (MAXOFF, MAXOFF), (0, 0)))
    row_count = rimmed.shape[1] - 2 * MAXOFF
    col_count = rimmed.shape[2]

    def pick_one(plane, offset):
        row_start = MAXOFF + direction * offset[0]
        col_start = MAXOFF + direction * offset[1]
        return lax.dynamic_slice(
            plane, (row_start, col_start, jnp.int32(0)), (row_count, col_count, plane.shape[2])
        )

    return jax.vmap(pick_one)(padded, offsets)


def body(feats, types, valid, offsets, w_qkv, w_out, d_out):
    f32 = jnp.float32
    bf16 = jnp.bfloat16
    highest = lax.Precision.HIGHEST
    own_count, row_count, col_count, channels = feats.shape
    agents = own_count * lax.axis_size("agent")
    first_agent = lax.axis_index("agent") * own_count
    own_offsets = lax.dynamic_slice_in_dim(offsets, first_agent, own_count, 0)
    rimmed = with_halo(feats, (("tile", 1),), MAXOFF)
    warped = relocate(rimmed, own_offsets, 1)
    cell_count = row_count * col_count
    head_size = channels // HEADS
    score_scale = head_size ** (-0.5)
    all_hot = (types[:, None] == jnp.arange(2)[None, :]).astype(bf16)
    flat_feats = warped.reshape(own_count, cell_count, channels)
    flat_grads = d_out.reshape(own_count, cell_count, channels)
    all_feats, all_grads = (
        lax.all_to_all(flat_feats, "agent", split_axis=1, concat_axis=0, tiled=True),
        lax.all_to_all(flat_grads, "agent", split_axis=1, concat_axis=0, tiled=True),
    )
    part_cells = all_feats.shape[1]
    wqkv_all = jnp.take(w_qkv, types, axis=0)
    wout_all = jnp.take(w_out, types, axis=0)
    qkv = jnp.einsum("bgc,bce->bge", all_feats, wqkv_all, preferred_element_type=f32).astype(bf16)
    query_heads = qkv[..., :channels].reshape(agents, part_cells, HEADS, head_size)
    key_heads = qkv[..., channels : 2 * channels].reshape(agents, part_cells, HEADS, head_size)
    value_heads = qkv[..., 2 * channels :].reshape(agents, part_cells, HEADS, head_size)
    scores = (
        jnp.einsum("aghd,bghd->ghab", query_heads, key_heads, preferred_element_type=f32)
        * score_scale
    )
    agent_ids = jnp.arange(agents)
    allowed = (valid[None, :] == 1) | (agent_ids[:, None] == agent_ids[None, :])
    raised = jnp.where(allowed, jnp.exp(scores), f32(0.0))
    attn_prob = raised / jnp.sum(raised, axis=-1, keepdims=True)
    prob_low = attn_prob.astype(bf16)
    attended = (
        jnp.einsum("ghab,bghd->aghd", prob_low, value_heads, preferred_element_type=f32)
        .astype(bf16)
        .reshape(agents, part_cells, channels)
    )
    d_attended = jnp.einsum("age,ace->agc", all_grads, wout_all, preferred_element_type=f32).astype(
        bf16
    )
    attended_typed = all_hot[:, :, None, None] * attended[:, None]
    raw_out = jnp.einsum("atgc,age->tce", attended_typed, all_grads, preferred_element_type=f32)
    attended_heads = d_attended.reshape(agents, part_cells, HEADS, head_size)
    prob_grad = jnp.einsum(
        "aghd,bghd->ghab", attended_heads, value_heads, preferred_element_type=f32
    )
    score_grad = (
        attn_prob
        * (prob_grad - jnp.sum(attn_prob * prob_grad, axis=-1, keepdims=True))
        * score_scale
    ).astype(bf16)
    d_query = (
        jnp.einsum("ghab,bghd->aghd", score_grad, key_heads, preferred_element_type=f32)
        .astype(bf16)
        .reshape(agents, part_cells, channels)
    )
    groups_n = agents // own_count
    grad_blocks = score_grad.reshape(part_cells, HEADS, groups_n, own_count, agents)
    prob_blocks = prob_low.reshape(part_cells, HEADS, groups_n, own_count, agents)
    query_blocks = query_heads.reshape(groups_n, own_count, part_cells, HEADS, head_size)
    dattn_blocks = attended_heads.reshape(groups_n, own_count, part_cells, HEADS, head_size)
    key_parts = jnp.einsum(
        "ghnyb,nyghd->nbghd", grad_blocks, query_blocks, preferred_element_type=f32
    ).astype(bf16)
    value_parts = jnp.einsum(
        "ghnyb,nyghd->nbghd", prob_blocks, dattn_blocks, preferred_element_type=f32
    ).astype(bf16)
    key_sum = jnp.sum(key_parts.astype(f32), axis=0).reshape(agents, part_cells, channels)
    value_sum = jnp.sum(value_parts.astype(f32), axis=0).reshape(agents, part_cells, channels)
    d_qkv = jnp.concatenate([d_query.astype(f32), key_sum, value_sum], axis=-1)
    d_part = jnp.einsum("bge,bce->bgc", d_qkv, wqkv_all.astype(f32), precision=highest).astype(bf16)
    returned = lax.all_to_all(d_part, "agent", split_axis=0, concat_axis=1, tiled=True)
    d_warped = returned.reshape(own_count, row_count, col_count, channels)
    type_wide = all_hot.astype(f32)
    raw_qkv = jnp.einsum(
        "bt,bgc,bge->tce", type_wide, all_feats.astype(f32), d_qkv, precision=highest
    )
    rimmed_grad = with_halo(d_warped, (("tile", 1),), MAXOFF)
    d_feats = relocate(rimmed_grad, own_offsets, -1)
    norm_limit = math.sqrt(8.0 * channels * channels)
    share_rows = channels // lax.axis_size("tile")
    total_qkv, total_out = lax.psum((raw_qkv, raw_out), ("agent", "tile"))
    square_sum = jnp.sum(total_qkv * total_qkv) + jnp.sum(total_out * total_out)
    share_start = lax.axis_index("tile") * share_rows
    share_qkv = lax.dynamic_slice_in_dim(total_qkv, share_start, share_rows, 1)
    share_out = lax.dynamic_slice_in_dim(total_out, share_start, share_rows, 1)
    factor = norm_limit / jnp.maximum(jnp.sqrt(square_sum), norm_limit)
    return (d_feats, share_qkv * factor, share_out * factor)


def solution(mesh):
    placed = (
        P("agent", "tile", None, None),
        P(),
        P(),
        P(),
        P(),
        P(),
        P("agent", "tile", None, None),
    )
    return jax.shard_map(
        body,
        mesh=mesh,
        in_specs=placed,
        out_specs=(P("agent", "tile", None, None), P(None, "tile", None), P(None, "tile", None)),
        check_vma=False,
    )
```

profile of v0, /device:TPU:2, one launch (start us, length us, event | category | flops | bytes accessed | tf_op | source)
XLA Modules:
  0.0 441.9 jit_solution(2251199737392983344)
XLA Ops:
  7.2 0.0 copy-start
  7.2 2.0 copy.64
  9.3 4.5 %all-to-all-start.1 = ((bf16[8,96,256]{2,0,1:T(8,128)(2,1)}), bf16[8,96,256]{2,0,1:T(8,128)(2,1)S(1)}, u32[]{:S(2)}, u32[]{:S(2)}) async-start(bf16[8,96,256]{2,0,1:T(8,128)(2,1)} %bitcast.6), calls=%async_computation.1 | async-start | bytes 786432 | tf_op jit(solution)/shard_map/all_to_all | solution.py:62
  13.7 1.2 copy.57
  15.0 1.9 collective-permute-start
  16.9 6.9 %collective-permute-start.1 = (bf16[8,2,24,256]{3,0,2,1:T(8,128)(2,1)S(1)}, bf16[8,2,24,256]{3,0,2,1:T(8,128)(2,1)S(1)}, u32[]{:S(2)}, u32[]{:S(2)}) collective-permute-start(bf16[8,2,24,256]{3,0,2,1:T(8,128)(2,1)S(1)} %get-tuple-element.20), channel_id=1, source_target_pairs={{1,0},{2,1},{3,2},{4,3},{5,4},{6,5},{7,6},{8,7},{9,8},{10,9},{11,1... | collective-permute-start | bytes 589832 | tf_op jit(solution)/shard_map/ppermute | solution.py:22
  23.9 0.1 constant_dynamic-slice_fusion
  24.0 0.1 fusion.46
  24.1 2.8 gather_fusion.1
  26.8 6.6 %gather_fusion = bf16[32,256,768]{2,1,0:T(8,128)(2,1)} fusion(bf16[2,256,768]{2,1,0:T(8,128)(2,1)S(1)} %copy-done, s32[1024]{0:T(1024)S(1)} %pad_clamp_fusion), kind=kCustom, calls=%fused_computation | custom fusion | bytes 25165952 | tf_op jit(solution)/shard_map/jit(_take)/gather | solution.py:65
  33.4 0.0 collective-permute-done
  33.5 0.0 collective-permute-done.1
  33.5 0.1 fusion.40
  33.5 2.4 gather_fusion.2
  36.0 0.0 all-to-all-done.1
  36.0 4.5 %all-to-all-start = ((bf16[8,96,256]{2,0,1:T(8,128)(2,1)}), bf16[8,96,256]{2,0,1:T(8,128)(2,1)S(1)}, u32[]{:S(2)}, u32[]{:S(2)}) async-start(bf16[8,96,256]{2,0,1:T(8,128)(2,1)} %bitcast.1), calls=%async_computation | async-start | bytes 786432 | tf_op jit(solution)/shard_map/all_to_all | solution.py:61
  40.5 0.1 copy.66
  40.6 3.5 fusion.33
  44.0 1.8 reshape_reshape.7
  45.9 1.8 reshape.76
  47.6 0.2 all-to-all-done
  47.9 0.1 copy.61
  48.0 6.7 %fusion.25 = bf16[32,24,768]{2,1,0:T(8,128)(2,1)S(1)} fusion(bf16[32,24,256]{2,1,0:T(8,128)(2,1)S(1)} %bitcast.74, bf16[32,256,768]{2,1,0:T(8,128)(2,1)} %gather_fusion, pred[32]{0:T(512)(128)(4,1)S(1)} %compare_and_fusion), kind=kOutput, calls=%fused_computation.39 | convolution fusion | flops 308871168 | bytes 14155808 | tf_op jit(solution)/shard_map/bgc,bce->bge/dot_general | solution.py:67
  54.6 0.1 fusion.66
  54.7 1.8 reshape_reshape.6
  56.5 1.9 reshape.74
  58.4 1.8 copy.96
  60.2 0.9 copy.95
  61.1 3.8 fusion.10
  64.9 1.7 copy-done.6
  66.6 0.8 fusion.64
  67.5 1.6 copy.75
  69.0 3.3 convolution_convert_fusion
  72.3 2.9 fusion.21
  75.2 8.4 %fusion.15 = f32[24,8,32,32]{3,2,1,0:T(8,128)} fusion(bf16[32,24,8,32]{0,3,2,1:T(8,128)(2,1)S(1)} %bitcast.73, f32[24,8,32,32]{2,3,1,0:T(8,128)} %fusion.21, f32[24,8,32,32]{2,3,1,0:T(8,128)} %copy-done.6, f32[24,8,32]{2,1,0:T(8,128)S(1)} %get-tuple-element.23, pred[32,32]{0,1:T(8,128)(4,1)S(1)} %fusion.46), kind=kOutput, calls=%fused_computation.28 | convolution fusion | flops 15144991 | bytes 2778112 | tf_op jit(solution)/shard_map/ghab,bghd->aghd/dot_general | solution.py:100
  83.6 7.8 %multiply_convert_fusion = bf16[24,8,32,32]{2,3,1,0:T(8,128)(2,1)} fusion(f32[24,8,32,32]{2,3,1,0:T(8,128)} %fusion.21, f32[24,8,32]{2,1,0:T(8,128)S(1)} %get-tuple-element.23, f32[24,8,32,32]{2,3,1,0:T(8,128)} %copy-done.6, pred[32,32]{0,1:T(8,128)(4,1)S(1)} %fusion.46), kind=kOutput, calls=%fused_computation.15 | output fusion | flops 2168863 | bytes 1991680 | tf_op jit(solution)/shard_map/sub | solution.py:96
  91.4 4.5 %convert_reduce_fusion = f32[24,8,32,32]{3,2,1,0:T(8,128)} fusion(bf16[4,8,24,8,32]{4,3,2,1,0:T(8,128)(2,1)S(1)} %copy-done.8, bf16[24,8,32,32]{3,2,1,0:T(8,128)(2,1)S(1)} %copy-done.7), kind=kOutput, calls=%fused_computation.7 | convolution fusion | flops 14745600 | bytes 1572864 | tf_op jit(solution)/shard_map/ghnyb,nyghd->nbghd/dot_general | solution.py:112
  96.0 2.5 copy.94
  98.5 0.6 copy.84
  99.1 1.9 copy.71
  101.0 5.6 %convert_reduce_fusion.1 = f32[24,8,32,32]{3,2,1,0:T(8,128)} fusion(bf16[4,8,24,8,32]{4,3,2,1,0:T(8,128)(2,1)} %reshape_reshape.6, bf16[24,8,32,32]{3,2,1,0:T(8,128)(2,1)S(1)} %copy.71), kind=kOutput, calls=%fused_computation.8 | convolution fusion | flops 14745600 | bytes 1572864 | tf_op jit(solution)/shard_map/ghnyb,nyghd->nbghd/dot_general | solution.py:109
  106.6 2.4 copy.93
  109.0 2.4 copy.79
  111.4 13.3 %fusion.16 = f32[32,768,256]{2,1,0:T(8,128)} fusion(bf16[32,24,256]{2,1,0:T(8,128)(2,1)S(1)} %bitcast.75, f32[32,24,256]{2,1,0:T(8,128)S(1)} %copy.94, f32[32,24,256]{2,1,0:T(8,128)S(1)} %copy.93, f32[32,24,256]{2,1,0:T(8,128)S(1)} %copy.79), kind=kOutput, calls=%fused_computation.29 | convolution fusion | flops 1813118976 | bytes 27918336 | tf_op jit(solution)/shard_map/bt,bgc,bge->tce/dot_general | solution.py:122
  124.7 33.8 %fusion.26 = f32[2,256,768]{1,0,2:T(2,128)} fusion(f32[32,768,256]{2,1,0:T(8,128)} %fusion.16, s32[32]{0:T(128)S(1)} %copy-done.12), kind=kOutput, calls=%fused_computation.40 | convolution fusion | flops 150995008 | bytes 26738816 | tf_op jit(solution)/shard_map/bt,bgc,bge->tce/dot_general | solution.py:122
  158.6 1.3 convolution_bitcast_fusion
  159.9 0.0 all-reduce.5.cloned.1.call-update
  159.9 12.5 %fusion.29 = bf16[32,24,256]{2,1,0:T(8,128)(2,1)S(1)} fusion(bf16[32,256,768]{2,1,0:T(8,128)(2,1)} %gather_fusion, pred[32]{0:T(512)(128)(4,1)S(1)} %compare_and_fusion, f32[32,24,256]{2,1,0:T(8,128)S(1)} %copy.94, f32[32,24,256]{2,1,0:T(8,128)S(1)} %copy.93, f32[32,24,256]{2,1,0:T(8,128)S(1)} %copy.79), kind=kOutput, calls=%fused_computation.41 | convolution fusion | flops 1819607040 | bytes 15335456 | tf_op jit(solution)/shard_map/bge,bce->bgc/dot_general | solution.py:118
  172.4 11.8 %all_to_all.51 = bf16[32,24,256]{2,1,0:T(8,128)(2,1)S(1)} all-to-all(bf16[32,24,256]{2,1,0:T(8,128)(2,1)S(1)} %fusion.29), channel_id=1, replica_groups=mesh['agent'=4,'tile'=64] {'agent'}, dimensions={0} | all-to-all | bytes 786432 | tf_op jit(solution)/shard_map/all_to_all | solution.py:119
  184.2 0.1 copy.120
  184.3 1.9 collective-permute-start.2
  186.2 6.0 %collective-permute-start.3 = (bf16[8,2,24,256]{3,0,2,1:T(8,128)(2,1)S(1)}, bf16[8,2,24,256]{3,0,2,1:T(8,128)(2,1)S(1)}, u32[]{:S(2)}, u32[]{:S(2)}) collective-permute-start(bf16[8,2,24,256]{3,0,2,1:T(8,128)(2,1)S(1)} %get-tuple-element.18), channel_id=1, source_target_pairs={{1,0},{2,1},{3,2},{4,3},{5,4},{6,5},{7,6},{8,7},{9,8},{10,9},{11,1... | collective-permute-start | bytes 589832 | tf_op jit(solution)/shard_map/ppermute | solution.py:22
  192.3 1.4 collective-permute-done.2
  193.7 1.8 collective-permute-done.3
  195.4 0.1 select_maximum_fusion
  195.5 0.0 copy-start.1
  195.5 1.7 gather_fusion.3
  197.2 0.8 copy.86
  198.0 225.5 %all-reduce.5.cloned.1.call-done = (f32[2,256,768]{1,0,2:T(2,128)}, f32[2,256,256]{2,1,0:T(8,128)}) async-done(((f32[2,256,768]{1,0,2:T(2,128)}, f32[2,256,256]{2,1,0:T(8,128)}), (f32[2,256,768]{1,0,2:T(2,128)}, f32[2,256,256]{2,1,0:T(8,128)})) %all-reduce.5.cloned.1.call-update) | async-done | bytes 2097168 | tf_op jit(solution)/shard_map/psum | solution.py:129
  423.5 1.8 multiply_reduce_fusion.2
  425.3 3.6 multiply_reduce_fusion.1
  430.3 2.0 dynamic-slice_multiply_fusion
  432.3 1.3 dynamic-slice_multiply_fusion.1
  433.7 1.0 copy.87
  (34 shorter events, 0.1 us)
Async XLA Ops:
  7.2 19.7 %copy-start = (bf16[2,256,768]{2,1,0:T(8,128)(2,1)S(1)}, bf16[2,256,768]{2,1,0:T(8,128)(2,1)}, u32[]{:S(2)}) copy-start(bf16[2,256,768]{2,1,0:T(8,128)(2,1)} %param.11) | copy-start | bytes 2359300
  7.2 16.6 %copy-start.12 = (s32[32]{0:T(128)S(1)}, s32[32]{0:T(128)}, u32[]{:S(2)}) copy-start(s32[32]{0:T(128)} %param.8) | copy-start | bytes 388
  7.2 16.7 %copy-start.13 = (s32[32]{0:T(128)S(1)}, s32[32]{0:T(128)}, u32[]{:S(2)}) copy-start(s32[32]{0:T(128)} %param.9) | copy-start | bytes 388
  7.2 16.7 %copy-start.11 = (s32[32,2]{0,1:T(2,128)S(1)}, s32[32,2]{0,1:T(2,128)}, u32[]{:S(2)}) copy-start(s32[32,2]{0,1:T(2,128)} %param.10) | copy-start | bytes 772
  7.2 16.9 %copy-start.2 = (bf16[2,256,256]{2,1,0:T(8,128)(2,1)S(1)}, bf16[2,256,256]{2,1,0:T(8,128)(2,1)}, u32[]{:S(2)}) copy-start(bf16[2,256,256]{2,1,0:T(8,128)(2,1)} %param.12) | copy-start | bytes 786436
  9.3 26.7 %all-to-all-start.1 = ((bf16[8,96,256]{2,0,1:T(8,128)(2,1)}), bf16[8,96,256]{2,0,1:T(8,128)(2,1)S(1)}, u32[]{:S(2)}, u32[]{:S(2)}) async-start(bf16[8,96,256]{2,0,1:T(8,128)(2,1)} %bitcast.6), calls=%async_computation.1 | async-start | bytes 786432 | tf_op jit(solution)/shard_map/all_to_all | solution.py:62
  15.0 18.5 %collective-permute-start = (bf16[8,2,24,256]{3,0,2,1:T(8,128)(2,1)S(1)}, bf16[8,2,24,256]{3,0,2,1:T(8,128)(2,1)S(1)}, u32[]{:S(2)}, u32[]{:S(2)}) collective-permute-start(bf16[8,2,24,256]{3,0,2,1:T(8,128)(2,1)S(1)} %get-tuple-element.19), channel_id=1, source_target_pairs={{0,1},{1,2},{2,3},{3,4},{4,5},{5,6},{6,7},{7,8},{8,9},{9,10},{10,1... | collective-permute-start | bytes 589832 | tf_op jit(solution)/shard_map/ppermute | solution.py:20
  16.9 16.5 %collective-permute-start.1 = (bf16[8,2,24,256]{3,0,2,1:T(8,128)(2,1)S(1)}, bf16[8,2,24,256]{3,0,2,1:T(8,128)(2,1)S(1)}, u32[]{:S(2)}, u32[]{:S(2)}) collective-permute-start(bf16[8,2,24,256]{3,0,2,1:T(8,128)(2,1)S(1)} %get-tuple-element.20), channel_id=1, source_target_pairs={{1,0},{2,1},{3,2},{4,3},{5,4},{6,5},{7,6},{8,7},{9,8},{10,9},{11,1... | collective-permute-start | bytes 589832 | tf_op jit(solution)/shard_map/ppermute | solution.py:22
  36.0 11.9 %all-to-all-start = ((bf16[8,96,256]{2,0,1:T(8,128)(2,1)}), bf16[8,96,256]{2,0,1:T(8,128)(2,1)S(1)}, u32[]{:S(2)}, u32[]{:S(2)}) async-start(bf16[8,96,256]{2,0,1:T(8,128)(2,1)} %bitcast.1), calls=%async_computation | async-start | bytes 786432 | tf_op jit(solution)/shard_map/all_to_all | solution.py:61
  40.5 383.0 %all-reduce.5.cloned.1.call-start = ((), (), s32[]{:S(2)}) async-start(), calls=%async_computation.3 | async-start | bytes 4194304 | tf_op jit(solution)/shard_map/psum | solution.py:129
  61.1 3.8 copy-start.9
  64.9 1.7 copy-start.6
  69.0 3.3 copy-start.3
  69.0 3.3 copy-start.4
  72.3 2.9 copy-start.10
  83.6 7.8 %copy-start.7 = (bf16[24,8,32,32]{3,2,1,0:T(8,128)(2,1)S(1)}, bf16[24,8,32,32]{3,2,1,0:T(8,128)(2,1)}, u32[]{:S(2)}) copy-start(bf16[24,8,32,32]{3,2,1,0:T(8,128)(2,1)} %copy.75) | copy-start | bytes 1179652
  83.6 7.8 %copy-start.8 = (bf16[4,8,24,8,32]{4,3,2,1,0:T(8,128)(2,1)S(1)}, bf16[4,8,24,8,32]{4,3,2,1,0:T(8,128)(2,1)}, u32[]{:S(2)}) copy-start(bf16[4,8,24,8,32]{4,3,2,1,0:T(8,128)(2,1)} %reshape_reshape.7) | copy-start | bytes 1179652
  96.0 2.5 copy-start.5
  184.3 9.4 %collective-permute-start.2 = (bf16[8,2,24,256]{3,0,2,1:T(8,128)(2,1)S(1)}, bf16[8,2,24,256]{3,0,2,1:T(8,128)(2,1)S(1)}, u32[]{:S(2)}, u32[]{:S(2)}) collective-permute-start(bf16[8,2,24,256]{3,0,2,1:T(8,128)(2,1)S(1)} %get-tuple-element.17), channel_id=1, source_target_pairs={{0,1},{1,2},{2,3},{3,4},{4,5},{5,6},{6,7},{7,8},{8,9},{9,10},{10,1... | collective-permute-start | bytes 589832 | tf_op jit(solution)/shard_map/ppermute | solution.py:20
  186.2 9.2 %collective-permute-start.3 = (bf16[8,2,24,256]{3,0,2,1:T(8,128)(2,1)S(1)}, bf16[8,2,24,256]{3,0,2,1:T(8,128)(2,1)S(1)}, u32[]{:S(2)}, u32[]{:S(2)}) collective-permute-start(bf16[8,2,24,256]{3,0,2,1:T(8,128)(2,1)S(1)} %get-tuple-element.18), channel_id=1, source_target_pairs={{1,0},{2,1},{3,2},{4,3},{5,4},{6,5},{7,6},{8,7},{9,8},{10,9},{11,1... | collective-permute-start | bytes 589832 | tf_op jit(solution)/shard_map/ppermute | solution.py:22
  195.5 239.1 %copy-start.1 = (bf16[2,256,768]{2,1,0:T(8,128)(2,1)S(1)}, bf16[2,256,768]{2,1,0:T(8,128)(2,1)}, u32[]{:S(2)}) copy-start(bf16[2,256,768]{2,1,0:T(8,128)(2,1)} %param.11) | copy-start | bytes 2359300
Sparse Core Ops, SparseCore 0:
  160.0 263.4 all-reduce.4
where the time goes:
time: 449 us; the launch traced here: 442 us
  waiting for transfers between devices  229 us (51%)
  matrix products  99.6 us (22%)
  local copies, waits for them, and re-layouts  42 us (9%)
  starting transfers between devices  25.7 us (6%)
  other arithmetic  17.6 us (4%)
  between operations  16.2 us (4%)
  blocking collectives  11.8 us (3%)
    psum x1, waiting for transfers between devices, body(): total_qkv, total_out = lax.psum((raw_qkv, raw_out), ('agent', 'tile'))  225 us
    dot_general x2, matrix products, body(): jnp.einsum('bt,bgc,bge->tce', type_wide, all_feats.astype(f32), d_qkv, pr...  47.2 us
    ppermute x2, starting transfers between devices, with_halo(): lax.ppermute(head, axis, [((i + 1) % count, i) for i in range(ends)])  12.9 us
    dot_general x1, matrix products, body(): jnp.einsum('bge,bce->bgc', d_qkv, wqkv_all.astype(f32), precision=highest)  12.5 us
    all_to_all x1, blocking collectives, body(): lax.all_to_all(d_part, 'agent', split_axis=0, concat_axis=1, tiled=True)  11.8 us
  transfers between devices with their start and end apart: 7, of which 4 were waited for; matrix products, arithmetic and copies ran while one was open for 8% of the time, Pallas kernels for 0%

commit v1 on v0

--- a/solution.py
+++ b/solution.py
@@ -62,9 +62,15 @@
         lax.all_to_all(flat_grads, "agent", split_axis=1, concat_axis=0, tiled=True),
     )
     part_cells = all_feats.shape[1]
-    wqkv_all = jnp.take(w_qkv, types, axis=0)
-    wout_all = jnp.take(w_out, types, axis=0)
-    qkv = jnp.einsum("bgc,bce->bge", all_feats, wqkv_all, preferred_element_type=f32).astype(bf16)
+    pairs = agents * part_cells
+    is_type1 = (types == 1)[:, None, None]
+    type_mask = jnp.stack([types == 0, types == 1], axis=0)[:, :, None, None]
+    feats_rows = all_feats.reshape(pairs, channels)
+    grads_rows = all_grads.reshape(pairs, channels)
+    qkv_both = jnp.einsum(
+        "pc,tce->tpe", feats_rows, w_qkv, preferred_element_type=f32
+    ).astype(bf16).reshape(2, agents, part_cells, 3 * channels)
+    qkv = jnp.where(is_type1, qkv_both[1], qkv_both[0])
     query_heads = qkv[..., :channels].reshape(agents, part_cells, HEADS, head_size)
     key_heads = qkv[..., channels : 2 * channels].reshape(agents, part_cells, HEADS, head_size)
     value_heads = qkv[..., 2 * channels :].reshape(agents, part_cells, HEADS, head_size)
@@ -82,11 +88,17 @@
         .astype(bf16)
         .reshape(agents, part_cells, channels)
     )
-    d_attended = jnp.einsum("age,ace->agc", all_grads, wout_all, preferred_element_type=f32).astype(
-        bf16
+    d_att_both = jnp.einsum(
+        "pe,tce->tpc", grads_rows, w_out, preferred_element_type=f32
+    ).astype(bf16).reshape(2, agents, part_cells, channels)
+    d_attended = jnp.where(is_type1, d_att_both[1], d_att_both[0])
+    attended_typed = jnp.where(type_mask, attended[None], jnp.zeros((), bf16))
+    raw_out = jnp.einsum(
+        "tpc,pe->tce",
+        attended_typed.reshape(2, pairs, channels),
+        grads_rows,
+        preferred_element_type=f32,
     )
-    attended_typed = all_hot[:, :, None, None] * attended[:, None]
-    raw_out = jnp.einsum("atgc,age->tce", attended_typed, all_grads, preferred_element_type=f32)
     attended_heads = d_attended.reshape(agents, part_cells, HEADS, head_size)
     prob_grad = jnp.einsum(
         "aghd,bghd->ghab", attended_heads, value_heads, preferred_element_type=f32
@@ -115,24 +127,33 @@
     key_sum = jnp.sum(key_parts.astype(f32), axis=0).reshape(agents, part_cells, channels)
     value_sum = jnp.sum(value_parts.astype(f32), axis=0).reshape(agents, part_cells, channels)
     d_qkv = jnp.concatenate([d_query.astype(f32), key_sum, value_sum], axis=-1)
-    d_part = jnp.einsum("bge,bce->bgc", d_qkv, wqkv_all.astype(f32), precision=highest).astype(bf16)
+    d_hi = d_qkv.astype(bf16)
+    d_lo = (d_qkv - d_hi.astype(f32)).astype(bf16)
+    d_split = jnp.stack([d_hi, d_lo], axis=0).reshape(2, pairs, 3 * channels)
+    d_part_terms = jnp.einsum(
+        "spe,tce->stpc", d_split, w_qkv, preferred_element_type=f32
+    )
+    d_part_sum = (d_part_terms[0] + d_part_terms[1]).reshape(2, agents, part_cells, channels)
+    d_part = jnp.where(is_type1, d_part_sum[1], d_part_sum[0]).astype(bf16)
     returned = lax.all_to_all(d_part, "agent", split_axis=0, concat_axis=1, tiled=True)
     d_warped = returned.reshape(own_count, row_count, col_count, channels)
-    type_wide = all_hot.astype(f32)
-    raw_qkv = jnp.einsum(
-        "bt,bgc,bge->tce", type_wide, all_feats.astype(f32), d_qkv, precision=highest
+    feats_typed = jnp.where(type_mask, all_feats[None], jnp.zeros((), bf16)).reshape(
+        2, pairs, channels
     )
+    qkv_terms = jnp.einsum(
+        "tpc,spe->stce", feats_typed, d_split, preferred_element_type=f32
+    )
+    raw_qkv = qkv_terms[0] + qkv_terms[1]
     rimmed_grad = with_halo(d_warped, (("tile", 1),), MAXOFF)
     d_feats = relocate(rimmed_grad, own_offsets, -1)
     norm_limit = math.sqrt(8.0 * channels * channels)
-    share_rows = channels // lax.axis_size("tile")
-    total_qkv, total_out = lax.psum((raw_qkv, raw_out), ("agent", "tile"))
-    square_sum = jnp.sum(total_qkv * total_qkv) + jnp.sum(total_out * total_out)
-    share_start = lax.axis_index("tile") * share_rows
-    share_qkv = lax.dynamic_slice_in_dim(total_qkv, share_start, share_rows, 1)
-    share_out = lax.dynamic_slice_in_dim(total_out, share_start, share_rows, 1)
+    raw_all = jnp.concatenate([raw_qkv, raw_out], axis=-1)
+    share_all = lax.psum_scatter(raw_all, "tile", scatter_dimension=1, tiled=True)
+    share_all = lax.psum(share_all, "agent")
+    square_sum = lax.psum(jnp.sum(share_all * share_all), "tile")
     factor = norm_limit / jnp.maximum(jnp.sqrt(square_sum), norm_limit)
-    return (d_feats, share_qkv * factor, share_out * factor)
+    scaled = share_all * factor
+    return (d_feats, scaled[..., : 3 * channels], scaled[..., 3 * channels :])
 
 
 def solution(mesh):

time: 449 us -> 471 us (1.049)
  the two profiles are of different devices: /device:TPU:2 before, /device:TPU:1 now
where the time goes in v1:
time: 471 us; the launch traced here: 463 us
  blocking collectives  154 us (33%)
  waiting for transfers between devices  145 us (31%)
  local copies, waits for them, and re-layouts  73.6 us (16%)
  matrix products  34.9 us (7%)
  starting transfers between devices  23.3 us (5%)
  other arithmetic  16.8 us (4%)
  between operations  16.4 us (3%)
    unnamed x2, waiting for transfers between devices  136 us
    psum x1, blocking collectives, body(): square_sum = lax.psum(jnp.sum(share_all * share_all), 'tile')  130 us
    concatenate x8, local copies, waits for them, and re-layouts, body(): d_qkv = jnp.concatenate([d_query.astype(f32), key_sum, value_sum], axis=-1)  21.4 us
    psum x1, blocking collectives, body(): share_all = lax.psum(share_all, 'agent')  13.3 us
    unnamed x55, local copies, waits for them, and re-layouts  12.3 us
    all_to_all x1, blocking collectives, body(): lax.all_to_all(d_part, 'agent', split_axis=0, concat_axis=1, tiled=True)  10.3 us
    ppermute x2, starting transfers between devices, with_halo(): lax.ppermute(tail, axis, [(i, (i + 1) % count) for i in range(ends)])  9.92 us
  transfers between devices with their start and end apart: 7, of which 3 were waited for; matrix products, arithmetic and copies ran while one was open for 10% of the time, Pallas kernels for 0%

profile of v1, /device:TPU:1, one launch (start us, length us, event | category | flops | bytes accessed | tf_op | source)
XLA Modules:
  0.0 463.5 jit_solution(607372187424560258)
XLA Ops:
  7.2 2.0 copy.108
  9.2 5.0 %all-to-all-start.1 = ((bf16[8,96,256]{2,0,1:T(8,128)(2,1)}), bf16[8,96,256]{2,0,1:T(8,128)(2,1)S(1)}, u32[]{:S(2)}, u32[]{:S(2)}) async-start(bf16[8,96,256]{2,0,1:T(8,128)(2,1)} %bitcast.10), calls=%async_computation.1 | async-start | bytes 786432 | tf_op jit(solution)/shard_map/all_to_all | solution.py:62
  14.3 1.2 copy.101
  15.5 4.4 collective-permute-start
  19.9 1.9 collective-permute-start.1
  23.1 3.8 collective-permute-done.1
  27.0 2.4 gather_fusion
  29.4 4.5 all-to-all-start
  35.0 0.6 squeeze.34
  35.6 1.8 squeeze.32
  37.5 1.8 squeeze.35
  39.4 1.8 squeeze.33
  41.1 3.4 broadcast_select_fusion
  44.5 1.5 broadcast_select_fusion.1
  46.1 0.8 convert_bitcast_fusion
  47.3 1.8 reshape_reshape.4
  49.1 1.9 reshape.307
  50.9 1.7 copy.155
  52.7 0.9 copy.154
  53.6 3.8 fusion.3
  57.4 1.6 copy-done.4
  59.1 0.8 fusion.59
  59.9 1.6 copy.124
  61.5 3.3 fusion.26
  64.8 2.9 fusion.22
  67.7 8.2 %fusion.15 = f32[24,8,32,32]{3,2,1,0:T(8,128)} fusion(bf16[32,24,8,32]{0,3,2,1:T(8,128)(2,1)S(1)} %bitcast.129, f32[24,8,32,32]{2,3,1,0:T(8,128)} %fusion.22, f32[24,8,32,32]{2,3,1,0:T(8,128)} %copy-done.4, f32[24,8,32]{2,1,0:T(8,128)S(1)} %get-tuple-element.35, pred[32,32]{0,1:T(8,128)(4,1)S(1)} %fusion.44), kind=kOutput, calls=%fused_computation.31 | convolution fusion | flops 15144991 | bytes 2778112 | tf_op jit(solution)/shard_map/ghab,bghd->aghd/dot_general | solution.py:112
  75.9 6.7 %multiply_convert_fusion = bf16[24,8,32,32]{2,3,1,0:T(8,128)(2,1)S(1)} fusion(f32[24,8,32,32]{2,3,1,0:T(8,128)} %fusion.22, f32[24,8,32]{2,1,0:T(8,128)} %copy-done.15, f32[24,8,32,32]{2,3,1,0:T(8,128)} %copy-done.4, pred[32,32]{0,1:T(8,128)(4,1)S(1)} %fusion.44), kind=kOutput, calls=%fused_computation.5 | output fusion | flops 2168863 | bytes 1991680 | tf_op jit(solution)/shard_map/sub | solution.py:108
  82.6 4.5 convert_reduce_fusion
  87.1 2.3 copy.151
  89.5 1.6 copy.118
  91.1 2.5 copy.131
  93.6 6.2 %convert_reduce_fusion.1 = f32[24,8,32,32]{3,2,1,0:T(8,128)} fusion(bf16[4,8,24,8,32]{4,3,2,1,0:T(8,128)(2,1)} %reshape_reshape.4, bf16[24,8,32,32]{3,2,1,0:T(8,128)(2,1)} %copy.118), kind=kOutput, calls=%fused_computation.4 | convolution fusion | flops 14745600 | bytes 1572864 | tf_op jit(solution)/shard_map/ghnyb,nyghd->nbghd/dot_general | solution.py:121
  99.8 2.3 copy.150
  102.1 1.3 subtract_convert_fusion
  103.3 1.3 fusion.16
  104.6 0.8 copy.133
  105.4 3.6 copy.136
  109.0 1.8 broadcast_in_dim.103
  110.9 2.8 fusion.12
  114.0 0.8 copy-done.9
  114.8 0.6 fusion.35
  115.6 2.5 copy.138
  118.1 4.8 %copy.117 = f32[32,24,8,32]{3,2,1,0:T(8,128)} copy(f32[32,24,8,32]{0,3,2,1:T(8,128)} %bitcast.114) | data formatting | bytes 1572864 | tf_op jit(solution)/shard_map/concatenate | solution.py:129
  122.9 3.1 reshape.313
  126.0 1.2 constant_dynamic-update-slice_fusion.2
  127.2 4.8 %copy.121 = f32[32,24,8,32]{3,2,1,0:T(8,128)} copy(f32[32,24,8,32]{0,3,2,1:T(8,128)} %bitcast.116) | data formatting | bytes 1572864 | tf_op jit(solution)/shard_map/reduce_sum | solution.py:127
  132.0 3.1 concatenate.75
  135.1 5.0 %copy.127 = f32[32,24,8,32]{3,2,1,0:T(8,128)} copy(f32[32,24,8,32]{0,3,2,1:T(8,128)} %bitcast.112) | data formatting | bytes 1572864 | tf_op jit(solution)/shard_map/reduce_sum | solution.py:128
  140.2 3.2 concatenate.76
  143.3 1.3 constant_dynamic-update-slice_fusion.1
  145.0 1.4 fusion.13
  146.8 10.3 %all_to_all.45 = bf16[32,24,256]{2,1,0:T(8,128)(2,1)S(1)} all-to-all(bf16[32,24,256]{2,1,0:T(8,128)(2,1)S(1)} %select_convert_fusion), channel_id=1, replica_groups=mesh['agent'=4,'tile'=64] {'agent'}, dimensions={0} | all-to-all | bytes 786432 | tf_op jit(solution)/shard_map/all_to_all | solution.py:138
  157.2 5.5 %collective-permute-start.2 = (bf16[8,2,24,256]{3,0,2,1:T(8,128)(2,1)S(1)}, bf16[8,2,24,256]{3,0,2,1:T(8,128)(2,1)S(1)}, u32[]{:S(2)}, u32[]{:S(2)}) collective-permute-start(bf16[8,2,24,256]{3,0,2,1:T(8,128)(2,1)S(1)} %get-tuple-element.26), channel_id=1, source_target_pairs={{0,1},{1,2},{2,3},{3,4},{4,5},{5,6},{6,7},{7,8},{8,9},{9,10},{10,1... | collective-permute-start | bytes 589832 | tf_op jit(solution)/shard_map/ppermute | solution.py:20
  162.7 1.9 collective-permute-start.3
  165.9 4.4 collective-permute-done.3
  170.4 1.7 gather_fusion.1
  172.1 136.5 %all-reduce.5.cloned.1.call-done = f32[2,256,1024]{2,0,1:T(2,128)} async-done(((f32[2,256,1024]{2,0,1:T(2,128)}), f32[2,256,1024]{2,0,1:T(2,128)}) %all-reduce.5.cloned.1.call-update) | async-done | bytes 2097168
  308.6 0.8 constant_dynamic-slice_fusion
  309.4 13.3 %psum.14 = f32[2,4,1024]{2,0,1:T(2,128)S(1)} all-reduce(f32[2,4,1024]{2,0,1:T(2,128)S(1)} %constant_dynamic-slice_fusion), channel_id=1, replica_groups=mesh['agent'=4,'tile'=64] {'agent'}, use_global_device_ids=true, to_apply=%region_5.6 | all-reduce | flops 8192 | bytes 65536 | tf_op jit(solution)/shard_map/psum | solution.py:152
  322.7 0.6 multiply_reduce_fusion.1
  323.3 0.8 copy.139
  324.1 130.1 %psum.15 = f32[]{:T(128)} all-reduce(f32[]{:T(128)} %multiply_reduce_fusion.1), channel_id=1, replica_groups=mesh['agent'=4,'tile'=64] {'tile'}, use_global_device_ids=true, to_apply=%region_7.8 | all-reduce | flops 1 | bytes 8 | tf_op jit(solution)/shard_map/psum | solution.py:153
  455.0 0.6 copy.140
  455.6 0.6 copy.141
  (84 shorter events, 5.0 us)
Async XLA Ops:
  7.2 38.9 %copy-start = (bf16[2,256,768]{2,1,0:T(8,128)(2,1)S(1)}, bf16[2,256,768]{2,1,0:T(8,128)(2,1)}, u32[]{:S(2)}) copy-start(bf16[2,256,768]{2,1,0:T(8,128)(2,1)} %param.11) | copy-start | bytes 2359300
  7.2 14.7 %copy-start.21 = (s32[32]{0:T(128)S(1)}, s32[32]{0:T(128)}, u32[]{:S(2)}) copy-start(s32[32]{0:T(128)} %param.9) | copy-start | bytes 388
  7.2 14.7 %copy-start.20 = (s32[32]{0:T(128)S(1)}, s32[32]{0:T(128)}, u32[]{:S(2)}) copy-start(s32[32]{0:T(128)} %param.8) | copy-start | bytes 388
  7.2 15.6 %copy-start.16 = (s32[32,2]{0,1:T(2,128)S(1)}, s32[32,2]{0,1:T(2,128)}, u32[]{:S(2)}) copy-start(s32[32,2]{0,1:T(2,128)} %param.10) | copy-start | bytes 772
  9.2 20.2 %all-to-all-start.1 = ((bf16[8,96,256]{2,0,1:T(8,128)(2,1)}), bf16[8,96,256]{2,0,1:T(8,128)(2,1)S(1)}, u32[]{:S(2)}, u32[]{:S(2)}) async-start(bf16[8,96,256]{2,0,1:T(8,128)(2,1)} %bitcast.10), calls=%async_computation.1 | async-start | bytes 786432 | tf_op jit(solution)/shard_map/all_to_all | solution.py:62
  15.5 7.4 %collective-permute-start = (bf16[8,2,24,256]{3,0,2,1:T(8,128)(2,1)S(1)}, bf16[8,2,24,256]{3,0,2,1:T(8,128)(2,1)S(1)}, u32[]{:S(2)}, u32[]{:S(2)}) collective-permute-start(bf16[8,2,24,256]{3,0,2,1:T(8,128)(2,1)S(1)} %get-tuple-element.28), channel_id=1, source_target_pairs={{0,1},{1,2},{2,3},{3,4},{4,5},{5,6},{6,7},{7,8},{8,9},{9,10},{10,1... | collective-permute-start | bytes 589832 | tf_op jit(solution)/shard_map/ppermute | solution.py:20
  19.9 7.0 %collective-permute-start.1 = (bf16[8,2,24,256]{3,0,2,1:T(8,128)(2,1)S(1)}, bf16[8,2,24,256]{3,0,2,1:T(8,128)(2,1)S(1)}, u32[]{:S(2)}, u32[]{:S(2)}) collective-permute-start(bf16[8,2,24,256]{3,0,2,1:T(8,128)(2,1)S(1)} %get-tuple-element.29), channel_id=1, source_target_pairs={{1,0},{2,1},{3,2},{4,3},{5,4},{6,5},{7,6},{8,7},{9,8},{10,9},{11,1... | collective-permute-start | bytes 589832 | tf_op jit(solution)/shard_map/ppermute | solution.py:22
  22.6 0.5 copy-start.18
  27.0 7.1 %copy-start.14 = (bf16[2,256,256]{2,1,0:T(8,128)(2,1)S(1)}, bf16[2,256,256]{2,1,0:T(8,128)(2,1)}, u32[]{:S(2)}) copy-start(bf16[2,256,256]{2,1,0:T(8,128)(2,1)} %param.12) | copy-start | bytes 786436
  29.4 16.6 %all-to-all-start = ((bf16[8,96,256]{2,0,1:T(8,128)(2,1)}), bf16[8,96,256]{2,0,1:T(8,128)(2,1)S(1)}, u32[]{:S(2)}, u32[]{:S(2)}) async-start(bf16[8,96,256]{2,0,1:T(8,128)(2,1)} %bitcast.1), calls=%async_computation | async-start | bytes 786432 | tf_op jit(solution)/shard_map/all_to_all | solution.py:61
  33.9 274.7 %all-reduce.5.cloned.1.call-start = ((), (), s32[]{:S(2)}) async-start(), calls=%async_computation.3 | async-start | bytes 4194304
  34.0 0.8 copy-start.8
  41.1 3.4 copy-start.3
  41.1 3.4 copy-start.17
  53.6 3.8 copy-start.10
  57.4 1.7 copy-start.4
  57.4 10.2 %copy-start.15 = (f32[24,8,32]{2,1,0:T(8,128)}, f32[24,8,32]{2,1,0:T(8,128)S(1)}, u32[]{:S(2)}) copy-start(f32[24,8,32]{2,1,0:T(8,128)S(1)} %get-tuple-element.35) | copy-start | bytes 73732
  61.5 3.3 copy-start.1
  61.5 3.3 copy-start.2
  64.8 2.9 copy-start.11
  75.9 6.7 %copy-start.6 = (bf16[4,8,24,8,32]{4,3,2,1,0:T(8,128)(2,1)S(1)}, bf16[4,8,24,8,32]{4,3,2,1,0:T(8,128)(2,1)}, u32[]{:S(2)}) copy-start(bf16[4,8,24,8,32]{4,3,2,1,0:T(8,128)(2,1)} %broadcast_select_fusion.1) | copy-start | bytes 1179652
  75.9 6.7 %copy-start.7 = (bf16[24,8,32,32]{3,2,1,0:T(8,128)(2,1)S(1)}, bf16[24,8,32,32]{3,2,1,0:T(8,128)(2,1)}, u32[]{:S(2)}) copy-start(bf16[24,8,32,32]{3,2,1,0:T(8,128)(2,1)} %copy.124) | copy-start | bytes 1179652
  105.4 5.4 %copy-start.12 = (bf16[1,32,24,768]{3,1,2,0:T(8,128)(2,1)S(1)}, bf16[1,32,24,768]{3,1,2,0:T(8,128)(2,1)}, u32[]{:S(2)}) copy-start(bf16[1,32,24,768]{3,1,2,0:T(8,128)(2,1)} %subtract_convert_fusion) | copy-start | bytes 3538948
  105.4 5.4 %copy-start.19 = (pred[2,32]{1,0:T(4,128)(4,1)S(1)}, pred[2,32]{1,0:T(4,128)(4,1)}, u32[]{:S(2)}) copy-start(pred[2,32]{1,0:T(4,128)(4,1)} %copy-done.18) | copy-start | bytes 196
  113.7 1.0 copy-start.9
  113.7 1.1 copy-start.13
  143.3 1.4 copy-start.5
  146.7 18.0 %copy-start.22 = (u32[256]{0:T(256)S(1)}, u32[256]{0:T(256)}, u32[]{:S(2)}) copy-start(u32[256]{0:T(256)} %constant.101) | copy-start | bytes 3076
  157.2 8.7 %collective-permute-start.2 = (bf16[8,2,24,256]{3,0,2,1:T(8,128)(2,1)S(1)}, bf16[8,2,24,256]{3,0,2,1:T(8,128)(2,1)S(1)}, u32[]{:S(2)}, u32[]{:S(2)}) collective-permute-start(bf16[8,2,24,256]{3,0,2,1:T(8,128)(2,1)S(1)} %get-tuple-element.26), channel_id=1, source_target_pairs={{0,1},{1,2},{2,3},{3,4},{4,5},{5,6},{6,7},{7,8},{8,9},{9,10},{10,1... | collective-permute-start | bytes 589832 | tf_op jit(solution)/shard_map/ppermute | solution.py:20
  162.7 7.6 %collective-permute-start.3 = (bf16[8,2,24,256]{3,0,2,1:T(8,128)(2,1)S(1)}, bf16[8,2,24,256]{3,0,2,1:T(8,128)(2,1)S(1)}, u32[]{:S(2)}, u32[]{:S(2)}) collective-permute-start(bf16[8,2,24,256]{3,0,2,1:T(8,128)(2,1)S(1)} %get-tuple-element.27), channel_id=1, source_target_pairs={{1,0},{2,1},{3,2},{4,3},{5,4},{6,5},{7,6},{8,7},{9,8},{10,9},{11,1... | collective-permute-start | bytes 589832 | tf_op jit(solution)/shard_map/ppermute | solution.py:22
Sparse Core Ops, SparseCore 0:
  118.2 190.3 all-reduce.4

commit v2 on v1

--- a/solution.py
+++ b/solution.py
@@ -7,6 +7,47 @@
 
 HEADS = 8
 MAXOFF = 2
+
+
+def axis_bits(axis):
+    count = lax.axis_size(axis)
+    bits = count.bit_length() - 1
+    assert 1 << bits == count
+    return bits
+
+
+def xor_pairs(count, bit):
+    return [(i, i ^ (1 << bit)) for i in range(count)]
+
+
+def tile_bit_order(count):
+    bits = count.bit_length() - 1
+    preferred = [0, 1, 4, 2, 5, 3]
+    return [b for b in preferred if b < bits] + [b for b in range(bits) if b not in preferred]
+
+
+def halving_sum(pieces, axis, bit_order):
+    count = lax.axis_size(axis)
+    me = lax.axis_index(axis)
+    bits = axis_bits(axis)
+    rest = pieces.shape[1:]
+    x = pieces.reshape((2,) * bits + rest)
+    for bit in bit_order:
+        dim = bits - 1 - bit
+        mine = (me >> bit) & 1
+        low = lax.index_in_dim(x, 0, dim, keepdims=True)
+        high = lax.index_in_dim(x, 1, dim, keepdims=True)
+        keep = jnp.where(mine == 1, high, low)
+        send = jnp.where(mine == 1, low, high)
+        x = keep + lax.ppermute(send, axis, xor_pairs(count, bit))
+    return x.reshape(rest)
+
+
+def doubling_sum(x, axis, bit_order):
+    count = lax.axis_size(axis)
+    for bit in bit_order:
+        x = x + lax.ppermute(x, axis, xor_pairs(count, bit))
+    return x
 
 
 def with_halo(cells, sides, width):
@@ -148,9 +189,13 @@
     d_feats = relocate(rimmed_grad, own_offsets, -1)
     norm_limit = math.sqrt(8.0 * channels * channels)
     raw_all = jnp.concatenate([raw_qkv, raw_out], axis=-1)
-    share_all = lax.psum_scatter(raw_all, "tile", scatter_dimension=1, tiled=True)
-    share_all = lax.psum(share_all, "agent")
-    square_sum = lax.psum(jnp.sum(share_all * share_all), "tile")
+    tiles = lax.axis_size("tile")
+    share_rows = channels // tiles
+    pieces = raw_all.reshape(2, tiles, share_rows, 4 * channels).transpose(1, 0, 2, 3)
+    share_all = halving_sum(pieces, "tile", tile_bit_order(tiles))
+    share_all = doubling_sum(share_all, "agent", list(range(axis_bits("agent"))))
+    square_sum = jnp.broadcast_to(jnp.sum(share_all * share_all), (8, 128))
+    square_sum = doubling_sum(square_sum, "tile", list(range(axis_bits("tile"))))[0, 0]
     factor = norm_limit / jnp.maximum(jnp.sqrt(square_sum), norm_limit)
     scaled = share_all * factor
     return (d_feats, scaled[..., : 3 * channels], scaled[..., 3 * channels :])

time: 471 us -> 235 us (0.50)
  the two profiles are of different devices: /device:TPU:1 before, /device:TPU:2 now
where the time goes in v2:
time: 235 us; the launch traced here: 232 us
  local copies, waits for them, and re-layouts  73.8 us (31%)
  starting transfers between devices  52.1 us (22%)
  waiting for transfers between devices  44.1 us (19%)
  matrix products  34.9 us (15%)
  other arithmetic  24.9 us (11%)
    ppermute x6, waiting for transfers between devices, halving_sum(): x = keep + lax.ppermute(send, axis, xor_pairs(count, bit))  23.4 us
    concatenate x8, local copies, waits for them, and re-layouts, body(): d_qkv = jnp.concatenate([d_query.astype(f32), key_sum, value_sum], axis=-1)  19.9 us
    ppermute x8, waiting for transfers between devices, doubling_sum(): x = x + lax.ppermute(x, axis, xor_pairs(count, bit))  18.5 us
    ppermute x2, starting transfers between devices, with_halo(): lax.ppermute(head, axis, [((i + 1) % count, i) for i in range(ends)])  12.5 us
    ppermute x6, starting transfers between devices, halving_sum(): x = keep + lax.ppermute(send, axis, xor_pairs(count, bit))  11.6 us
    ppermute x8, starting transfers between devices, doubling_sum(): x = x + lax.ppermute(x, axis, xor_pairs(count, bit))  10.8 us
    unnamed x51, local copies, waits for them, and re-layouts  9.01 us
    dot_general x1, matrix products, body(): jnp.einsum('ghab,bghd->aghd', score_grad, key_heads, preferred_element_ty...  8.25 us
  transfers between devices with their start and end apart: 21, of which 13 were waited for; matrix products, arithmetic and copies ran while one was open for 20% of the time, Pallas kernels for 0%

profile of v2, /device:TPU:2, one launch (start us, length us, event | category | flops | bytes accessed | tf_op | source)
XLA Modules:
  0.0 232.2 jit_solution(8492455447294959551)
XLA Ops:
  0.7 2.0 copy.109
  2.7 4.5 %all-to-all-start.1 = ((bf16[8,96,256]{2,0,1:T(8,128)(2,1)}), bf16[8,96,256]{2,0,1:T(8,128)(2,1)S(1)}, u32[]{:S(2)}, u32[]{:S(2)}) async-start(bf16[8,96,256]{2,0,1:T(8,128)(2,1)} %bitcast.10), calls=%async_computation.1 | async-start | bytes 786432 | tf_op jit(solution)/shard_map/all_to_all | solution.py:103
  7.2 1.2 copy.102
  8.4 1.9 collective-permute-start
  10.4 6.9 %collective-permute-start.1 = (bf16[8,2,24,256]{3,0,2,1:T(8,128)(2,1)S(1)}, bf16[8,2,24,256]{3,0,2,1:T(8,128)(2,1)S(1)}, u32[]{:S(2)}, u32[]{:S(2)}) collective-permute-start(bf16[8,2,24,256]{3,0,2,1:T(8,128)(2,1)S(1)} %get-tuple-element.33), channel_id=1, source_target_pairs={{1,0},{2,1},{3,2},{4,3},{5,4},{6,5},{7,6},{8,7},{9,8},{10,9},{11,1... | collective-permute-start | bytes 589832 | tf_op jit(solution)/shard_map/ppermute | solution.py:63
  18.7 1.8 collective-permute-done.1
  20.5 2.4 %gather_fusion = bf16[8,4,24,256]{3,0,2,1:T(8,128)(2,1)} fusion(bf16[8,8,28,256]{3,0,2,1:T(8,128)(2,1)S(1)} %fusion.32, s32[8]{0:T(128)S(1)} %get-tuple-element.35), kind=kCustom, calls=%fused_computation | custom fusion | bytes 786560 | tf_op jit(solution)/shard_map/vmap()/gather | solution.py:78
  23.0 4.8 %all-to-all-start = ((bf16[8,96,256]{2,0,1:T(8,128)(2,1)}), bf16[8,96,256]{2,0,1:T(8,128)(2,1)S(1)}, u32[]{:S(2)}, u32[]{:S(2)}) async-start(bf16[8,96,256]{2,0,1:T(8,128)(2,1)} %bitcast.1), calls=%async_computation | async-start | bytes 786432 | tf_op jit(solution)/shard_map/all_to_all | solution.py:102
  29.4 1.8 squeeze.33
  31.4 1.8 squeeze.36
  33.2 1.8 squeeze.34
  35.0 3.4 %broadcast_select_fusion = bf16[32,24,8,32]{3,2,1,0:T(8,128)(2,1)} fusion(bf16[32,24,8,32]{3,2,1,0:T(8,128)(2,1)} %squeeze.33, bf16[32,24,8,32]{3,2,1,0:T(8,128)(2,1)} %squeeze.34, pred[32]{0:T(512)(128)(4,1)S(1)} %get-tuple-element.38), kind=kLoop, calls=%fused_computation.44 | loop fusion | flops 196608 | bytes 1179680 | tf_op jit(solution)/shard_map/jit(_where)/select_n | solution.py:135
  38.4 1.4 broadcast_select_fusion.1
  41.2 1.8 reshape_reshape.4
  42.9 1.8 reshape.321
  44.8 1.6 copy.158
  47.3 3.8 %fusion.3 = (f32[24,8,32]{2,1,0:T(8,128)S(1)}, f32[24,8,32,32]{2,3,1,0:T(8,128)S(1)}) fusion(pred[32,32]{0,1:T(8,128)(4,1)S(1)} %fusion.44, bf16[32,24,8,32]{0,3,2,1:T(8,128)(2,1)S(1)} %bitcast.136, bf16[32,24,8,32]{3,2,1,0:T(8,128)(2,1)} %reshape.321), kind=kOutput, calls=%fused_computation.12 | convolution fusion | flops 13166592 | bytes 1598464 | tf_op jit(solution)/shard_map/aghd,bghd->ghab/dot_general | solution.py:119
  51.2 1.6 copy-done.5
  53.6 2.1 copy.125
  55.7 3.3 %fusion.26 = bf16[32,24,8,32]{0,3,2,1:T(8,128)(2,1)} fusion(bf16[32,24,8,32]{0,3,2,1:T(8,128)(2,1)} %bitcast.116, bf16[24,8,32,32]{2,3,1,0:T(8,128)(2,1)S(1)} %fusion.59), kind=kOutput, calls=%fused_computation.46 | convolution fusion | flops 12779520 | bytes 1179648 | tf_op jit(solution)/shard_map/ghab,bghd->aghd/dot_general | solution.py:128
  59.0 2.9 %fusion.22 = f32[24,8,32,32]{2,3,1,0:T(8,128)} fusion(bf16[32,24,8,32]{0,3,2,1:T(8,128)(2,1)S(1)} %bitcast.117, bf16[32,24,8,32]{3,2,1,0:T(8,128)(2,1)S(1)} %copy-done.3), kind=kOutput, calls=%fused_computation.40 | convolution fusion | flops 12582912 | bytes 1572864 | tf_op jit(solution)/shard_map/aghd,bghd->ghab/dot_general | solution.py:144
  61.9 8.2 %fusion.15 = f32[24,8,32,32]{3,2,1,0:T(8,128)} fusion(bf16[32,24,8,32]{0,3,2,1:T(8,128)(2,1)S(1)} %bitcast.137, f32[24,8,32,32]{2,3,1,0:T(8,128)} %fusion.22, f32[24,8,32,32]{2,3,1,0:T(8,128)} %copy-done.5, f32[24,8,32]{2,1,0:T(8,128)S(1)} %get-tuple-element.39, pred[32,32]{0,1:T(8,128)(4,1)S(1)} %fusion.44), kind=kOutput, calls=%fused_computation.31 | convolution fusion | flops 15144991 | bytes 2778112 | tf_op jit(solution)/shard_map/ghab,bghd->aghd/dot_general | solution.py:153
  70.2 6.7 %multiply_convert_fusion = bf16[24,8,32,32]{2,3,1,0:T(8,128)(2,1)S(1)} fusion(f32[24,8,32,32]{2,3,1,0:T(8,128)} %fusion.22, f32[24,8,32]{2,1,0:T(8,128)} %copy-done.16, f32[24,8,32,32]{2,3,1,0:T(8,128)} %copy-done.5, pred[32,32]{0,1:T(8,128)(4,1)S(1)} %fusion.44), kind=kOutput, calls=%fused_computation.5 | output fusion | flops 2168863 | bytes 1991680 | tf_op jit(solution)/shard_map/sub | solution.py:149
  76.9 4.5 %convert_reduce_fusion = f32[24,8,32,32]{3,2,1,0:T(8,128)} fusion(bf16[4,8,24,8,32]{4,3,2,1,0:T(8,128)(2,1)S(1)} %copy-done.7, bf16[24,8,32,32]{3,2,1,0:T(8,128)(2,1)S(1)} %copy-done.8), kind=kOutput, calls=%fused_computation.3 | convolution fusion | flops 14745600 | bytes 1572864 | tf_op jit(solution)/shard_map/ghnyb,nyghd->nbghd/dot_general | solution.py:165
  81.4 2.3 copy.152
  83.7 1.6 copy.119
  85.3 2.3 copy.132
  87.6 6.2 %convert_reduce_fusion.1 = f32[24,8,32,32]{3,2,1,0:T(8,128)} fusion(bf16[4,8,24,8,32]{4,3,2,1,0:T(8,128)(2,1)} %reshape_reshape.4, bf16[24,8,32,32]{3,2,1,0:T(8,128)(2,1)} %copy.119), kind=kOutput, calls=%fused_computation.4 | convolution fusion | flops 14745600 | bytes 1572864 | tf_op jit(solution)/shard_map/ghnyb,nyghd->nbghd/dot_general | solution.py:162
  93.8 2.3 copy.151
  96.1 1.2 subtract_convert_fusion
  99.4 3.7 %copy.137 = bf16[32,24,8,32]{3,2,1,0:T(8,128)(2,1)S(1)} copy(bf16[32,24,8,32]{0,3,2,1:T(8,128)(2,1)} %fusion.26) | data formatting | bytes 786432 | tf_op jit(solution)/shard_map/convert_element_type | solution.py:129
  103.1 1.8 broadcast_in_dim.106
  105.0 2.8 %fusion.12 = f32[2,2,256,768]{2,3,1,0:T(8,128)S(1)} fusion(bf16[1,32,24,768]{3,1,2,0:T(8,128)(2,1)S(1)} %copy-done.13, bf16[1,32,24,768]{3,1,2,0:T(8,128)(2,1)} %fusion.16, pred[2,32]{1,0:T(4,128)(4,1)S(1)} %copy-done.20, bf16[32,24,256]{2,0,1:T(8,128)(2,1)} %copy.134), kind=kOutput, calls=%fused_computation.26 | convolution fusion | flops 1213071360 | bytes 5898304 | tf_op jit(solution)/shard_map/tpc,spe->stce/dot_general | solution.py:184
  109.7 2.4 %copy.139 = f32[2,256,1024]{2,0,1:T(2,128)} copy(f32[2,256,1024]{1,2,0:T(8,128)S(1)} %pad_maximum_fusion.1) | data formatting | bytes 4194304 | tf_op jit(solution)/shard_map/concatenate | solution.py:191
  112.1 2.4 %fusion.62 = (f32[2,2,2,2,2,1,2,4,1024]{8,6,7,5,4,3,2,1,0:T(2,128)S(1)}, f32[2,2,2,2,2,1,2,4,1024]{8,6,7,5,4,3,2,1,0:T(2,128)S(1)}) fusion(f32[2,2,2,2,2,2,2,4,1024]{8,6,7,5,4,3,2,1,0:T(2,128)} %bitcast.124), kind=kLoop, calls=%fused_computation.114 | loop fusion | bytes 4194304 | tf_op jit(solution)/shard_map/slice | solution.py:39
  116.5 2.8 %collective-permute-done.4 = f32[2,2,2,2,2,1,2,4,1024]{8,7,6,5,4,3,2,1,0:T(4,128)} collective-permute-done((f32[2,2,2,2,2,1,2,4,1024]{8,7,6,5,4,3,2,1,0:T(4,128)S(1)}, f32[2,2,2,2,2,1,2,4,1024]{8,7,6,5,4,3,2,1,0:T(4,128)}, u32[]{:S(2)}, u32[]{:S(2)}) %collective-permute-start.4) | collective-permute-done | bytes 1048608 | tf_op jit(solution)/shard_map/ppermute | solution.py:42
  119.3 2.6 %select_add_fusion = f32[2,2,2,2,2,1,2,4,1024]{8,7,6,5,4,3,2,1,0:T(4,128)S(1)} fusion(f32[2,2,2,2,2,1,2,4,1024]{8,7,6,5,4,3,2,1,0:T(4,128)} %collective-permute-done.4, f32[2,2,2,2,2,1,2,4,1024]{8,6,7,5,4,3,2,1,0:T(2,128)} %copy-done.2, f32[2,2,2,2,2,1,2,4,1024]{8,6,7,5,4,3,2,1,0:T(2,128)S(1)} %get-tuple-element.21, pred[]{:T(512)S(6)} %eq.62), kind=kLoop, calls=%fused_computation.50 | loop fusion | flops 524288 | bytes 4194305 | tf_op jit(solution)/shard_map/add | solution.py:42
  123.3 5.0 %copy.118 = f32[32,24,8,32]{3,2,1,0:T(8,128)} copy(f32[32,24,8,32]{0,3,2,1:T(8,128)} %bitcast.121) | data formatting | bytes 1572864 | tf_op jit(solution)/shard_map/concatenate | solution.py:170
  128.3 2.4 %reshape.330 = f32[1,768,256]{2,1,0:T(8,128)S(1)} reshape(f32[32,24,8,32]{3,2,1,0:T(8,128)} %copy.118) | data formatting | bytes 1572864 | tf_op jit(solution)/shard_map/concatenate | solution.py:170
  130.7 4.8 %copy.122 = f32[32,24,8,32]{3,2,1,0:T(8,128)} copy(f32[32,24,8,32]{0,3,2,1:T(8,128)} %bitcast.123) | data formatting | bytes 1572864 | tf_op jit(solution)/shard_map/reduce_sum | solution.py:168
  135.5 2.4 %concatenate.75 = f32[1,768,256]{2,1,0:T(8,128)S(1)} reshape(f32[32,24,8,32]{3,2,1,0:T(8,128)} %copy.122) | data formatting | bytes 1572864 | tf_op jit(solution)/shard_map/concatenate | solution.py:170
  137.9 4.8 %copy.128 = f32[32,24,8,32]{3,2,1,0:T(8,128)} copy(f32[32,24,8,32]{0,3,2,1:T(8,128)} %bitcast.119) | data formatting | bytes 1572864 | tf_op jit(solution)/shard_map/reduce_sum | solution.py:169
  142.6 3.1 %concatenate.76 = f32[1,768,256]{2,1,0:T(8,128)} reshape(f32[32,24,8,32]{3,2,1,0:T(8,128)} %copy.128) | data formatting | bytes 1572864 | tf_op jit(solution)/shard_map/concatenate | solution.py:170
  147.0 1.3 select_add_fusion.1
  149.2 7.5 %collective-permute-done.6 = f32[2,1,2,2,1,1,2,4,1024]{8,7,6,5,4,3,2,1,0:T(4,128)S(1)} collective-permute-done((f32[2,1,2,2,1,1,2,4,1024]{8,7,6,5,4,3,2,1,0:T(4,128)S(1)}, f32[2,1,2,2,1,1,2,4,1024]{8,7,6,5,4,3,2,1,0:T(4,128)S(1)}, u32[]{:S(2)}, u32[]{:S(2)}) %collective-permute-start.6) | collective-permute-done | bytes 262176 | tf_op jit(solution)/shard_map/ppermute | solution.py:42
  156.9 5.8 %collective-permute-start.7 = (f32[2,1,2,1,1,1,2,4,1024]{8,7,6,5,4,3,2,1,0:T(4,128)S(1)}, f32[2,1,2,1,1,1,2,4,1024]{8,7,6,5,4,3,2,1,0:T(4,128)S(1)}, u32[]{:S(2)}, u32[]{:S(2)}) collective-permute-start(f32[2,1,2,1,1,1,2,4,1024]{8,7,6,5,4,3,2,1,0:T(4,128)S(1)} %slice_select_fusion.2), channel_id=1, source_target_pairs={{0,4},{1,5},{2,6},{3,7},{4,0},{5,1},{6,2},{7,3},{8,12},{9,13},{10,... | collective-permute-start | bytes 393224 | tf_op jit(solution)/shard_map/ppermute | solution.py:42
  162.7 1.4 fusion.13
  164.1 4.3 %collective-permute-done.7 = f32[2,1,2,1,1,1,2,4,1024]{8,7,6,5,4,3,2,1,0:T(4,128)S(1)} collective-permute-done((f32[2,1,2,1,1,1,2,4,1024]{8,7,6,5,4,3,2,1,0:T(4,128)S(1)}, f32[2,1,2,1,1,1,2,4,1024]{8,7,6,5,4,3,2,1,0:T(4,128)S(1)}, u32[]{:S(2)}, u32[]{:S(2)}) %collective-permute-start.7) | collective-permute-done | bytes 131104 | tf_op jit(solution)/shard_map/ppermute | solution.py:42
  168.5 2.2 collective-permute-start.8
  170.9 3.5 %collective-permute-done.8 = f32[1,1,2,1,1,1,2,4,1024]{8,7,6,5,4,3,2,1,0:T(4,128)S(1)} collective-permute-done((f32[1,1,2,1,1,1,2,4,1024]{8,7,6,5,4,3,2,1,0:T(4,128)S(1)}, f32[1,1,2,1,1,1,2,4,1024]{8,7,6,5,4,3,2,1,0:T(4,128)S(1)}, u32[]{:S(2)}, u32[]{:S(2)}) %collective-permute-start.8) | collective-permute-done | bytes 65568 | tf_op jit(solution)/shard_map/ppermute | solution.py:42
  174.4 2.4 %collective-permute-start.9 = (f32[1,1,1,1,1,1,2,4,1024]{8,7,6,5,4,3,2,1,0:T(4,128)S(1)}, f32[1,1,1,1,1,1,2,4,1024]{8,7,6,5,4,3,2,1,0:T(4,128)S(1)}, u32[]{:S(2)}, u32[]{:S(2)}) collective-permute-start(f32[1,1,1,1,1,1,2,4,1024]{8,7,6,5,4,3,2,1,0:T(4,128)S(1)} %slice_select_fusion.4), channel_id=1, source_target_pairs={{0,8},{1,9},{2,10},{3,11},{4,12},{5,13},{6,14},{7,15},{8,0},{9,1},... | collective-permute-start | bytes 98312 | tf_op jit(solution)/shard_map/ppermute | solution.py:42
  176.9 5.4 %collective-permute-done.9 = f32[1,1,1,1,1,1,2,4,1024]{8,7,6,5,4,3,2,1,0:T(4,128)S(1)} collective-permute-done((f32[1,1,1,1,1,1,2,4,1024]{8,7,6,5,4,3,2,1,0:T(4,128)S(1)}, f32[1,1,1,1,1,1,2,4,1024]{8,7,6,5,4,3,2,1,0:T(4,128)S(1)}, u32[]{:S(2)}, u32[]{:S(2)}) %collective-permute-start.9) | collective-permute-done | bytes 32800 | tf_op jit(solution)/shard_map/ppermute | solution.py:42
  182.3 1.8 collective-permute-start.10
  185.0 3.9 %all-to-all-start.2 = ((bf16[32,24,256]{2,1,0:T(8,128)(2,1)}), bf16[32,24,256]{2,1,0:T(8,128)(2,1)S(1)}, u32[]{:S(2)}, u32[]{:S(2)}) async-start(bf16[32,24,256]{2,1,0:T(8,128)(2,1)} %select_convert_fusion), calls=%async_computation.2 | async-start | bytes 786432 | tf_op jit(solution)/shard_map/all_to_all | solution.py:179
  188.9 3.6 %collective-permute-start.11 = (f32[2,4,1024]{2,1,0:T(4,128)S(1)}, f32[2,4,1024]{2,1,0:T(4,128)S(1)}, u32[]{:S(2)}, u32[]{:S(2)}) collective-permute-start(f32[2,4,1024]{2,1,0:T(4,128)S(1)} %add.123), channel_id=1, source_target_pairs={{0,128},{64,192},{128,0},{192,64},{1,129},{65,193},{129,1},{193,65... | collective-permute-start | bytes 98312 | tf_op jit(solution)/shard_map/ppermute | solution.py:49
  192.6 4.1 %collective-permute-done.11 = f32[2,4,1024]{2,1,0:T(4,128)S(1)} collective-permute-done((f32[2,4,1024]{2,1,0:T(4,128)S(1)}, f32[2,4,1024]{2,1,0:T(4,128)S(1)}, u32[]{:S(2)}, u32[]{:S(2)}) %collective-permute-start.11) | collective-permute-done | bytes 32800 | tf_op jit(solution)/shard_map/ppermute | solution.py:49
  200.2 2.1 collective-permute-start.2
  202.3 5.6 %collective-permute-start.3 = (bf16[8,2,24,256]{3,0,2,1:T(8,128)(2,1)S(1)}, bf16[8,2,24,256]{3,0,2,1:T(8,128)(2,1)S(1)}, u32[]{:S(2)}, u32[]{:S(2)}) collective-permute-start(bf16[8,2,24,256]{3,0,2,1:T(8,128)(2,1)S(1)} %get-tuple-element.31), channel_id=1, source_target_pairs={{1,0},{2,1},{3,2},{4,3},{5,4},{6,5},{7,6},{8,7},{9,8},{10,9},{11,1... | collective-permute-start | bytes 589832 | tf_op jit(solution)/shard_map/ppermute | solution.py:63
  209.8 3.4 %collective-permute-done.14 = f32[8,128]{1,0:T(8,128)S(1)} collective-permute-done((f32[8,128]{1,0:T(8,128)S(1)}, f32[8,128]{1,0:T(8,128)S(1)}, u32[]{:S(2)}, u32[]{:S(2)}) %collective-permute-start.14) | collective-permute-done | bytes 4128 | tf_op jit(solution)/shard_map/ppermute | solution.py:49
  213.2 1.4 collective-permute-start.15
  214.6 6.1 %collective-permute-done.15 = f32[8,128]{1,0:T(8,128)S(1)} collective-permute-done((f32[8,128]{1,0:T(8,128)S(1)}, f32[8,128]{1,0:T(8,128)S(1)}, u32[]{:S(2)}, u32[]{:S(2)}) %collective-permute-start.15) | collective-permute-done | bytes 4128 | tf_op jit(solution)/shard_map/ppermute | solution.py:49
  220.8 3.5 %collective-permute-done.16 = f32[8,128]{1,0:T(8,128)S(1)} collective-permute-done((f32[8,128]{1,0:T(8,128)S(1)}, f32[8,128]{1,0:T(8,128)S(1)}, u32[]{:S(2)}, u32[]{:S(2)}) %collective-permute-start.16) | collective-permute-done | bytes 4128 | tf_op jit(solution)/shard_map/ppermute | solution.py:49
  224.3 2.1 collective-permute-start.17
  226.5 1.7 gather_fusion.1
  (126 shorter events, 25.6 us)
Async XLA Ops:
  0.6 39.3 %copy-start = (bf16[2,256,768]{2,1,0:T(8,128)(2,1)S(1)}, bf16[2,256,768]{2,1,0:T(8,128)(2,1)}, u32[]{:S(2)}) copy-start(bf16[2,256,768]{2,1,0:T(8,128)(2,1)} %param.11) | copy-start | bytes 2359300
  0.6 16.6 %copy-start.22 = (s32[32]{0:T(128)S(1)}, s32[32]{0:T(128)}, u32[]{:S(2)}) copy-start(s32[32]{0:T(128)} %param.9) | copy-start | bytes 388
  0.7 16.6 %copy-start.21 = (s32[32]{0:T(128)S(1)}, s32[32]{0:T(128)}, u32[]{:S(2)}) copy-start(s32[32]{0:T(128)} %param.8) | copy-start | bytes 388
  0.7 17.5 %copy-start.17 = (s32[32,2]{0,1:T(2,128)S(1)}, s32[32,2]{0,1:T(2,128)}, u32[]{:S(2)}) copy-start(s32[32,2]{0,1:T(2,128)} %param.10) | copy-start | bytes 772
  2.7 20.2 %all-to-all-start.1 = ((bf16[8,96,256]{2,0,1:T(8,128)(2,1)}), bf16[8,96,256]{2,0,1:T(8,128)(2,1)S(1)}, u32[]{:S(2)}, u32[]{:S(2)}) async-start(bf16[8,96,256]{2,0,1:T(8,128)(2,1)} %bitcast.10), calls=%async_computation.1 | async-start | bytes 786432 | tf_op jit(solution)/shard_map/all_to_all | solution.py:103
  8.4 10.2 %collective-permute-start = (bf16[8,2,24,256]{3,0,2,1:T(8,128)(2,1)S(1)}, bf16[8,2,24,256]{3,0,2,1:T(8,128)(2,1)S(1)}, u32[]{:S(2)}, u32[]{:S(2)}) collective-permute-start(bf16[8,2,24,256]{3,0,2,1:T(8,128)(2,1)S(1)} %get-tuple-element.32), channel_id=1, source_target_pairs={{0,1},{1,2},{2,3},{3,4},{4,5},{5,6},{6,7},{7,8},{8,9},{9,10},{10,1... | collective-permute-start | bytes 589832 | tf_op jit(solution)/shard_map/ppermute | solution.py:61
  10.4 10.1 %collective-permute-start.1 = (bf16[8,2,24,256]{3,0,2,1:T(8,128)(2,1)S(1)}, bf16[8,2,24,256]{3,0,2,1:T(8,128)(2,1)S(1)}, u32[]{:S(2)}, u32[]{:S(2)}) collective-permute-start(bf16[8,2,24,256]{3,0,2,1:T(8,128)(2,1)S(1)} %get-tuple-element.33), channel_id=1, source_target_pairs={{1,0},{2,1},{3,2},{4,3},{5,4},{6,5},{7,6},{8,7},{9,8},{10,9},{11,1... | collective-permute-start | bytes 589832 | tf_op jit(solution)/shard_map/ppermute | solution.py:63
  18.0 0.7 copy-start.19
  20.5 7.4 %copy-start.15 = (bf16[2,256,256]{2,1,0:T(8,128)(2,1)S(1)}, bf16[2,256,256]{2,1,0:T(8,128)(2,1)}, u32[]{:S(2)}) copy-start(bf16[2,256,256]{2,1,0:T(8,128)(2,1)} %param.12) | copy-start | bytes 786436
  23.0 16.9 %all-to-all-start = ((bf16[8,96,256]{2,0,1:T(8,128)(2,1)}), bf16[8,96,256]{2,0,1:T(8,128)(2,1)S(1)}, u32[]{:S(2)}, u32[]{:S(2)}) async-start(bf16[8,96,256]{2,0,1:T(8,128)(2,1)} %bitcast.1), calls=%async_computation | async-start | bytes 786432 | tf_op jit(solution)/shard_map/all_to_all | solution.py:102
  27.9 0.8 copy-start.9
  35.0 3.4 %copy-start.4 = (bf16[4,8,24,8,32]{4,3,2,1,0:T(8,128)(2,1)S(1)}, bf16[4,8,24,8,32]{4,3,2,1,0:T(8,128)(2,1)}, u32[]{:S(2)}) copy-start(bf16[4,8,24,8,32]{4,3,2,1,0:T(8,128)(2,1)} %squeeze.36) | copy-start | bytes 1179652
  35.0 3.4 %copy-start.18 = (pred[4,8]{1,0:T(4,128)(4,1)S(1)}, pred[4,8]{1,0:T(4,128)(4,1)}, u32[]{:S(2)}) copy-start(pred[4,8]{1,0:T(4,128)(4,1)} %broadcast_in_dim.97) | copy-start | bytes 100
  47.3 3.8 %copy-start.11 = (bf16[32,24,256]{0,2,1:T(8,128)(2,1)}, bf16[32,24,256]{0,2,1:T(8,128)(2,1)S(1)}, u32[]{:S(2)}) copy-start(bf16[32,24,256]{0,2,1:T(8,128)(2,1)S(1)} %copy.157) | copy-start | bytes 1179652
  51.1 1.6 copy-start.5
  51.1 10.8 %copy-start.16 = (f32[24,8,32]{2,1,0:T(8,128)}, f32[24,8,32]{2,1,0:T(8,128)S(1)}, u32[]{:S(2)}) copy-start(f32[24,8,32]{2,1,0:T(8,128)S(1)} %get-tuple-element.39) | copy-start | bytes 73732
  55.7 3.3 %copy-start.1 = (bf16[32,24,256]{0,2,1:T(8,128)(2,1)S(1)}, bf16[32,24,256]{0,2,1:T(8,128)(2,1)}, u32[]{:S(2)}) copy-start(bf16[32,24,256]{0,2,1:T(8,128)(2,1)} %copy.158) | copy-start | bytes 1179652
  55.7 3.3 %copy-start.3 = (bf16[32,24,8,32]{3,2,1,0:T(8,128)(2,1)S(1)}, bf16[32,24,8,32]{3,2,1,0:T(8,128)(2,1)}, u32[]{:S(2)}) copy-start(bf16[32,24,8,32]{3,2,1,0:T(8,128)(2,1)} %broadcast_select_fusion) | copy-start | bytes 1179652
  59.0 2.9 %copy-start.12 = (bf16[32,24,256]{0,2,1:T(8,128)(2,1)S(1)}, bf16[32,24,256]{0,2,1:T(8,128)(2,1)}, u32[]{:S(2)}) copy-start(bf16[32,24,256]{0,2,1:T(8,128)(2,1)} %copy-done.11) | copy-start | bytes 1179652
  70.2 6.7 %copy-start.7 = (bf16[4,8,24,8,32]{4,3,2,1,0:T(8,128)(2,1)S(1)}, bf16[4,8,24,8,32]{4,3,2,1,0:T(8,128)(2,1)}, u32[]{:S(2)}) copy-start(bf16[4,8,24,8,32]{4,3,2,1,0:T(8,128)(2,1)} %broadcast_select_fusion.1) | copy-start | bytes 1179652
  70.2 6.7 %copy-start.8 = (bf16[24,8,32,32]{3,2,1,0:T(8,128)(2,1)S(1)}, bf16[24,8,32,32]{3,2,1,0:T(8,128)(2,1)}, u32[]{:S(2)}) copy-start(bf16[24,8,32,32]{3,2,1,0:T(8,128)(2,1)} %copy.125) | copy-start | bytes 1179652
  99.4 5.6 %copy-start.13 = (bf16[1,32,24,768]{3,1,2,0:T(8,128)(2,1)S(1)}, bf16[1,32,24,768]{3,1,2,0:T(8,128)(2,1)}, u32[]{:S(2)}) copy-start(bf16[1,32,24,768]{3,1,2,0:T(8,128)(2,1)} %subtract_convert_fusion) | copy-start | bytes 3538948
  99.4 5.6 %copy-start.20 = (pred[2,32]{1,0:T(4,128)(4,1)S(1)}, pred[2,32]{1,0:T(4,128)(4,1)}, u32[]{:S(2)}) copy-start(pred[2,32]{1,0:T(4,128)(4,1)} %copy-done.19) | copy-start | bytes 196
  107.8 1.0 copy-start.10
  107.8 1.1 copy-start.14
  114.5 1.0 copy-start.2
  116.4 2.9 %collective-permute-start.4 = (f32[2,2,2,2,2,1,2,4,1024]{8,7,6,5,4,3,2,1,0:T(4,128)S(1)}, f32[2,2,2,2,2,1,2,4,1024]{8,7,6,5,4,3,2,1,0:T(4,128)}, u32[]{:S(2)}, u32[]{:S(2)}) collective-permute-start(f32[2,2,2,2,2,1,2,4,1024]{8,7,6,5,4,3,2,1,0:T(4,128)S(1)} %copy_select_fusion), channel_id=1, source_target_pairs={{0,1},{1,0},{2,3},{3,2},{4,5},{5,4},{6,7},{7,6},{8,9},{9,8},{10,11... | collective-permute-start | bytes 3145736 | tf_op jit(solution)/shard_map/ppermute | solution.py:42
  122.8 24.1 %collective-permute-start.5 = (f32[2,2,2,2,1,1,2,4,1024]{8,7,6,5,4,3,2,1,0:T(4,128)}, f32[2,2,2,2,1,1,2,4,1024]{8,7,6,5,4,3,2,1,0:T(4,128)}, u32[]{:S(2)}, u32[]{:S(2)}) collective-permute-start(f32[2,2,2,2,1,1,2,4,1024]{8,7,6,5,4,3,2,1,0:T(4,128)} %slice_select_fusion), channel_id=1, source_target_pairs={{0,2},{1,3},{2,0},{3,1},{4,6},{5,7},{6,4},{7,5},{8,10},{9,11},{10,... | collective-permute-start | bytes 1572872 | tf_op jit(solution)/shard_map/ppermute | solution.py:42
  145.8 1.1 copy-start.6
  148.4 8.4 %collective-permute-start.6 = (f32[2,1,2,2,1,1,2,4,1024]{8,7,6,5,4,3,2,1,0:T(4,128)S(1)}, f32[2,1,2,2,1,1,2,4,1024]{8,7,6,5,4,3,2,1,0:T(4,128)S(1)}, u32[]{:S(2)}, u32[]{:S(2)}) collective-permute-start(f32[2,1,2,2,1,1,2,4,1024]{8,7,6,5,4,3,2,1,0:T(4,128)S(1)} %slice_select_fusion.1), channel_id=1, source_target_pairs={{0,16},{1,17},{2,18},{3,19},{4,20},{5,21},{6,22},{7,23},{8,24},{9,... | collective-permute-start | bytes 786440 | tf_op jit(solution)/shard_map/ppermute | solution.py:42
  156.9 11.5 %collective-permute-start.7 = (f32[2,1,2,1,1,1,2,4,1024]{8,7,6,5,4,3,2,1,0:T(4,128)S(1)}, f32[2,1,2,1,1,1,2,4,1024]{8,7,6,5,4,3,2,1,0:T(4,128)S(1)}, u32[]{:S(2)}, u32[]{:S(2)}) collective-permute-start(f32[2,1,2,1,1,1,2,4,1024]{8,7,6,5,4,3,2,1,0:T(4,128)S(1)} %slice_select_fusion.2), channel_id=1, source_target_pairs={{0,4},{1,5},{2,6},{3,7},{4,0},{5,1},{6,2},{7,3},{8,12},{9,13},{10,... | collective-permute-start | bytes 393224 | tf_op jit(solution)/shard_map/ppermute | solution.py:42
  168.5 5.9 %collective-permute-start.8 = (f32[1,1,2,1,1,1,2,4,1024]{8,7,6,5,4,3,2,1,0:T(4,128)S(1)}, f32[1,1,2,1,1,1,2,4,1024]{8,7,6,5,4,3,2,1,0:T(4,128)S(1)}, u32[]{:S(2)}, u32[]{:S(2)}) collective-permute-start(f32[1,1,2,1,1,1,2,4,1024]{8,7,6,5,4,3,2,1,0:T(4,128)S(1)} %slice_select_fusion.3), channel_id=1, source_target_pairs={{0,32},{1,33},{2,34},{3,35},{4,36},{5,37},{6,38},{7,39},{8,40},{9,... | collective-permute-start | bytes 196616 | tf_op jit(solution)/shard_map/ppermute | solution.py:42
  174.4 7.9 %collective-permute-start.9 = (f32[1,1,1,1,1,1,2,4,1024]{8,7,6,5,4,3,2,1,0:T(4,128)S(1)}, f32[1,1,1,1,1,1,2,4,1024]{8,7,6,5,4,3,2,1,0:T(4,128)S(1)}, u32[]{:S(2)}, u32[]{:S(2)}) collective-permute-start(f32[1,1,1,1,1,1,2,4,1024]{8,7,6,5,4,3,2,1,0:T(4,128)S(1)} %slice_select_fusion.4), channel_id=1, source_target_pairs={{0,8},{1,9},{2,10},{3,11},{4,12},{5,13},{6,14},{7,15},{8,0},{9,1},... | collective-permute-start | bytes 98312 | tf_op jit(solution)/shard_map/ppermute | solution.py:42
  182.3 6.6 %collective-permute-start.10 = (f32[2,4,1024]{2,1,0:T(4,128)S(1)}, f32[2,4,1024]{2,1,0:T(4,128)S(1)}, u32[]{:S(2)}, u32[]{:S(2)}) collective-permute-start(f32[2,4,1024]{2,1,0:T(4,128)S(1)} %add_bitcast_fusion), channel_id=1, source_target_pairs={{0,64},{64,0},{128,192},{192,128},{1,65},{65,1},{129,193},{193,129... | collective-permute-start | bytes 98312 | tf_op jit(solution)/shard_map/ppermute | solution.py:49
  185.0 13.3 %all-to-all-start.2 = ((bf16[32,24,256]{2,1,0:T(8,128)(2,1)}), bf16[32,24,256]{2,1,0:T(8,128)(2,1)S(1)}, u32[]{:S(2)}, u32[]{:S(2)}) async-start(bf16[32,24,256]{2,1,0:T(8,128)(2,1)} %select_convert_fusion), calls=%async_computation.2 | async-start | bytes 786432 | tf_op jit(solution)/shard_map/all_to_all | solution.py:179
  188.9 7.7 %collective-permute-start.11 = (f32[2,4,1024]{2,1,0:T(4,128)S(1)}, f32[2,4,1024]{2,1,0:T(4,128)S(1)}, u32[]{:S(2)}, u32[]{:S(2)}) collective-permute-start(f32[2,4,1024]{2,1,0:T(4,128)S(1)} %add.123), channel_id=1, source_target_pairs={{0,128},{64,192},{128,0},{192,64},{1,129},{65,193},{129,1},{193,65... | collective-permute-start | bytes 98312 | tf_op jit(solution)/shard_map/ppermute | solution.py:49
  197.9 1.5 collective-permute-start.12
  200.1 7.8 %collective-permute-start.13 = (f32[8,128]{1,0:T(8,128)S(1)}, f32[8,128]{1,0:T(8,128)S(1)}, u32[]{:S(2)}, u32[]{:S(2)}) collective-permute-start(f32[8,128]{1,0:T(8,128)S(1)} %broadcast_add_fusion), channel_id=1, source_target_pairs={{0,2},{1,3},{2,0},{3,1},{4,6},{5,7},{6,4},{7,5},{8,10},{9,11},{10,... | collective-permute-start | bytes 12296 | tf_op jit(solution)/shard_map/ppermute | solution.py:49
  200.2 26.2 %collective-permute-start.2 = (bf16[8,2,24,256]{3,0,2,1:T(8,128)(2,1)S(1)}, bf16[8,2,24,256]{3,0,2,1:T(8,128)(2,1)S(1)}, u32[]{:S(2)}, u32[]{:S(2)}) collective-permute-start(bf16[8,2,24,256]{3,0,2,1:T(8,128)(2,1)S(1)} %get-tuple-element.30), channel_id=1, source_target_pairs={{0,1},{1,2},{2,3},{3,4},{4,5},{5,6},{6,7},{7,8},{8,9},{9,10},{10,1... | collective-permute-start | bytes 589832 | tf_op jit(solution)/shard_map/ppermute | solution.py:61
  202.3 24.1 %collective-permute-start.3 = (bf16[8,2,24,256]{3,0,2,1:T(8,128)(2,1)S(1)}, bf16[8,2,24,256]{3,0,2,1:T(8,128)(2,1)S(1)}, u32[]{:S(2)}, u32[]{:S(2)}) collective-permute-start(bf16[8,2,24,256]{3,0,2,1:T(8,128)(2,1)S(1)} %get-tuple-element.31), channel_id=1, source_target_pairs={{1,0},{2,1},{3,2},{4,3},{5,4},{6,5},{7,6},{8,7},{9,8},{10,9},{11,1... | collective-permute-start | bytes 589832 | tf_op jit(solution)/shard_map/ppermute | solution.py:63
  208.6 4.6 %collective-permute-start.14 = (f32[8,128]{1,0:T(8,128)S(1)}, f32[8,128]{1,0:T(8,128)S(1)}, u32[]{:S(2)}, u32[]{:S(2)}) collective-permute-start(f32[8,128]{1,0:T(8,128)S(1)} %fusion.78), channel_id=1, source_target_pairs={{0,4},{1,5},{2,6},{3,7},{4,0},{5,1},{6,2},{7,3},{8,12},{9,13},{10,... | collective-permute-start | bytes 12296 | tf_op jit(solution)/shard_map/ppermute | solution.py:49
  213.2 7.5 %collective-permute-start.15 = (f32[8,128]{1,0:T(8,128)S(1)}, f32[8,128]{1,0:T(8,128)S(1)}, u32[]{:S(2)}, u32[]{:S(2)}) collective-permute-start(f32[8,128]{1,0:T(8,128)S(1)} %add.127), channel_id=1, source_target_pairs={{0,8},{1,9},{2,10},{3,11},{4,12},{5,13},{6,14},{7,15},{8,0},{9,1},... | collective-permute-start | bytes 12296 | tf_op jit(solution)/shard_map/ppermute | solution.py:49
  220.7 3.6 %collective-permute-start.16 = (f32[8,128]{1,0:T(8,128)S(1)}, f32[8,128]{1,0:T(8,128)S(1)}, u32[]{:S(2)}, u32[]{:S(2)}) collective-permute-start(f32[8,128]{1,0:T(8,128)S(1)} %add.128), channel_id=1, source_target_pairs={{0,16},{1,17},{2,18},{3,19},{4,20},{5,21},{6,22},{7,23},{8,24},{9,... | collective-permute-start | bytes 12296 | tf_op jit(solution)/shard_map/ppermute | solution.py:49
  224.3 5.1 %collective-permute-start.17 = (f32[8,128]{1,0:T(8,128)S(1)}, f32[8,128]{1,0:T(8,128)S(1)}, u32[]{:S(2)}, u32[]{:S(2)}) collective-permute-start(f32[8,128]{1,0:T(8,128)S(1)} %add.129), channel_id=1, source_target_pairs={{0,32},{1,33},{2,34},{3,35},{4,36},{5,37},{6,38},{7,39},{8,40},{9,... | collective-permute-start | bytes 12296 | tf_op jit(solution)/shard_map/ppermute | solution.py:49

commit v3 on v2

--- a/solution.py
+++ b/solution.py
@@ -1,8 +1,10 @@
+import functools
 import math
 
 import jax
 import jax.numpy as jnp
 from jax import lax
+from jax.experimental import pallas as pl
 from jax.sharding import PartitionSpec as P
 
 HEADS = 8
@@ -80,6 +82,96 @@
         )
 
     return jax.vmap(pick_one)(padded, offsets)
+
+
+def attention_kernel(block_size, valid_ref, qkv_ref, da_ref, att_ref, split_ref):
+    f32 = jnp.float32
+    bf16 = jnp.bfloat16
+    cells, agents, channels = da_ref.shape
+    head_size = channels // HEADS
+    blocks = agents // block_size
+    rows = blocks * HEADS * block_size
+    scale = head_size ** (-0.5)
+    dims_nt = (((1,), (1,)), ((), ()))
+    dims_tn = (((0,), (0,)), ((), ()))
+    lane = lax.broadcasted_iota(jnp.int32, (HEADS, channels), 1)
+    head = lax.broadcasted_iota(jnp.int32, (HEADS, channels), 0)
+    head_mask = (lane // head_size == head).astype(f32).reshape(1, HEADS, 1, channels)
+    row_id = lax.broadcasted_iota(jnp.int32, (rows, agents), 0)
+    col_id = lax.broadcasted_iota(jnp.int32, (rows, agents), 1)
+    row_agent = (row_id // (HEADS * block_size)) * block_size + row_id % block_size
+    allowed = (valid_ref[...] > 0.5) | (row_agent == col_id)
+
+    def stack(x):
+        spread = x.astype(f32).reshape(blocks, 1, block_size, channels) * head_mask
+        return spread.reshape(rows, channels).astype(bf16)
+
+    def unstack(y):
+        return jnp.sum(y.reshape(blocks, HEADS, block_size, channels) * head_mask, axis=1).reshape(
+            agents, channels
+        )
+
+    def one_cell(c, carry):
+        q = qkv_ref[c, :, 0:channels]
+        k = qkv_ref[c, :, channels : 2 * channels]
+        v = qkv_ref[c, :, 2 * channels : 3 * channels]
+        q_rows = stack(q)
+        da_rows = stack(da_ref[c])
+        scores = lax.dot_general(q_rows, k, dims_nt, preferred_element_type=f32) * scale
+        raised = jnp.where(allowed, jnp.exp(scores), f32(0.0))
+        prob = raised / jnp.sum(raised, axis=1, keepdims=True)
+        prob_low = prob.astype(bf16)
+        att = unstack(jnp.dot(prob_low, v, preferred_element_type=f32))
+        att_ref[c] = att.astype(bf16)
+        prob_grad = lax.dot_general(da_rows, v, dims_nt, preferred_element_type=f32)
+        score_grad = (
+            prob * (prob_grad - jnp.sum(prob * prob_grad, axis=1, keepdims=True)) * scale
+        ).astype(bf16)
+        d_q = unstack(jnp.dot(score_grad, k, preferred_element_type=f32)).astype(bf16).astype(f32)
+        d_k = jnp.zeros((agents, channels), f32)
+        d_v = jnp.zeros((agents, channels), f32)
+        for n in range(blocks):
+            part = slice(n * HEADS * block_size, (n + 1) * HEADS * block_size)
+            d_k = d_k + lax.dot_general(
+                score_grad[part], q_rows[part], dims_tn, preferred_element_type=f32
+            ).astype(bf16).astype(f32)
+            d_v = d_v + lax.dot_general(
+                prob_low[part], da_rows[part], dims_tn, preferred_element_type=f32
+            ).astype(bf16).astype(f32)
+        for i, d in enumerate((d_q, d_k, d_v)):
+            hi = d.astype(bf16)
+            split_ref[0, c, :, i * channels : (i + 1) * channels] = hi
+            split_ref[1, c, :, i * channels : (i + 1) * channels] = (d - hi.astype(f32)).astype(bf16)
+        return carry
+
+    lax.fori_loop(0, cells, one_cell, 0)
+
+
+def cell_attention(valid_row, qkv, d_attended, block_size):
+    cells, agents, channels = d_attended.shape
+    step = 4 if cells % 4 == 0 else 1
+    return pl.pallas_call(
+        functools.partial(attention_kernel, block_size),
+        grid=(cells // step,),
+        in_specs=[
+            pl.BlockSpec((1, agents), lambda i: (0, 0)),
+            pl.BlockSpec((step, agents, 3 * channels), lambda i: (i, 0, 0)),
+            pl.BlockSpec((step, agents, channels), lambda i: (i, 0, 0)),
+        ],
+        out_specs=[
+            pl.BlockSpec((step, agents, channels), lambda i: (i, 0, 0)),
+            pl.BlockSpec((2, step, agents, 3 * channels), lambda i: (0, i, 0, 0)),
+        ],
+        out_shape=[
+            jax.ShapeDtypeStruct((cells, agents, channels), jnp.bfloat16),
+            jax.ShapeDtypeStruct((2, cells, agents, 3 * channels), jnp.bfloat16),
+        ],
+        cost_estimate=pl.CostEstimate(
+            flops=cells * 48 * agents * HEADS * agents * channels,
+            transcendentals=cells * agents * HEADS * agents,
+            bytes_accessed=cells * agents * channels * 2 * 11,
+        ),
+    )(valid_row, qkv, d_attended)
 
 
 def body(feats, types, valid, offsets, w_qkv, w_out, d_out):
@@ -104,85 +196,35 @@
     )
     part_cells = all_feats.shape[1]
     pairs = agents * part_cells
-    is_type1 = (types == 1)[:, None, None]
-    type_mask = jnp.stack([types == 0, types == 1], axis=0)[:, :, None, None]
-    feats_rows = all_feats.reshape(pairs, channels)
-    grads_rows = all_grads.reshape(pairs, channels)
+    is_type1 = (types == 1)[None, :, None]
+    type_mask = jnp.stack([types == 0, types == 1], axis=0)[:, None, :, None]
+    feats_cm = jnp.transpose(all_feats, (1, 0, 2))
+    grads_cm = jnp.transpose(all_grads, (1, 0, 2))
     qkv_both = jnp.einsum(
-        "pc,tce->tpe", feats_rows, w_qkv, preferred_element_type=f32
-    ).astype(bf16).reshape(2, agents, part_cells, 3 * channels)
+        "gac,tce->tgae", feats_cm, w_qkv, preferred_element_type=f32
+    ).astype(bf16)
     qkv = jnp.where(is_type1, qkv_both[1], qkv_both[0])
-    query_heads = qkv[..., :channels].reshape(agents, part_cells, HEADS, head_size)
-    key_heads = qkv[..., channels : 2 * channels].reshape(agents, part_cells, HEADS, head_size)
-    value_heads = qkv[..., 2 * channels :].reshape(agents, part_cells, HEADS, head_size)
-    scores = (
-        jnp.einsum("aghd,bghd->ghab", query_heads, key_heads, preferred_element_type=f32)
-        * score_scale
-    )
-    agent_ids = jnp.arange(agents)
-    allowed = (valid[None, :] == 1) | (agent_ids[:, None] == agent_ids[None, :])
-    raised = jnp.where(allowed, jnp.exp(scores), f32(0.0))
-    attn_prob = raised / jnp.sum(raised, axis=-1, keepdims=True)
-    prob_low = attn_prob.astype(bf16)
-    attended = (
-        jnp.einsum("ghab,bghd->aghd", prob_low, value_heads, preferred_element_type=f32)
-        .astype(bf16)
-        .reshape(agents, part_cells, channels)
-    )
     d_att_both = jnp.einsum(
-        "pe,tce->tpc", grads_rows, w_out, preferred_element_type=f32
-    ).astype(bf16).reshape(2, agents, part_cells, channels)
+        "gae,tce->tgac", grads_cm, w_out, preferred_element_type=f32
+    ).astype(bf16)
     d_attended = jnp.where(is_type1, d_att_both[1], d_att_both[0])
+    valid_row = (valid == 1).astype(f32).reshape(1, agents)
+    attended, d_split = cell_attention(valid_row, qkv, d_attended, own_count)
     attended_typed = jnp.where(type_mask, attended[None], jnp.zeros((), bf16))
     raw_out = jnp.einsum(
-        "tpc,pe->tce",
-        attended_typed.reshape(2, pairs, channels),
-        grads_rows,
-        preferred_element_type=f32,
-    )
-    attended_heads = d_attended.reshape(agents, part_cells, HEADS, head_size)
-    prob_grad = jnp.einsum(
-        "aghd,bghd->ghab", attended_heads, value_heads, preferred_element_type=f32
-    )
-    score_grad = (
-        attn_prob
-        * (prob_grad - jnp.sum(attn_prob * prob_grad, axis=-1, keepdims=True))
-        * score_scale
-    ).astype(bf16)
-    d_query = (
-        jnp.einsum("ghab,bghd->aghd", score_grad, key_heads, preferred_element_type=f32)
-        .astype(bf16)
-        .reshape(agents, part_cells, channels)
-    )
-    groups_n = agents // own_count
-    grad_blocks = score_grad.reshape(part_cells, HEADS, groups_n, own_count, agents)
-    prob_blocks = prob_low.reshape(part_cells, HEADS, groups_n, own_count, agents)
-    query_blocks = query_heads.reshape(groups_n, own_count, part_cells, HEADS, head_size)
-    dattn_blocks = attended_heads.reshape(groups_n, own_count, part_cells, HEADS, head_size)
-    key_parts = jnp.einsum(
-        "ghnyb,nyghd->nbghd", grad_blocks, query_blocks, preferred_element_type=f32
-    ).astype(bf16)
-    value_parts = jnp.einsum(
-        "ghnyb,nyghd->nbghd", prob_blocks, dattn_blocks, preferred_element_type=f32
-    ).astype(bf16)
-    key_sum = jnp.sum(key_parts.astype(f32), axis=0).reshape(agents, part_cells, channels)
-    value_sum = jnp.sum(value_parts.astype(f32), axis=0).reshape(agents, part_cells, channels)
-    d_qkv = jnp.concatenate([d_query.astype(f32), key_sum, value_sum], axis=-1)
-    d_hi = d_qkv.astype(bf16)
-    d_lo = (d_qkv - d_hi.astype(f32)).astype(bf16)
-    d_split = jnp.stack([d_hi, d_lo], axis=0).reshape(2, pairs, 3 * channels)
+        "tgac,gae->tce", attended_typed, grads_cm, preferred_element_type=f32
+    )
     d_part_terms = jnp.einsum(
-        "spe,tce->stpc", d_split, w_qkv, preferred_element_type=f32
-    )
-    d_part_sum = (d_part_terms[0] + d_part_terms[1]).reshape(2, agents, part_cells, channels)
+        "sgae,tce->stgac", d_split, w_qkv, preferred_element_type=f32
+    )
+    d_part_sum = d_part_terms[0] + d_part_terms[1]
     d_part = jnp.where(is_type1, d_part_sum[1], d_part_sum[0]).astype(bf16)
+    d_part = jnp.transpose(d_part, (1, 0, 2))
     returned = lax.all_to_all(d_part, "agent", split_axis=0, concat_axis=1, tiled=True)
     d_warped = returned.reshape(own_count, row_count, col_count, channels)
-    feats_typed = jnp.where(type_mask, all_feats[None], jnp.zeros((), bf16)).reshape(
-        2, pairs, channels
-    )
+    feats_typed = jnp.where(type_mask, feats_cm[None], jnp.zeros((), bf16))
     qkv_terms = jnp.einsum(
-        "tpc,spe->stce", feats_typed, d_split, preferred_element_type=f32
+        "tgac,sgae->stce", feats_typed, d_split, preferred_element_type=f32
     )
     raw_qkv = qkv_terms[0] + qkv_terms[1]
     rimmed_grad = with_halo(d_warped, (("tile", 1),), MAXOFF)

time: 235 us -> 166 us (0.71)
  local copies, waits for them, and re-layouts: 73.8 us -> 16.5 us
  matrix products: 34.9 us -> 8.84 us
  Pallas kernels: 0 us -> 19.5 us
  waiting for transfers between devices: 44.1 us -> 61.6 us
  other arithmetic: 24.9 us -> 9.41 us
  starting transfers between devices: 52.1 us -> 47.6 us
    dot_general x11 -> x5, matrix products: 34.9 us -> 8.84 us  [the longest x1 3.13 us: body(): jnp.einsum('tgac,sgae->stce', feats_typed, d_split, preferred_element_typ...]
    concatenate x8 -> x0, local copies, waits for them, and re-layouts: 19.9 us -> none  [body(): d_qkv = jnp.concatenate([d_query.astype(f32), key_sum, value_sum], axis=-1)]
    pallas_call x0 -> x1, Pallas kernels: none -> 19.5 us  [cell_attention(): pl.pallas_call(functools.partial(attention_kernel, block_size), grid=(cel...]
    reduce_sum x2 -> x0, local copies, waits for them, and re-layouts: 9.53 us -> none  [the longest x1 4.77 us: body(): jnp.sum(key_parts.astype(f32), axis=0).reshape(agents, part_cells, channels)]
    ppermute x6, waiting for transfers between devices: 23.4 us -> 31.9 us  [halving_sum(): x = keep + lax.ppermute(send, axis, xor_pairs(count, bit))]
    convert_element_type x3 -> x0, local copies, waits for them, and re-layouts: 7.41 us -> none  [the longest x1 3.75 us: body(): attended = jnp.einsum('ghab,bghd->aghd', prob_low, value_heads, preferred...]
    sub x1 -> x0, other arithmetic: 6.73 us -> none  [body(): prob_grad - jnp.sum(attn_prob * prob_grad, axis=-1, keepdims=True)]
    all_to_all x1, waiting for transfers between devices: 0.01 us -> 6.08 us  [body(): lax.all_to_all(flat_feats, 'agent', split_axis=1, concat_axis=0, tiled=True)]
  transfers between devices with their start and end apart: 21 -> 21, of which waited for: 13 -> 15; matrix products, arithmetic and copies ran while one was open for 20% -> 9% of each run, Pallas kernels for 0% -> 0%
where the time goes in v3:
time: 166 us; the launch traced here: 165 us
  waiting for transfers between devices  61.6 us (37%)
  starting transfers between devices  47.6 us (29%)
  Pallas kernels  19.5 us (12%)
  local copies, waits for them, and re-layouts  16.5 us (10%)
  other arithmetic  9.41 us (6%)
  matrix products  8.84 us (5%)
  between operations  1.86 us (1%)
    ppermute x6, waiting for transfers between devices, halving_sum(): x = keep + lax.ppermute(send, axis, xor_pairs(count, bit))  31.9 us
    pallas_call x1, Pallas kernels, cell_attention(): pl.pallas_call(functools.partial(attention_kernel, block_size), grid=(cel...  19.5 us
    ppermute x8, waiting for transfers between devices, doubling_sum(): x = x + lax.ppermute(x, axis, xor_pairs(count, bit))  19.4 us
    ppermute x2, starting transfers between devices, with_halo(): lax.ppermute(head, axis, [((i + 1) % count, i) for i in range(ends)])  13.3 us
    ppermute x6, starting transfers between devices, halving_sum(): x = keep + lax.ppermute(send, axis, xor_pairs(count, bit))  10.7 us
    ppermute x8, starting transfers between devices, doubling_sum(): x = x + lax.ppermute(x, axis, xor_pairs(count, bit))  8.38 us
    all_to_all x1, waiting for transfers between devices, body(): lax.all_to_all(flat_feats, 'agent', split_axis=1, concat_axis=0, tiled=True)  6.08 us
    all_to_all x1, starting transfers between devices, body(): lax.all_to_all(flat_grads, 'agent', split_axis=1, concat_axis=0, tiled=True)  4.46 us
  transfers between devices with their start and end apart: 21, of which 15 were waited for; matrix products, arithmetic and copies ran while one was open for 9% of the time, Pallas kernels for 0%

profile of v3, /device:TPU:2, one launch (start us, length us, event | category | flops | bytes accessed | tf_op | source)
XLA Modules:
  0.0 165.3 jit_solution(11654960638000430497)
XLA Ops:
  0.7 1.3 copy.46
  2.0 7.2 %collective-permute-start.1 = (bf16[8,2,24,256]{3,0,2,1:T(8,128)(2,1)S(1)}, bf16[8,2,24,256]{3,0,2,1:T(8,128)(2,1)S(1)}, u32[]{:S(2)}, u32[]{:S(2)}) collective-permute-start(bf16[8,2,24,256]{3,0,2,1:T(8,128)(2,1)S(1)} %get-tuple-element.26), channel_id=1, source_target_pairs={{1,0},{2,1},{3,2},{4,3},{5,4},{6,5},{7,6},{8,7},{9,8},{10,9},{11,1... | collective-permute-start | bytes 589832 | tf_op jit(solution)/shard_map/ppermute | solution.py:65
  9.2 1.9 %collective-permute-start = (bf16[8,2,24,256]{3,0,2,1:T(8,128)(2,1)S(1)}, bf16[8,2,24,256]{3,0,2,1:T(8,128)(2,1)S(1)}, u32[]{:S(2)}, u32[]{:S(2)}) collective-permute-start(bf16[8,2,24,256]{3,0,2,1:T(8,128)(2,1)S(1)} %get-tuple-element.25), channel_id=1, source_target_pairs={{0,1},{1,2},{2,3},{3,4},{4,5},{5,6},{6,7},{7,8},{8,9},{9,10},{10,1... | collective-permute-start | bytes 589832 | tf_op jit(solution)/shard_map/ppermute | solution.py:63
  11.2 1.0 copy.52
  12.1 4.5 %all-to-all-start.1 = ((bf16[8,96,256]{2,0,1:T(8,128)(2,1)}), bf16[8,96,256]{2,0,1:T(8,128)(2,1)S(1)}, u32[]{:S(2)}, u32[]{:S(2)}) async-start(bf16[8,96,256]{2,0,1:T(8,128)(2,1)} %bitcast.16), calls=%async_computation.1 | async-start | bytes 786432 | tf_op jit(solution)/shard_map/all_to_all | solution.py:195
  16.7 0.5 fusion.41.valid_ref
  17.2 1.1 collective-permute-done
  18.4 2.4 %gather_fusion = bf16[8,4,24,256]{3,0,2,1:T(8,128)(2,1)} fusion(bf16[8,8,28,256]{3,0,2,1:T(8,128)(2,1)S(1)} %fusion.18, s32[8]{0:T(128)S(1)} %get-tuple-element.28), kind=kCustom, calls=%fused_computation | custom fusion | bytes 786560 | tf_op jit(solution)/shard_map/vmap()/gather | solution.py:80
  20.8 3.1 %all-to-all-done.1 = bf16[8,96,256]{2,0,1:T(8,128)(2,1)S(1)} async-done(((bf16[8,96,256]{2,0,1:T(8,128)(2,1)}), bf16[8,96,256]{2,0,1:T(8,128)(2,1)S(1)}, u32[]{:S(2)}, u32[]{:S(2)}) %all-to-all-start.1) | async-done | bytes 393248 | tf_op jit(solution)/shard_map/all_to_all | solution.py:195
  24.0 3.5 %all-to-all-start = ((bf16[8,96,256]{2,0,1:T(8,128)(2,1)}), bf16[8,96,256]{2,0,1:T(8,128)(2,1)S(1)}, u32[]{:S(2)}, u32[]{:S(2)}) async-start(bf16[8,96,256]{2,0,1:T(8,128)(2,1)} %bitcast.2), calls=%async_computation | async-start | bytes 786432 | tf_op jit(solution)/shard_map/all_to_all | solution.py:194
  27.4 0.4 fusion.12
  27.9 0.8 fusion.29.da_ref
  28.7 6.1 %all-to-all-done = bf16[8,96,256]{2,0,1:T(8,128)(2,1)S(1)} async-done(((bf16[8,96,256]{2,0,1:T(8,128)(2,1)}), bf16[8,96,256]{2,0,1:T(8,128)(2,1)S(1)}, u32[]{:S(2)}, u32[]{:S(2)}) %all-to-all-start) | async-done | bytes 393248 | tf_op jit(solution)/shard_map/all_to_all | solution.py:194
  34.8 0.8 convert_bitcast_fusion
  35.6 1.2 fusion.13.qkv_ref
  36.8 19.5 %shard_map.94 = (bf16[24,32,256]{2,1,0:T(8,128)(2,1)}, bf16[2,24,32,768]{3,2,1,0:T(8,128)(2,1)}) custom-call(f32[1,32]{1,0:T(1,128)} %fusion.41.valid_ref, bf16[24,32,768]{2,1,0:T(8,128)(2,1)} %fusion.13.qkv_ref, bf16[24,32,256]{2,1,0:T(8,128)(2,1)} %fusion.29.da_ref), custom_call_target="tpu_custom_call" | custom-call | flops 2415919104 | bytes 4325376 | tf_op jit(solution)/shard_map/pallas_call | solution.py:153
  56.3 1.4 convolution_bitcast_fusion
  57.8 3.1 %fusion.7 = f32[2,2,256,768]{2,3,1,0:T(8,128)S(1)} fusion(bf16[2,24,32,768]{3,2,1,0:T(8,128)(2,1)} %get-tuple-element.5, pred[2,32]{1,0:T(4,128)(4,1)S(1)} %pad_add_fusion, bf16[24,32,256]{2,1,0:T(8,128)(2,1)S(1)} %bitcast.135), kind=kOutput, calls=%fused_computation.11 | convolution fusion | flops 1208352768 | bytes 5898304 | tf_op jit(solution)/shard_map/tgac,sgae->stce/dot_general | solution.py:226
  60.9 0.2 fusion.11
  61.1 0.1 pad_maximum_fusion
  61.3 2.4 %copy.58 = f32[2,256,1024]{2,0,1:T(2,128)} copy(f32[2,256,1024]{1,2,0:T(8,128)S(1)} %pad_maximum_fusion) | data formatting | bytes 4194304 | tf_op jit(solution)/shard_map/concatenate | solution.py:233
  63.7 2.3 %fusion.49 = (f32[2,2,2,2,2,1,2,4,1024]{8,6,7,5,4,3,2,1,0:T(2,128)S(1)}, f32[2,2,2,2,2,1,2,4,1024]{8,6,7,5,4,3,2,1,0:T(2,128)S(1)}) fusion(f32[2,2,2,2,2,2,2,4,1024]{8,6,7,5,4,3,2,1,0:T(2,128)} %bitcast.127), kind=kLoop, calls=%fused_computation.92 | loop fusion | bytes 4194304 | tf_op jit(solution)/shard_map/slice | solution.py:41
  66.0 1.0 copy-done.1
  67.0 0.9 copy_select_fusion
  68.0 2.8 %collective-permute-done.4 = f32[2,2,2,2,2,1,2,4,1024]{8,7,6,5,4,3,2,1,0:T(4,128)} collective-permute-done((f32[2,2,2,2,2,1,2,4,1024]{8,7,6,5,4,3,2,1,0:T(4,128)S(1)}, f32[2,2,2,2,2,1,2,4,1024]{8,7,6,5,4,3,2,1,0:T(4,128)}, u32[]{:S(2)}, u32[]{:S(2)}) %collective-permute-start.4) | collective-permute-done | bytes 1048608 | tf_op jit(solution)/shard_map/ppermute | solution.py:44
  70.7 2.4 %select_add_fusion = f32[2,2,2,2,2,1,2,4,1024]{8,7,6,5,4,3,2,1,0:T(4,128)S(1)} fusion(f32[2,2,2,2,2,1,2,4,1024]{8,7,6,5,4,3,2,1,0:T(4,128)} %collective-permute-done.4, f32[2,2,2,2,2,1,2,4,1024]{8,6,7,5,4,3,2,1,0:T(2,128)} %copy-done.1, f32[2,2,2,2,2,1,2,4,1024]{8,6,7,5,4,3,2,1,0:T(2,128)S(1)} %get-tuple-element.21, pred[]{:T(512)S(6)} %eq.44), kind=kLoop, calls=%fused_computation.22 | loop fusion | flops 524288 | bytes 4194305 | tf_op jit(solution)/shard_map/add | solution.py:44
  73.1 0.2 slice_select_fusion
  73.3 0.3 collective-permute-start.5
  73.6 13.7 %collective-permute-done.5 = f32[2,2,2,2,1,1,2,4,1024]{8,7,6,5,4,3,2,1,0:T(4,128)S(1)} collective-permute-done((f32[2,2,2,2,1,1,2,4,1024]{8,7,6,5,4,3,2,1,0:T(4,128)S(1)}, f32[2,2,2,2,1,1,2,4,1024]{8,7,6,5,4,3,2,1,0:T(4,128)S(1)}, u32[]{:S(2)}, u32[]{:S(2)}) %collective-permute-start.5) | collective-permute-done | bytes 524320 | tf_op jit(solution)/shard_map/ppermute | solution.py:44
  87.3 0.3 select_add_fusion.1
  87.8 7.5 %collective-permute-done.6 = f32[2,1,2,2,1,1,2,4,1024]{8,7,6,5,4,3,2,1,0:T(4,128)S(1)} collective-permute-done((f32[2,1,2,2,1,1,2,4,1024]{8,7,6,5,4,3,2,1,0:T(4,128)S(1)}, f32[2,1,2,2,1,1,2,4,1024]{8,7,6,5,4,3,2,1,0:T(4,128)S(1)}, u32[]{:S(2)}, u32[]{:S(2)}) %collective-permute-start.6) | collective-permute-done | bytes 262176 | tf_op jit(solution)/shard_map/ppermute | solution.py:44
  95.3 0.1 select_add_fusion.2
  95.5 1.8 %collective-permute-start.7 = (f32[2,1,2,1,1,1,2,4,1024]{8,7,6,5,4,3,2,1,0:T(4,128)S(1)}, f32[2,1,2,1,1,1,2,4,1024]{8,7,6,5,4,3,2,1,0:T(4,128)S(1)}, u32[]{:S(2)}, u32[]{:S(2)}) collective-permute-start(f32[2,1,2,1,1,1,2,4,1024]{8,7,6,5,4,3,2,1,0:T(4,128)S(1)} %slice_select_fusion.2), channel_id=1, source_target_pairs={{0,4},{1,5},{2,6},{3,7},{4,0},{5,1},{6,2},{7,3},{8,12},{9,13},{10,... | collective-permute-start | bytes 393224 | tf_op jit(solution)/shard_map/ppermute | solution.py:44
  97.3 5.8 %collective-permute-done.7 = f32[2,1,2,1,1,1,2,4,1024]{8,7,6,5,4,3,2,1,0:T(4,128)S(1)} collective-permute-done((f32[2,1,2,1,1,1,2,4,1024]{8,7,6,5,4,3,2,1,0:T(4,128)S(1)}, f32[2,1,2,1,1,1,2,4,1024]{8,7,6,5,4,3,2,1,0:T(4,128)S(1)}, u32[]{:S(2)}, u32[]{:S(2)}) %collective-permute-start.7) | collective-permute-done | bytes 131104 | tf_op jit(solution)/shard_map/ppermute | solution.py:44
  103.2 2.7 %collective-permute-start.8 = (f32[1,1,2,1,1,1,2,4,1024]{8,7,6,5,4,3,2,1,0:T(4,128)S(1)}, f32[1,1,2,1,1,1,2,4,1024]{8,7,6,5,4,3,2,1,0:T(4,128)S(1)}, u32[]{:S(2)}, u32[]{:S(2)}) collective-permute-start(f32[1,1,2,1,1,1,2,4,1024]{8,7,6,5,4,3,2,1,0:T(4,128)S(1)} %slice_select_fusion.3), channel_id=1, source_target_pairs={{0,32},{1,33},{2,34},{3,35},{4,36},{5,37},{6,38},{7,39},{8,40},{9,... | collective-permute-start | bytes 196616 | tf_op jit(solution)/shard_map/ppermute | solution.py:44
  105.8 3.1 %fusion.4 = f32[2,2,24,32,256]{4,3,2,1,0:T(8,128)S(1)} fusion(bf16[2,24,32,768]{3,2,1,0:T(8,128)(2,1)} %get-tuple-element.5, bf16[2,256,768]{2,1,0:T(8,128)(2,1)S(1)} %copy-done), kind=kOutput, calls=%fused_computation.10 | convolution fusion | flops 1207959552 | bytes 6291456 | tf_op jit(solution)/shard_map/sgae,tce->stgac/dot_general | solution.py:217
  108.9 0.1 collective-permute-done.8
  109.1 5.7 %collective-permute-start.9 = (f32[1,1,1,1,1,1,2,4,1024]{8,7,6,5,4,3,2,1,0:T(4,128)S(1)}, f32[1,1,1,1,1,1,2,4,1024]{8,7,6,5,4,3,2,1,0:T(4,128)S(1)}, u32[]{:S(2)}, u32[]{:S(2)}) collective-permute-start(f32[1,1,1,1,1,1,2,4,1024]{8,7,6,5,4,3,2,1,0:T(4,128)S(1)} %slice_select_fusion.4), channel_id=1, source_target_pairs={{0,8},{1,9},{2,10},{3,11},{4,12},{5,13},{6,14},{7,15},{8,0},{9,1},... | collective-permute-start | bytes 98312 | tf_op jit(solution)/shard_map/ppermute | solution.py:44
  114.7 0.2 slice_add_fusion.1
  115.0 2.0 %collective-permute-done.9 = f32[1,1,1,1,1,1,2,4,1024]{8,7,6,5,4,3,2,1,0:T(4,128)S(1)} collective-permute-done((f32[1,1,1,1,1,1,2,4,1024]{8,7,6,5,4,3,2,1,0:T(4,128)S(1)}, f32[1,1,1,1,1,1,2,4,1024]{8,7,6,5,4,3,2,1,0:T(4,128)S(1)}, u32[]{:S(2)}, u32[]{:S(2)}) %collective-permute-start.9) | collective-permute-done | bytes 32800 | tf_op jit(solution)/shard_map/ppermute | solution.py:44
  117.0 0.7 collective-permute-start.10
  117.7 0.1 fusion.28
  117.8 1.0 copy.56
  118.7 3.5 %all-to-all-start.2 = ((bf16[32,24,256]{2,1,0:T(8,128)(2,1)}), bf16[32,24,256]{2,1,0:T(8,128)(2,1)S(1)}, u32[]{:S(2)}, u32[]{:S(2)}) async-start(bf16[32,24,256]{2,1,0:T(8,128)(2,1)} %copy.56), calls=%async_computation.2 | async-start | bytes 786432 | tf_op jit(solution)/shard_map/all_to_all | solution.py:223
  122.2 3.6 %collective-permute-start.11 = (f32[2,4,1024]{2,1,0:T(4,128)S(1)}, f32[2,4,1024]{2,1,0:T(4,128)S(1)}, u32[]{:S(2)}, u32[]{:S(2)}) collective-permute-start(f32[2,4,1024]{2,1,0:T(4,128)S(1)} %add.123), channel_id=1, source_target_pairs={{0,128},{64,192},{128,0},{192,64},{1,129},{65,193},{129,1},{193,65... | collective-permute-start | bytes 98312 | tf_op jit(solution)/shard_map/ppermute | solution.py:51
  125.8 4.1 %collective-permute-done.11 = f32[2,4,1024]{2,1,0:T(4,128)S(1)} collective-permute-done((f32[2,4,1024]{2,1,0:T(4,128)S(1)}, f32[2,4,1024]{2,1,0:T(4,128)S(1)}, u32[]{:S(2)}, u32[]{:S(2)}) %collective-permute-start.11) | collective-permute-done | bytes 32800 | tf_op jit(solution)/shard_map/ppermute | solution.py:51
  129.9 0.6 multiply_reduce_fusion
  130.5 0.6 broadcast_in_dim.68
  131.4 1.1 collective-permute-done.12
  132.4 0.6 broadcast_add_fusion
  133.2 6.2 %collective-permute-start.3 = (bf16[8,2,24,256]{3,0,2,1:T(8,128)(2,1)S(1)}, bf16[8,2,24,256]{3,0,2,1:T(8,128)(2,1)S(1)}, u32[]{:S(2)}, u32[]{:S(2)}) collective-permute-start(bf16[8,2,24,256]{3,0,2,1:T(8,128)(2,1)S(1)} %get-tuple-element.24), channel_id=1, source_target_pairs={{1,0},{2,1},{3,2},{4,3},{5,4},{6,5},{7,6},{8,7},{9,8},{10,9},{11,1... | collective-permute-start | bytes 589832 | tf_op jit(solution)/shard_map/ppermute | solution.py:65
  139.4 1.9 %collective-permute-start.2 = (bf16[8,2,24,256]{3,0,2,1:T(8,128)(2,1)S(1)}, bf16[8,2,24,256]{3,0,2,1:T(8,128)(2,1)S(1)}, u32[]{:S(2)}, u32[]{:S(2)}) collective-permute-start(bf16[8,2,24,256]{3,0,2,1:T(8,128)(2,1)S(1)} %get-tuple-element.23), channel_id=1, source_target_pairs={{0,1},{1,2},{2,3},{3,4},{4,5},{5,6},{6,7},{7,8},{8,9},{9,10},{10,1... | collective-permute-start | bytes 589832 | tf_op jit(solution)/shard_map/ppermute | solution.py:63
  141.3 0.7 fusion.52
  142.1 4.5 %collective-permute-done.14 = f32[8,128]{1,0:T(8,128)S(1)} collective-permute-done((f32[8,128]{1,0:T(8,128)S(1)}, f32[8,128]{1,0:T(8,128)S(1)}, u32[]{:S(2)}, u32[]{:S(2)}) %collective-permute-start.14) | collective-permute-done | bytes 4128 | tf_op jit(solution)/shard_map/ppermute | solution.py:51
  146.6 1.8 %collective-permute-start.15 = (f32[8,128]{1,0:T(8,128)S(1)}, f32[8,128]{1,0:T(8,128)S(1)}, u32[]{:S(2)}, u32[]{:S(2)}) collective-permute-start(f32[8,128]{1,0:T(8,128)S(1)} %add.127), channel_id=1, source_target_pairs={{0,8},{1,9},{2,10},{3,11},{4,12},{5,13},{6,14},{7,15},{8,0},{9,1},... | collective-permute-start | bytes 12296 | tf_op jit(solution)/shard_map/ppermute | solution.py:51
  148.4 5.7 %collective-permute-done.15 = f32[8,128]{1,0:T(8,128)S(1)} collective-permute-done((f32[8,128]{1,0:T(8,128)S(1)}, f32[8,128]{1,0:T(8,128)S(1)}, u32[]{:S(2)}, u32[]{:S(2)}) %collective-permute-start.15) | collective-permute-done | bytes 4128 | tf_op jit(solution)/shard_map/ppermute | solution.py:51
  154.1 3.6 %collective-permute-done.16 = f32[8,128]{1,0:T(8,128)S(1)} collective-permute-done((f32[8,128]{1,0:T(8,128)S(1)}, f32[8,128]{1,0:T(8,128)S(1)}, u32[]{:S(2)}, u32[]{:S(2)}) %collective-permute-start.16) | collective-permute-done | bytes 4128 | tf_op jit(solution)/shard_map/ppermute | solution.py:51
  157.7 2.1 %collective-permute-start.17 = (f32[8,128]{1,0:T(8,128)S(1)}, f32[8,128]{1,0:T(8,128)S(1)}, u32[]{:S(2)}, u32[]{:S(2)}) collective-permute-start(f32[8,128]{1,0:T(8,128)S(1)} %add.129), channel_id=1, source_target_pairs={{0,32},{1,33},{2,34},{3,35},{4,36},{5,37},{6,38},{7,39},{8,40},{9,... | collective-permute-start | bytes 12296 | tf_op jit(solution)/shard_map/ppermute | solution.py:51
  159.9 1.7 %gather_fusion.1 = bf16[8,4,24,256]{3,0,2,1:T(8,128)(2,1)S(1)} fusion(bf16[8,8,28,256]{3,0,2,1:T(8,128)(2,1)S(1)} %select_maximum_fusion, s32[8]{0:T(128)S(1)} %get-tuple-element.27), kind=kCustom, calls=%fused_computation.1 | custom fusion | bytes 786560 | tf_op jit(solution)/shard_map/vmap()/gather | solution.py:80
  161.6 0.8 copy.61
  162.4 0.4 collective-permute-done.17
  162.8 0.5 slice.125
  164.1 0.6 slice.162
  164.7 0.6 slice.163
  (48 shorter events, 1.2 us)
Async XLA Ops:
  0.6 34.2 %copy-start = (bf16[2,256,768]{2,1,0:T(8,128)(2,1)S(1)}, bf16[2,256,768]{2,1,0:T(8,128)(2,1)}, u32[]{:S(2)}) copy-start(bf16[2,256,768]{2,1,0:T(8,128)(2,1)} %param.11) | copy-start | bytes 2359300
  0.6 10.5 %copy-start.2 = (bf16[8,4,24,256]{3,2,1,0:T(8,128)(2,1)S(1)}, bf16[8,4,24,256]{3,2,1,0:T(8,128)(2,1)}, u32[]{:S(2)}) copy-start(bf16[8,4,24,256]{3,2,1,0:T(8,128)(2,1)} %param.13) | copy-start | bytes 1179652
  0.7 15.9 %copy-start.4 = (s32[32,2]{0,1:T(2,128)S(1)}, s32[32,2]{0,1:T(2,128)}, u32[]{:S(2)}) copy-start(s32[32,2]{0,1:T(2,128)} %param.10) | copy-start | bytes 772
  0.7 16.0 %copy-start.5 = (s32[32]{0:T(128)S(1)}, s32[32]{0:T(128)}, u32[]{:S(2)}) copy-start(s32[32]{0:T(128)} %param.8) | copy-start | bytes 388
  0.7 16.0 %copy-start.6 = (s32[32]{0:T(128)S(1)}, s32[32]{0:T(128)}, u32[]{:S(2)}) copy-start(s32[32]{0:T(128)} %param.9) | copy-start | bytes 388
  2.0 15.2 %collective-permute-start.1 = (bf16[8,2,24,256]{3,0,2,1:T(8,128)(2,1)S(1)}, bf16[8,2,24,256]{3,0,2,1:T(8,128)(2,1)S(1)}, u32[]{:S(2)}, u32[]{:S(2)}) collective-permute-start(bf16[8,2,24,256]{3,0,2,1:T(8,128)(2,1)S(1)} %get-tuple-element.26), channel_id=1, source_target_pairs={{1,0},{2,1},{3,2},{4,3},{5,4},{6,5},{7,6},{8,7},{9,8},{10,9},{11,1... | collective-permute-start | bytes 589832 | tf_op jit(solution)/shard_map/ppermute | solution.py:65
  9.2 9.1 %collective-permute-start = (bf16[8,2,24,256]{3,0,2,1:T(8,128)(2,1)S(1)}, bf16[8,2,24,256]{3,0,2,1:T(8,128)(2,1)S(1)}, u32[]{:S(2)}, u32[]{:S(2)}) collective-permute-start(bf16[8,2,24,256]{3,0,2,1:T(8,128)(2,1)S(1)} %get-tuple-element.25), channel_id=1, source_target_pairs={{0,1},{1,2},{2,3},{3,4},{4,5},{5,6},{6,7},{7,8},{8,9},{9,10},{10,1... | collective-permute-start | bytes 589832 | tf_op jit(solution)/shard_map/ppermute | solution.py:63
  12.1 11.8 %all-to-all-start.1 = ((bf16[8,96,256]{2,0,1:T(8,128)(2,1)}), bf16[8,96,256]{2,0,1:T(8,128)(2,1)S(1)}, u32[]{:S(2)}, u32[]{:S(2)}) async-start(bf16[8,96,256]{2,0,1:T(8,128)(2,1)} %bitcast.16), calls=%async_computation.1 | async-start | bytes 786432 | tf_op jit(solution)/shard_map/all_to_all | solution.py:195
  18.4 9.1 %copy-start.3 = (bf16[2,256,256]{2,1,0:T(8,128)(2,1)S(1)}, bf16[2,256,256]{2,1,0:T(8,128)(2,1)}, u32[]{:S(2)}) copy-start(bf16[2,256,256]{2,1,0:T(8,128)(2,1)} %param.12) | copy-start | bytes 786436
  24.0 10.8 %all-to-all-start = ((bf16[8,96,256]{2,0,1:T(8,128)(2,1)}), bf16[8,96,256]{2,0,1:T(8,128)(2,1)S(1)}, u32[]{:S(2)}, u32[]{:S(2)}) async-start(bf16[8,96,256]{2,0,1:T(8,128)(2,1)} %bitcast.2), calls=%async_computation | async-start | bytes 786432 | tf_op jit(solution)/shard_map/all_to_all | solution.py:194
  66.0 1.0 copy-start.1
  67.9 2.9 %collective-permute-start.4 = (f32[2,2,2,2,2,1,2,4,1024]{8,7,6,5,4,3,2,1,0:T(4,128)S(1)}, f32[2,2,2,2,2,1,2,4,1024]{8,7,6,5,4,3,2,1,0:T(4,128)}, u32[]{:S(2)}, u32[]{:S(2)}) collective-permute-start(f32[2,2,2,2,2,1,2,4,1024]{8,7,6,5,4,3,2,1,0:T(4,128)S(1)} %copy_select_fusion), channel_id=1, source_target_pairs={{0,1},{1,0},{2,3},{3,2},{4,5},{5,4},{6,7},{7,6},{8,9},{9,8},{10,11... | collective-permute-start | bytes 3145736 | tf_op jit(solution)/shard_map/ppermute | solution.py:44
  73.3 14.1 %collective-permute-start.5 = (f32[2,2,2,2,1,1,2,4,1024]{8,7,6,5,4,3,2,1,0:T(4,128)S(1)}, f32[2,2,2,2,1,1,2,4,1024]{8,7,6,5,4,3,2,1,0:T(4,128)S(1)}, u32[]{:S(2)}, u32[]{:S(2)}) collective-permute-start(f32[2,2,2,2,1,1,2,4,1024]{8,7,6,5,4,3,2,1,0:T(4,128)S(1)} %slice_select_fusion), channel_id=1, source_target_pairs={{0,2},{1,3},{2,0},{3,1},{4,6},{5,7},{6,4},{7,5},{8,10},{9,11},{10,... | collective-permute-start | bytes 1572872 | tf_op jit(solution)/shard_map/ppermute | solution.py:44
  87.7 7.6 %collective-permute-start.6 = (f32[2,1,2,2,1,1,2,4,1024]{8,7,6,5,4,3,2,1,0:T(4,128)S(1)}, f32[2,1,2,2,1,1,2,4,1024]{8,7,6,5,4,3,2,1,0:T(4,128)S(1)}, u32[]{:S(2)}, u32[]{:S(2)}) collective-permute-start(f32[2,1,2,2,1,1,2,4,1024]{8,7,6,5,4,3,2,1,0:T(4,128)S(1)} %slice_select_fusion.1), channel_id=1, source_target_pairs={{0,16},{1,17},{2,18},{3,19},{4,20},{5,21},{6,22},{7,23},{8,24},{9,... | collective-permute-start | bytes 786440 | tf_op jit(solution)/shard_map/ppermute | solution.py:44
  95.5 7.6 %collective-permute-start.7 = (f32[2,1,2,1,1,1,2,4,1024]{8,7,6,5,4,3,2,1,0:T(4,128)S(1)}, f32[2,1,2,1,1,1,2,4,1024]{8,7,6,5,4,3,2,1,0:T(4,128)S(1)}, u32[]{:S(2)}, u32[]{:S(2)}) collective-permute-start(f32[2,1,2,1,1,1,2,4,1024]{8,7,6,5,4,3,2,1,0:T(4,128)S(1)} %slice_select_fusion.2), channel_id=1, source_target_pairs={{0,4},{1,5},{2,6},{3,7},{4,0},{5,1},{6,2},{7,3},{8,12},{9,13},{10,... | collective-permute-start | bytes 393224 | tf_op jit(solution)/shard_map/ppermute | solution.py:44
  103.2 5.9 %collective-permute-start.8 = (f32[1,1,2,1,1,1,2,4,1024]{8,7,6,5,4,3,2,1,0:T(4,128)S(1)}, f32[1,1,2,1,1,1,2,4,1024]{8,7,6,5,4,3,2,1,0:T(4,128)S(1)}, u32[]{:S(2)}, u32[]{:S(2)}) collective-permute-start(f32[1,1,2,1,1,1,2,4,1024]{8,7,6,5,4,3,2,1,0:T(4,128)S(1)} %slice_select_fusion.3), channel_id=1, source_target_pairs={{0,32},{1,33},{2,34},{3,35},{4,36},{5,37},{6,38},{7,39},{8,40},{9,... | collective-permute-start | bytes 196616 | tf_op jit(solution)/shard_map/ppermute | solution.py:44
  109.1 7.9 %collective-permute-start.9 = (f32[1,1,1,1,1,1,2,4,1024]{8,7,6,5,4,3,2,1,0:T(4,128)S(1)}, f32[1,1,1,1,1,1,2,4,1024]{8,7,6,5,4,3,2,1,0:T(4,128)S(1)}, u32[]{:S(2)}, u32[]{:S(2)}) collective-permute-start(f32[1,1,1,1,1,1,2,4,1024]{8,7,6,5,4,3,2,1,0:T(4,128)S(1)} %slice_select_fusion.4), channel_id=1, source_target_pairs={{0,8},{1,9},{2,10},{3,11},{4,12},{5,13},{6,14},{7,15},{8,0},{9,1},... | collective-permute-start | bytes 98312 | tf_op jit(solution)/shard_map/ppermute | solution.py:44
  117.0 5.2 %collective-permute-start.10 = (f32[2,4,1024]{2,1,0:T(4,128)S(1)}, f32[2,4,1024]{2,1,0:T(4,128)S(1)}, u32[]{:S(2)}, u32[]{:S(2)}) collective-permute-start(f32[2,4,1024]{2,1,0:T(4,128)S(1)} %add_bitcast_fusion), channel_id=1, source_target_pairs={{0,64},{64,0},{128,192},{192,128},{1,65},{65,1},{129,193},{193,129... | collective-permute-start | bytes 98312 | tf_op jit(solution)/shard_map/ppermute | solution.py:51
  118.7 12.5 %all-to-all-start.2 = ((bf16[32,24,256]{2,1,0:T(8,128)(2,1)}), bf16[32,24,256]{2,1,0:T(8,128)(2,1)S(1)}, u32[]{:S(2)}, u32[]{:S(2)}) async-start(bf16[32,24,256]{2,1,0:T(8,128)(2,1)} %copy.56), calls=%async_computation.2 | async-start | bytes 786432 | tf_op jit(solution)/shard_map/all_to_all | solution.py:223
  122.2 7.7 %collective-permute-start.11 = (f32[2,4,1024]{2,1,0:T(4,128)S(1)}, f32[2,4,1024]{2,1,0:T(4,128)S(1)}, u32[]{:S(2)}, u32[]{:S(2)}) collective-permute-start(f32[2,4,1024]{2,1,0:T(4,128)S(1)} %add.123), channel_id=1, source_target_pairs={{0,128},{64,192},{128,0},{192,64},{1,129},{65,193},{129,1},{193,65... | collective-permute-start | bytes 98312 | tf_op jit(solution)/shard_map/ppermute | solution.py:51
  131.2 1.3 collective-permute-start.12
  133.1 8.2 %collective-permute-start.13 = (f32[8,128]{1,0:T(8,128)S(1)}, f32[8,128]{1,0:T(8,128)S(1)}, u32[]{:S(2)}, u32[]{:S(2)}) collective-permute-start(f32[8,128]{1,0:T(8,128)S(1)} %broadcast_add_fusion), channel_id=1, source_target_pairs={{0,2},{1,3},{2,0},{3,1},{4,6},{5,7},{6,4},{7,5},{8,10},{9,11},{10,... | collective-permute-start | bytes 12296 | tf_op jit(solution)/shard_map/ppermute | solution.py:51
  133.2 26.6 %collective-permute-start.3 = (bf16[8,2,24,256]{3,0,2,1:T(8,128)(2,1)S(1)}, bf16[8,2,24,256]{3,0,2,1:T(8,128)(2,1)S(1)}, u32[]{:S(2)}, u32[]{:S(2)}) collective-permute-start(bf16[8,2,24,256]{3,0,2,1:T(8,128)(2,1)S(1)} %get-tuple-element.24), channel_id=1, source_target_pairs={{1,0},{2,1},{3,2},{4,3},{5,4},{6,5},{7,6},{8,7},{9,8},{10,9},{11,1... | collective-permute-start | bytes 589832 | tf_op jit(solution)/shard_map/ppermute | solution.py:65
  139.4 20.4 %collective-permute-start.2 = (bf16[8,2,24,256]{3,0,2,1:T(8,128)(2,1)S(1)}, bf16[8,2,24,256]{3,0,2,1:T(8,128)(2,1)S(1)}, u32[]{:S(2)}, u32[]{:S(2)}) collective-permute-start(bf16[8,2,24,256]{3,0,2,1:T(8,128)(2,1)S(1)} %get-tuple-element.23), channel_id=1, source_target_pairs={{0,1},{1,2},{2,3},{3,4},{4,5},{5,6},{6,7},{7,8},{8,9},{9,10},{10,1... | collective-permute-start | bytes 589832 | tf_op jit(solution)/shard_map/ppermute | solution.py:63
  142.0 4.6 %collective-permute-start.14 = (f32[8,128]{1,0:T(8,128)S(1)}, f32[8,128]{1,0:T(8,128)S(1)}, u32[]{:S(2)}, u32[]{:S(2)}) collective-permute-start(f32[8,128]{1,0:T(8,128)S(1)} %fusion.52), channel_id=1, source_target_pairs={{0,4},{1,5},{2,6},{3,7},{4,0},{5,1},{6,2},{7,3},{8,12},{9,13},{10,... | collective-permute-start | bytes 12296 | tf_op jit(solution)/shard_map/ppermute | solution.py:51
  146.6 7.5 %collective-permute-start.15 = (f32[8,128]{1,0:T(8,128)S(1)}, f32[8,128]{1,0:T(8,128)S(1)}, u32[]{:S(2)}, u32[]{:S(2)}) collective-permute-start(f32[8,128]{1,0:T(8,128)S(1)} %add.127), channel_id=1, source_target_pairs={{0,8},{1,9},{2,10},{3,11},{4,12},{5,13},{6,14},{7,15},{8,0},{9,1},... | collective-permute-start | bytes 12296 | tf_op jit(solution)/shard_map/ppermute | solution.py:51
  154.1 3.6 %collective-permute-start.16 = (f32[8,128]{1,0:T(8,128)S(1)}, f32[8,128]{1,0:T(8,128)S(1)}, u32[]{:S(2)}, u32[]{:S(2)}) collective-permute-start(f32[8,128]{1,0:T(8,128)S(1)} %add.128), channel_id=1, source_target_pairs={{0,16},{1,17},{2,18},{3,19},{4,20},{5,21},{6,22},{7,23},{8,24},{9,... | collective-permute-start | bytes 12296 | tf_op jit(solution)/shard_map/ppermute | solution.py:51
  157.7 5.1 %collective-permute-start.17 = (f32[8,128]{1,0:T(8,128)S(1)}, f32[8,128]{1,0:T(8,128)S(1)}, u32[]{:S(2)}, u32[]{:S(2)}) collective-permute-start(f32[8,128]{1,0:T(8,128)S(1)} %add.129), channel_id=1, source_target_pairs={{0,32},{1,33},{2,34},{3,35},{4,36},{5,37},{6,38},{7,39},{8,40},{9,... | collective-permute-start | bytes 12296 | tf_op jit(solution)/shard_map/ppermute | solution.py:51

commit v4 on v3

--- a/solution.py
+++ b/solution.py
@@ -97,10 +97,11 @@
     lane = lax.broadcasted_iota(jnp.int32, (HEADS, channels), 1)
     head = lax.broadcasted_iota(jnp.int32, (HEADS, channels), 0)
     head_mask = (lane // head_size == head).astype(f32).reshape(1, HEADS, 1, channels)
-    row_id = lax.broadcasted_iota(jnp.int32, (rows, agents), 0)
-    col_id = lax.broadcasted_iota(jnp.int32, (rows, agents), 1)
+    key_id = lax.broadcasted_iota(jnp.int32, (agents, rows), 0)
+    row_id = lax.broadcasted_iota(jnp.int32, (agents, rows), 1)
     row_agent = (row_id // (HEADS * block_size)) * block_size + row_id % block_size
-    allowed = (valid_ref[...] > 0.5) | (row_agent == col_id)
+    allowed = (valid_ref[...] > 0.5) | (row_agent == key_id)
+    row_block = row_id // (HEADS * block_size)
 
     def stack(x):
         spread = x.astype(f32).reshape(blocks, 1, block_size, channels) * head_mask
@@ -117,26 +118,28 @@
         v = qkv_ref[c, :, 2 * channels : 3 * channels]
         q_rows = stack(q)
         da_rows = stack(da_ref[c])
-        scores = lax.dot_general(q_rows, k, dims_nt, preferred_element_type=f32) * scale
+        scores = lax.dot_general(k, q_rows, dims_nt, preferred_element_type=f32) * scale
         raised = jnp.where(allowed, jnp.exp(scores), f32(0.0))
-        prob = raised / jnp.sum(raised, axis=1, keepdims=True)
+        prob = raised / jnp.sum(raised, axis=0, keepdims=True)
         prob_low = prob.astype(bf16)
-        att = unstack(jnp.dot(prob_low, v, preferred_element_type=f32))
+        att = unstack(lax.dot_general(prob_low, v, dims_tn, preferred_element_type=f32))
         att_ref[c] = att.astype(bf16)
-        prob_grad = lax.dot_general(da_rows, v, dims_nt, preferred_element_type=f32)
+        prob_grad = lax.dot_general(v, da_rows, dims_nt, preferred_element_type=f32)
         score_grad = (
-            prob * (prob_grad - jnp.sum(prob * prob_grad, axis=1, keepdims=True)) * scale
+            prob * (prob_grad - jnp.sum(prob * prob_grad, axis=0, keepdims=True)) * scale
         ).astype(bf16)
-        d_q = unstack(jnp.dot(score_grad, k, preferred_element_type=f32)).astype(bf16).astype(f32)
+        d_q = unstack(lax.dot_general(score_grad, k, dims_tn, preferred_element_type=f32))
+        d_q = d_q.astype(bf16).astype(f32)
         d_k = jnp.zeros((agents, channels), f32)
         d_v = jnp.zeros((agents, channels), f32)
+        zero = jnp.zeros((), bf16)
         for n in range(blocks):
-            part = slice(n * HEADS * block_size, (n + 1) * HEADS * block_size)
-            d_k = d_k + lax.dot_general(
-                score_grad[part], q_rows[part], dims_tn, preferred_element_type=f32
+            in_block = row_block == n
+            d_k = d_k + jnp.dot(
+                jnp.where(in_block, score_grad, zero), q_rows, preferred_element_type=f32
             ).astype(bf16).astype(f32)
-            d_v = d_v + lax.dot_general(
-                prob_low[part], da_rows[part], dims_tn, preferred_element_type=f32
+            d_v = d_v + jnp.dot(
+                jnp.where(in_block, prob_low, zero), da_rows, preferred_element_type=f32
             ).astype(bf16).astype(f32)
         for i, d in enumerate((d_q, d_k, d_v)):
             hi = d.astype(bf16)
@@ -154,7 +157,7 @@
         functools.partial(attention_kernel, block_size),
         grid=(cells // step,),
         in_specs=[
-            pl.BlockSpec((1, agents), lambda i: (0, 0)),
+            pl.BlockSpec((agents, 1), lambda i: (0, 0)),
             pl.BlockSpec((step, agents, 3 * channels), lambda i: (i, 0, 0)),
             pl.BlockSpec((step, agents, channels), lambda i: (i, 0, 0)),
         ],
@@ -190,10 +193,14 @@
     all_hot = (types[:, None] == jnp.arange(2)[None, :]).astype(bf16)
     flat_feats = warped.reshape(own_count, cell_count, channels)
     flat_grads = d_out.reshape(own_count, cell_count, channels)
-    all_feats, all_grads = (
-        lax.all_to_all(flat_feats, "agent", split_axis=1, concat_axis=0, tiled=True),
-        lax.all_to_all(flat_grads, "agent", split_axis=1, concat_axis=0, tiled=True),
-    )
+    both = lax.all_to_all(
+        jnp.concatenate([flat_feats, flat_grads], axis=-1),
+        "agent",
+        split_axis=1,
+        concat_axis=0,
+        tiled=True,
+    )
+    all_feats, all_grads = both[..., :channels], both[..., channels:]
     part_cells = all_feats.shape[1]
     pairs = agents * part_cells
     is_type1 = (types == 1)[None, :, None]
@@ -208,7 +215,7 @@
         "gae,tce->tgac", grads_cm, w_out, preferred_element_type=f32
     ).astype(bf16)
     d_attended = jnp.where(is_type1, d_att_both[1], d_att_both[0])
-    valid_row = (valid == 1).astype(f32).reshape(1, agents)
+    valid_row = (valid == 1).astype(f32).reshape(agents, 1)
     attended, d_split = cell_attention(valid_row, qkv, d_attended, own_count)
     attended_typed = jnp.where(type_mask, attended[None], jnp.zeros((), bf16))
     raw_out = jnp.einsum(

time: 166 us -> 168 us (1.012)
  waiting for transfers between devices: 61.6 us -> 72 us
  starting transfers between devices: 47.6 us -> 37.7 us
  Pallas kernels: 19.5 us -> 21.4 us
    ppermute x2, waiting for transfers between devices: 1.07 us -> 5.93 us  [with_halo(): lax.ppermute(tail, axis, [(i, (i + 1) % count) for i in range(ends)])]
    ppermute x6, waiting for transfers between devices: 31.9 us -> 36.6 us  [halving_sum(): x = keep + lax.ppermute(send, axis, xor_pairs(count, bit))]
    ppermute x6, starting transfers between devices: 10.7 us -> 6.04 us  [halving_sum(): x = keep + lax.ppermute(send, axis, xor_pairs(count, bit))]
    all_to_all x2 -> x1, starting transfers between devices: 7.92 us -> 4.46 us  [body(): lax.all_to_all(jnp.concatenate([flat_feats, flat_grads], axis=-1), 'agent...]
    pallas_call x1, Pallas kernels: 19.5 us -> 21.4 us  [cell_attention(): pl.pallas_call(functools.partial(attention_kernel, block_size), grid=(cel...]
    all_to_all x2 -> x1, waiting for transfers between devices: 9.2 us -> 8.76 us  [body(): lax.all_to_all(jnp.concatenate([flat_feats, flat_grads], axis=-1), 'agent...]
  transfers between devices with their start and end apart: 21 -> 20, of which waited for: 15 -> 15; matrix products, arithmetic and copies ran while one was open for 9% -> 6% of each run, Pallas kernels for 0% -> 0%
where the time goes in v4:
time: 168 us
  waiting for transfers between devices  72 us (43%)
  starting transfers between devices  37.7 us (22%)
  Pallas kernels  21.4 us (13%)
  local copies, waits for them, and re-layouts  16 us (10%)
  other arithmetic  9.88 us (6%)
  matrix products  8.83 us (5%)
  between operations  1.86 us (1%)
    ppermute x6, waiting for transfers between devices, halving_sum(): x = keep + lax.ppermute(send, axis, xor_pairs(count, bit))  36.6 us
    pallas_call x1, Pallas kernels, cell_attention(): pl.pallas_call(functools.partial(attention_kernel, block_size), grid=(cel...  21.4 us
    ppermute x8, waiting for transfers between devices, doubling_sum(): x = x + lax.ppermute(x, axis, xor_pairs(count, bit))  19.8 us
    ppermute x2, starting transfers between devices, with_halo(): lax.ppermute(head, axis, [((i + 1) % count, i) for i in range(ends)])  11.8 us
    all_to_all x1, waiting for transfers between devices, body(): lax.all_to_all(jnp.concatenate([flat_feats, flat_grads], axis=-1), 'agent...  8.76 us
    ppermute x8, starting transfers between devices, doubling_sum(): x = x + lax.ppermute(x, axis, xor_pairs(count, bit))  8.04 us
    ppermute x6, starting transfers between devices, halving_sum(): x = keep + lax.ppermute(send, axis, xor_pairs(count, bit))  6.04 us
    ppermute x2, waiting for transfers between devices, with_halo(): lax.ppermute(tail, axis, [(i, (i + 1) % count) for i in range(ends)])  5.93 us
  transfers between devices with their start and end apart: 20, of which 15 were waited for; matrix products, arithmetic and copies ran while one was open for 6% of the time, Pallas kernels for 0%

profile of v4, /device:TPU:2, one launch (start us, length us, event | category | flops | bytes accessed | tf_op | source)
XLA Modules:
  0.0 167.6 jit_solution(16406469004267765216)
XLA Ops:
  0.7 1.3 copy.50
  2.0 7.2 %collective-permute-start.1 = (bf16[8,2,24,256]{3,0,2,1:T(8,128)(2,1)S(1)}, bf16[8,2,24,256]{3,0,2,1:T(8,128)(2,1)S(1)}, u32[]{:S(2)}, u32[]{:S(2)}) collective-permute-start(bf16[8,2,24,256]{3,0,2,1:T(8,128)(2,1)S(1)} %get-tuple-element.26), channel_id=1, source_target_pairs={{1,0},{2,1},{3,2},{4,3},{5,4},{6,5},{7,6},{8,7},{9,8},{10,9},{11,1... | collective-permute-start | bytes 589832 | tf_op jit(solution)/shard_map/ppermute | solution.py:65
  9.2 1.9 %collective-permute-start = (bf16[8,2,24,256]{3,0,2,1:T(8,128)(2,1)S(1)}, bf16[8,2,24,256]{3,0,2,1:T(8,128)(2,1)S(1)}, u32[]{:S(2)}, u32[]{:S(2)}) collective-permute-start(bf16[8,2,24,256]{3,0,2,1:T(8,128)(2,1)S(1)} %get-tuple-element.25), channel_id=1, source_target_pairs={{0,1},{1,2},{2,3},{3,4},{4,5},{5,6},{6,7},{7,8},{8,9},{9,10},{10,1... | collective-permute-start | bytes 589832 | tf_op jit(solution)/shard_map/ppermute | solution.py:63
  11.1 0.2 copy.53
  11.5 0.9 collective-permute-done.1
  12.4 5.9 %collective-permute-done = bf16[8,2,24,256]{3,0,2,1:T(8,128)(2,1)S(1)} collective-permute-done((bf16[8,2,24,256]{3,0,2,1:T(8,128)(2,1)S(1)}, bf16[8,2,24,256]{3,0,2,1:T(8,128)(2,1)S(1)}, u32[]{:S(2)}, u32[]{:S(2)}) %collective-permute-start) | collective-permute-done | bytes 196640 | tf_op jit(solution)/shard_map/ppermute | solution.py:63
  18.4 1.7 %gather_fusion = bf16[8,4,24,256]{3,0,2,1:T(8,128)(2,1)S(1)} fusion(bf16[8,8,28,256]{3,0,2,1:T(8,128)(2,1)S(1)} %fusion.18, s32[8]{0:T(128)S(1)} %get-tuple-element.28), kind=kCustom, calls=%fused_computation | custom fusion | bytes 786560 | tf_op jit(solution)/shard_map/vmap()/gather | solution.py:80
  20.1 1.0 pad_maximum_fusion.1
  21.1 4.5 %all-to-all-start = ((bf16[8,96,512]{2,0,1:T(8,128)(2,1)}), bf16[8,96,512]{2,0,1:T(8,128)(2,1)S(1)}, u32[]{:S(2)}, u32[]{:S(2)}) async-start(bf16[8,96,512]{2,0,1:T(8,128)(2,1)} %pad_maximum_fusion.1), calls=%async_computation | async-start | bytes 1572864 | tf_op jit(solution)/shard_map/all_to_all | solution.py:196
  25.5 0.7 copy.58.valid_ref
  26.3 8.8 %all-to-all-done = bf16[8,96,512]{2,0,1:T(8,128)(2,1)S(1)} async-done(((bf16[8,96,512]{2,0,1:T(8,128)(2,1)}), bf16[8,96,512]{2,0,1:T(8,128)(2,1)S(1)}, u32[]{:S(2)}, u32[]{:S(2)}) %all-to-all-start) | async-done | bytes 786464 | tf_op jit(solution)/shard_map/all_to_all | solution.py:196
  35.2 0.8 convert_bitcast_fusion
  36.0 0.2 copy-done.3
  36.1 0.4 fusion.12
  36.5 1.2 fusion.13.qkv_ref
  37.7 0.8 fusion.29.da_ref
  38.6 21.4 %shard_map.94 = (bf16[24,32,256]{2,1,0:T(8,128)(2,1)}, bf16[2,24,32,768]{3,2,1,0:T(8,128)(2,1)}) custom-call(f32[32,1]{1,0:T(8,128)} %copy.58.valid_ref, bf16[24,32,768]{2,1,0:T(8,128)(2,1)} %fusion.13.qkv_ref, bf16[24,32,256]{2,1,0:T(8,128)(2,1)} %fusion.29.da_ref), custom_call_target="tpu_custom_call" | custom-call | flops 2415919104 | bytes 4325376 | tf_op jit(solution)/shard_map/pallas_call | solution.py:156
  60.0 1.4 convolution_bitcast_fusion
  61.4 3.1 %fusion.7 = f32[2,2,256,768]{2,3,1,0:T(8,128)S(1)} fusion(bf16[2,24,32,768]{3,2,1,0:T(8,128)(2,1)} %get-tuple-element.5, pred[2,32]{1,0:T(4,128)(4,1)S(1)} %pad_add_fusion, bf16[24,32,256]{2,1,0:T(8,128)(2,1)S(1)} %slice_bitcast_fusion.7), kind=kOutput, calls=%fused_computation.11 | convolution fusion | flops 1208352768 | bytes 5898304 | tf_op jit(solution)/shard_map/tgac,sgae->stce/dot_general | solution.py:233
  64.6 0.2 fusion.11
  64.8 0.1 pad_maximum_fusion
  64.9 2.4 %copy.62 = f32[2,256,1024]{2,0,1:T(2,128)} copy(f32[2,256,1024]{1,2,0:T(8,128)S(1)} %pad_maximum_fusion) | data formatting | bytes 4194304 | tf_op jit(solution)/shard_map/concatenate | solution.py:240
  67.3 2.3 %fusion.45 = (f32[2,2,2,2,2,1,2,4,1024]{8,6,7,5,4,3,2,1,0:T(2,128)S(1)}, f32[2,2,2,2,2,1,2,4,1024]{8,6,7,5,4,3,2,1,0:T(2,128)S(1)}) fusion(f32[2,2,2,2,2,2,2,4,1024]{8,6,7,5,4,3,2,1,0:T(2,128)} %bitcast.121), kind=kLoop, calls=%fused_computation.91 | loop fusion | bytes 4194304 | tf_op jit(solution)/shard_map/slice | solution.py:41
  69.6 1.0 copy-done.1
  70.6 0.9 copy_select_fusion
  71.6 2.8 %collective-permute-done.4 = f32[2,2,2,2,2,1,2,4,1024]{8,7,6,5,4,3,2,1,0:T(4,128)} collective-permute-done((f32[2,2,2,2,2,1,2,4,1024]{8,7,6,5,4,3,2,1,0:T(4,128)S(1)}, f32[2,2,2,2,2,1,2,4,1024]{8,7,6,5,4,3,2,1,0:T(4,128)}, u32[]{:S(2)}, u32[]{:S(2)}) %collective-permute-start.4) | collective-permute-done | bytes 1048608 | tf_op jit(solution)/shard_map/ppermute | solution.py:44
  74.4 2.4 %select_add_fusion = f32[2,2,2,2,2,1,2,4,1024]{8,7,6,5,4,3,2,1,0:T(4,128)S(1)} fusion(f32[2,2,2,2,2,1,2,4,1024]{8,7,6,5,4,3,2,1,0:T(4,128)} %collective-permute-done.4, f32[2,2,2,2,2,1,2,4,1024]{8,6,7,5,4,3,2,1,0:T(2,128)} %copy-done.1, f32[2,2,2,2,2,1,2,4,1024]{8,6,7,5,4,3,2,1,0:T(2,128)S(1)} %get-tuple-element.21, pred[]{:T(512)S(6)} %eq.44), kind=kLoop, calls=%fused_computation.22 | loop fusion | flops 524288 | bytes 4194305 | tf_op jit(solution)/shard_map/add | solution.py:44
  76.7 0.2 slice_select_fusion
  77.0 13.9 %collective-permute-done.5 = f32[2,2,2,2,1,1,2,4,1024]{8,7,6,5,4,3,2,1,0:T(4,128)S(1)} collective-permute-done((f32[2,2,2,2,1,1,2,4,1024]{8,7,6,5,4,3,2,1,0:T(4,128)S(1)}, f32[2,2,2,2,1,1,2,4,1024]{8,7,6,5,4,3,2,1,0:T(4,128)S(1)}, u32[]{:S(2)}, u32[]{:S(2)}) %collective-permute-start.5) | collective-permute-done | bytes 524320 | tf_op jit(solution)/shard_map/ppermute | solution.py:44
  91.0 0.3 select_add_fusion.1
  91.4 7.5 %collective-permute-done.6 = f32[2,1,2,2,1,1,2,4,1024]{8,7,6,5,4,3,2,1,0:T(4,128)S(1)} collective-permute-done((f32[2,1,2,2,1,1,2,4,1024]{8,7,6,5,4,3,2,1,0:T(4,128)S(1)}, f32[2,1,2,2,1,1,2,4,1024]{8,7,6,5,4,3,2,1,0:T(4,128)S(1)}, u32[]{:S(2)}, u32[]{:S(2)}) %collective-permute-start.6) | collective-permute-done | bytes 262176 | tf_op jit(solution)/shard_map/ppermute | solution.py:44
  99.1 0.4 collective-permute-start.7
  99.5 7.4 %collective-permute-done.7 = f32[2,1,2,1,1,1,2,4,1024]{8,7,6,5,4,3,2,1,0:T(4,128)S(1)} collective-permute-done((f32[2,1,2,1,1,1,2,4,1024]{8,7,6,5,4,3,2,1,0:T(4,128)S(1)}, f32[2,1,2,1,1,1,2,4,1024]{8,7,6,5,4,3,2,1,0:T(4,128)S(1)}, u32[]{:S(2)}, u32[]{:S(2)}) %collective-permute-start.7) | collective-permute-done | bytes 131104 | tf_op jit(solution)/shard_map/ppermute | solution.py:44
  107.0 2.5 %collective-permute-start.8 = (f32[1,1,2,1,1,1,2,4,1024]{8,7,6,5,4,3,2,1,0:T(4,128)S(1)}, f32[1,1,2,1,1,1,2,4,1024]{8,7,6,5,4,3,2,1,0:T(4,128)S(1)}, u32[]{:S(2)}, u32[]{:S(2)}) collective-permute-start(f32[1,1,2,1,1,1,2,4,1024]{8,7,6,5,4,3,2,1,0:T(4,128)S(1)} %slice_select_fusion.3), channel_id=1, source_target_pairs={{0,32},{1,33},{2,34},{3,35},{4,36},{5,37},{6,38},{7,39},{8,40},{9,... | collective-permute-start | bytes 196616 | tf_op jit(solution)/shard_map/ppermute | solution.py:44
  109.5 3.1 %fusion.4 = f32[2,2,24,32,256]{4,3,2,1,0:T(8,128)S(1)} fusion(bf16[2,24,32,768]{3,2,1,0:T(8,128)(2,1)} %get-tuple-element.5, bf16[2,256,768]{2,1,0:T(8,128)(2,1)S(1)} %copy-done), kind=kOutput, calls=%fused_computation.10 | convolution fusion | flops 1207959552 | bytes 6291456 | tf_op jit(solution)/shard_map/sgae,tce->stgac/dot_general | solution.py:224
  112.6 0.2 collective-permute-done.8
  112.9 2.9 %collective-permute-start.9 = (f32[1,1,1,1,1,1,2,4,1024]{8,7,6,5,4,3,2,1,0:T(4,128)S(1)}, f32[1,1,1,1,1,1,2,4,1024]{8,7,6,5,4,3,2,1,0:T(4,128)S(1)}, u32[]{:S(2)}, u32[]{:S(2)}) collective-permute-start(f32[1,1,1,1,1,1,2,4,1024]{8,7,6,5,4,3,2,1,0:T(4,128)S(1)} %slice_select_fusion.4), channel_id=1, source_target_pairs={{0,8},{1,9},{2,10},{3,11},{4,12},{5,13},{6,14},{7,15},{8,0},{9,1},... | collective-permute-start | bytes 98312 | tf_op jit(solution)/shard_map/ppermute | solution.py:44
  115.7 0.2 slice_add_fusion.1
  116.0 4.8 %collective-permute-done.9 = f32[1,1,1,1,1,1,2,4,1024]{8,7,6,5,4,3,2,1,0:T(4,128)S(1)} collective-permute-done((f32[1,1,1,1,1,1,2,4,1024]{8,7,6,5,4,3,2,1,0:T(4,128)S(1)}, f32[1,1,1,1,1,1,2,4,1024]{8,7,6,5,4,3,2,1,0:T(4,128)S(1)}, u32[]{:S(2)}, u32[]{:S(2)}) %collective-permute-start.9) | collective-permute-done | bytes 32800 | tf_op jit(solution)/shard_map/ppermute | solution.py:44
  120.8 0.7 collective-permute-start.10
  121.5 0.1 fusion.28
  121.6 1.0 copy.60
  122.5 3.5 %all-to-all-start.1 = ((bf16[32,24,256]{2,1,0:T(8,128)(2,1)}), bf16[32,24,256]{2,1,0:T(8,128)(2,1)S(1)}, u32[]{:S(2)}, u32[]{:S(2)}) async-start(bf16[32,24,256]{2,1,0:T(8,128)(2,1)} %copy.60), calls=%async_computation.1 | async-start | bytes 786432 | tf_op jit(solution)/shard_map/all_to_all | solution.py:230
  126.0 3.6 %collective-permute-start.11 = (f32[2,4,1024]{2,1,0:T(4,128)S(1)}, f32[2,4,1024]{2,1,0:T(4,128)S(1)}, u32[]{:S(2)}, u32[]{:S(2)}) collective-permute-start(f32[2,4,1024]{2,1,0:T(4,128)S(1)} %add.123), channel_id=1, source_target_pairs={{0,128},{64,192},{128,0},{192,64},{1,129},{65,193},{129,1},{193,65... | collective-permute-start | bytes 98312 | tf_op jit(solution)/shard_map/ppermute | solution.py:51
  129.6 4.1 %collective-permute-done.11 = f32[2,4,1024]{2,1,0:T(4,128)S(1)} collective-permute-done((f32[2,4,1024]{2,1,0:T(4,128)S(1)}, f32[2,4,1024]{2,1,0:T(4,128)S(1)}, u32[]{:S(2)}, u32[]{:S(2)}) %collective-permute-start.11) | collective-permute-done | bytes 32800 | tf_op jit(solution)/shard_map/ppermute | solution.py:51
  133.7 0.6 multiply_reduce_fusion
  134.3 0.6 broadcast_in_dim.68
  135.2 1.1 collective-permute-done.12
  136.2 0.6 broadcast_add_fusion
  137.0 4.7 %collective-permute-start.3 = (bf16[8,2,24,256]{3,0,2,1:T(8,128)(2,1)S(1)}, bf16[8,2,24,256]{3,0,2,1:T(8,128)(2,1)S(1)}, u32[]{:S(2)}, u32[]{:S(2)}) collective-permute-start(bf16[8,2,24,256]{3,0,2,1:T(8,128)(2,1)S(1)} %get-tuple-element.24), channel_id=1, source_target_pairs={{1,0},{2,1},{3,2},{4,3},{5,4},{6,5},{7,6},{8,7},{9,8},{10,9},{11,1... | collective-permute-start | bytes 589832 | tf_op jit(solution)/shard_map/ppermute | solution.py:65
  141.7 1.9 %collective-permute-start.2 = (bf16[8,2,24,256]{3,0,2,1:T(8,128)(2,1)S(1)}, bf16[8,2,24,256]{3,0,2,1:T(8,128)(2,1)S(1)}, u32[]{:S(2)}, u32[]{:S(2)}) collective-permute-start(bf16[8,2,24,256]{3,0,2,1:T(8,128)(2,1)S(1)} %get-tuple-element.23), channel_id=1, source_target_pairs={{0,1},{1,2},{2,3},{3,4},{4,5},{5,6},{6,7},{7,8},{8,9},{9,10},{10,1... | collective-permute-start | bytes 589832 | tf_op jit(solution)/shard_map/ppermute | solution.py:63
  143.6 0.7 fusion.48
  144.3 0.3 collective-permute-start.14
  144.6 4.3 %collective-permute-done.14 = f32[8,128]{1,0:T(8,128)S(1)} collective-permute-done((f32[8,128]{1,0:T(8,128)S(1)}, f32[8,128]{1,0:T(8,128)S(1)}, u32[]{:S(2)}, u32[]{:S(2)}) %collective-permute-start.14) | collective-permute-done | bytes 4128 | tf_op jit(solution)/shard_map/ppermute | solution.py:51
  148.9 1.3 collective-permute-start.15
  150.2 6.2 %collective-permute-done.15 = f32[8,128]{1,0:T(8,128)S(1)} collective-permute-done((f32[8,128]{1,0:T(8,128)S(1)}, f32[8,128]{1,0:T(8,128)S(1)}, u32[]{:S(2)}, u32[]{:S(2)}) %collective-permute-start.15) | collective-permute-done | bytes 4128 | tf_op jit(solution)/shard_map/ppermute | solution.py:51
  156.4 3.6 %collective-permute-done.16 = f32[8,128]{1,0:T(8,128)S(1)} collective-permute-done((f32[8,128]{1,0:T(8,128)S(1)}, f32[8,128]{1,0:T(8,128)S(1)}, u32[]{:S(2)}, u32[]{:S(2)}) %collective-permute-start.16) | collective-permute-done | bytes 4128 | tf_op jit(solution)/shard_map/ppermute | solution.py:51
  160.0 2.1 %collective-permute-start.17 = (f32[8,128]{1,0:T(8,128)S(1)}, f32[8,128]{1,0:T(8,128)S(1)}, u32[]{:S(2)}, u32[]{:S(2)}) collective-permute-start(f32[8,128]{1,0:T(8,128)S(1)} %add.129), channel_id=1, source_target_pairs={{0,32},{1,33},{2,34},{3,35},{4,36},{5,37},{6,38},{7,39},{8,40},{9,... | collective-permute-start | bytes 12296 | tf_op jit(solution)/shard_map/ppermute | solution.py:51
  162.1 1.7 %gather_fusion.1 = bf16[8,4,24,256]{3,0,2,1:T(8,128)(2,1)S(1)} fusion(bf16[8,8,28,256]{3,0,2,1:T(8,128)(2,1)S(1)} %select_maximum_fusion, s32[8]{0:T(128)S(1)} %get-tuple-element.27), kind=kCustom, calls=%fused_computation.1 | custom fusion | bytes 786560 | tf_op jit(solution)/shard_map/vmap()/gather | solution.py:80
  163.8 0.8 copy.65
  164.7 0.5 collective-permute-done.17
  165.1 0.5 slice.133
  166.4 0.6 slice.172
  167.0 0.6 slice.173
  (49 shorter events, 1.4 us)
Async XLA Ops:
  0.6 34.5 %copy-start = (bf16[2,256,768]{2,1,0:T(8,128)(2,1)S(1)}, bf16[2,256,768]{2,1,0:T(8,128)(2,1)}, u32[]{:S(2)}) copy-start(bf16[2,256,768]{2,1,0:T(8,128)(2,1)} %param.11) | copy-start | bytes 2359300
  0.6 10.5 %copy-start.2 = (bf16[8,4,24,256]{3,2,1,0:T(8,128)(2,1)S(1)}, bf16[8,4,24,256]{3,2,1,0:T(8,128)(2,1)}, u32[]{:S(2)}) copy-start(bf16[8,4,24,256]{3,2,1,0:T(8,128)(2,1)} %param.13) | copy-start | bytes 1179652
  0.7 10.7 %copy-start.4 = (s32[32,2]{0,1:T(2,128)S(1)}, s32[32,2]{0,1:T(2,128)}, u32[]{:S(2)}) copy-start(s32[32,2]{0,1:T(2,128)} %param.10) | copy-start | bytes 772
  2.0 10.3 %collective-permute-start.1 = (bf16[8,2,24,256]{3,0,2,1:T(8,128)(2,1)S(1)}, bf16[8,2,24,256]{3,0,2,1:T(8,128)(2,1)S(1)}, u32[]{:S(2)}, u32[]{:S(2)}) collective-permute-start(bf16[8,2,24,256]{3,0,2,1:T(8,128)(2,1)S(1)} %get-tuple-element.26), channel_id=1, source_target_pairs={{1,0},{2,1},{3,2},{4,3},{5,4},{6,5},{7,6},{8,7},{9,8},{10,9},{11,1... | collective-permute-start | bytes 589832 | tf_op jit(solution)/shard_map/ppermute | solution.py:65
  9.2 9.1 %collective-permute-start = (bf16[8,2,24,256]{3,0,2,1:T(8,128)(2,1)S(1)}, bf16[8,2,24,256]{3,0,2,1:T(8,128)(2,1)S(1)}, u32[]{:S(2)}, u32[]{:S(2)}) collective-permute-start(bf16[8,2,24,256]{3,0,2,1:T(8,128)(2,1)S(1)} %get-tuple-element.25), channel_id=1, source_target_pairs={{0,1},{1,2},{2,3},{3,4},{4,5},{5,6},{6,7},{7,8},{8,9},{9,10},{10,1... | collective-permute-start | bytes 589832 | tf_op jit(solution)/shard_map/ppermute | solution.py:63
  20.1 5.5 %copy-start.6 = (s32[32]{0:T(128)S(1)}, s32[32]{0:T(128)}, u32[]{:S(2)}) copy-start(s32[32]{0:T(128)} %param.9) | copy-start | bytes 388
  20.1 6.1 %copy-start.5 = (s32[32]{0:T(128)S(1)}, s32[32]{0:T(128)}, u32[]{:S(2)}) copy-start(s32[32]{0:T(128)} %param.8) | copy-start | bytes 388
  21.1 14.0 %all-to-all-start = ((bf16[8,96,512]{2,0,1:T(8,128)(2,1)}), bf16[8,96,512]{2,0,1:T(8,128)(2,1)S(1)}, u32[]{:S(2)}, u32[]{:S(2)}) async-start(bf16[8,96,512]{2,0,1:T(8,128)(2,1)} %pad_maximum_fusion.1), calls=%async_computation | async-start | bytes 1572864 | tf_op jit(solution)/shard_map/all_to_all | solution.py:196
  35.2 1.0 copy-start.3
  69.6 1.0 copy-start.1
  71.5 2.9 %collective-permute-start.4 = (f32[2,2,2,2,2,1,2,4,1024]{8,7,6,5,4,3,2,1,0:T(4,128)S(1)}, f32[2,2,2,2,2,1,2,4,1024]{8,7,6,5,4,3,2,1,0:T(4,128)}, u32[]{:S(2)}, u32[]{:S(2)}) collective-permute-start(f32[2,2,2,2,2,1,2,4,1024]{8,7,6,5,4,3,2,1,0:T(4,128)S(1)} %copy_select_fusion), channel_id=1, source_target_pairs={{0,1},{1,0},{2,3},{3,2},{4,5},{5,4},{6,7},{7,6},{8,9},{9,8},{10,11... | collective-permute-start | bytes 3145736 | tf_op jit(solution)/shard_map/ppermute | solution.py:44
  76.9 14.1 %collective-permute-start.5 = (f32[2,2,2,2,1,1,2,4,1024]{8,7,6,5,4,3,2,1,0:T(4,128)S(1)}, f32[2,2,2,2,1,1,2,4,1024]{8,7,6,5,4,3,2,1,0:T(4,128)S(1)}, u32[]{:S(2)}, u32[]{:S(2)}) collective-permute-start(f32[2,2,2,2,1,1,2,4,1024]{8,7,6,5,4,3,2,1,0:T(4,128)S(1)} %slice_select_fusion), channel_id=1, source_target_pairs={{0,2},{1,3},{2,0},{3,1},{4,6},{5,7},{6,4},{7,5},{8,10},{9,11},{10,... | collective-permute-start | bytes 1572872 | tf_op jit(solution)/shard_map/ppermute | solution.py:44
  91.3 7.6 %collective-permute-start.6 = (f32[2,1,2,2,1,1,2,4,1024]{8,7,6,5,4,3,2,1,0:T(4,128)S(1)}, f32[2,1,2,2,1,1,2,4,1024]{8,7,6,5,4,3,2,1,0:T(4,128)S(1)}, u32[]{:S(2)}, u32[]{:S(2)}) collective-permute-start(f32[2,1,2,2,1,1,2,4,1024]{8,7,6,5,4,3,2,1,0:T(4,128)S(1)} %slice_select_fusion.1), channel_id=1, source_target_pairs={{0,16},{1,17},{2,18},{3,19},{4,20},{5,21},{6,22},{7,23},{8,24},{9,... | collective-permute-start | bytes 786440 | tf_op jit(solution)/shard_map/ppermute | solution.py:44
  99.1 7.8 %collective-permute-start.7 = (f32[2,1,2,1,1,1,2,4,1024]{8,7,6,5,4,3,2,1,0:T(4,128)S(1)}, f32[2,1,2,1,1,1,2,4,1024]{8,7,6,5,4,3,2,1,0:T(4,128)S(1)}, u32[]{:S(2)}, u32[]{:S(2)}) collective-permute-start(f32[2,1,2,1,1,1,2,4,1024]{8,7,6,5,4,3,2,1,0:T(4,128)S(1)} %slice_select_fusion.2), channel_id=1, source_target_pairs={{0,4},{1,5},{2,6},{3,7},{4,0},{5,1},{6,2},{7,3},{8,12},{9,13},{10,... | collective-permute-start | bytes 393224 | tf_op jit(solution)/shard_map/ppermute | solution.py:44
  107.0 5.9 %collective-permute-start.8 = (f32[1,1,2,1,1,1,2,4,1024]{8,7,6,5,4,3,2,1,0:T(4,128)S(1)}, f32[1,1,2,1,1,1,2,4,1024]{8,7,6,5,4,3,2,1,0:T(4,128)S(1)}, u32[]{:S(2)}, u32[]{:S(2)}) collective-permute-start(f32[1,1,2,1,1,1,2,4,1024]{8,7,6,5,4,3,2,1,0:T(4,128)S(1)} %slice_select_fusion.3), channel_id=1, source_target_pairs={{0,32},{1,33},{2,34},{3,35},{4,36},{5,37},{6,38},{7,39},{8,40},{9,... | collective-permute-start | bytes 196616 | tf_op jit(solution)/shard_map/ppermute | solution.py:44
  112.9 7.9 %collective-permute-start.9 = (f32[1,1,1,1,1,1,2,4,1024]{8,7,6,5,4,3,2,1,0:T(4,128)S(1)}, f32[1,1,1,1,1,1,2,4,1024]{8,7,6,5,4,3,2,1,0:T(4,128)S(1)}, u32[]{:S(2)}, u32[]{:S(2)}) collective-permute-start(f32[1,1,1,1,1,1,2,4,1024]{8,7,6,5,4,3,2,1,0:T(4,128)S(1)} %slice_select_fusion.4), channel_id=1, source_target_pairs={{0,8},{1,9},{2,10},{3,11},{4,12},{5,13},{6,14},{7,15},{8,0},{9,1},... | collective-permute-start | bytes 98312 | tf_op jit(solution)/shard_map/ppermute | solution.py:44
  120.8 5.2 %collective-permute-start.10 = (f32[2,4,1024]{2,1,0:T(4,128)S(1)}, f32[2,4,1024]{2,1,0:T(4,128)S(1)}, u32[]{:S(2)}, u32[]{:S(2)}) collective-permute-start(f32[2,4,1024]{2,1,0:T(4,128)S(1)} %add_bitcast_fusion), channel_id=1, source_target_pairs={{0,64},{64,0},{128,192},{192,128},{1,65},{65,1},{129,193},{193,129... | collective-permute-start | bytes 98312 | tf_op jit(solution)/shard_map/ppermute | solution.py:51
  122.5 12.5 %all-to-all-start.1 = ((bf16[32,24,256]{2,1,0:T(8,128)(2,1)}), bf16[32,24,256]{2,1,0:T(8,128)(2,1)S(1)}, u32[]{:S(2)}, u32[]{:S(2)}) async-start(bf16[32,24,256]{2,1,0:T(8,128)(2,1)} %copy.60), calls=%async_computation.1 | async-start | bytes 786432 | tf_op jit(solution)/shard_map/all_to_all | solution.py:230
  126.0 7.7 %collective-permute-start.11 = (f32[2,4,1024]{2,1,0:T(4,128)S(1)}, f32[2,4,1024]{2,1,0:T(4,128)S(1)}, u32[]{:S(2)}, u32[]{:S(2)}) collective-permute-start(f32[2,4,1024]{2,1,0:T(4,128)S(1)} %add.123), channel_id=1, source_target_pairs={{0,128},{64,192},{128,0},{192,64},{1,129},{65,193},{129,1},{193,65... | collective-permute-start | bytes 98312 | tf_op jit(solution)/shard_map/ppermute | solution.py:51
  135.0 1.3 collective-permute-start.12
  136.9 6.7 %collective-permute-start.13 = (f32[8,128]{1,0:T(8,128)S(1)}, f32[8,128]{1,0:T(8,128)S(1)}, u32[]{:S(2)}, u32[]{:S(2)}) collective-permute-start(f32[8,128]{1,0:T(8,128)S(1)} %broadcast_add_fusion), channel_id=1, source_target_pairs={{0,2},{1,3},{2,0},{3,1},{4,6},{5,7},{6,4},{7,5},{8,10},{9,11},{10,... | collective-permute-start | bytes 12296 | tf_op jit(solution)/shard_map/ppermute | solution.py:51
  137.0 25.1 %collective-permute-start.3 = (bf16[8,2,24,256]{3,0,2,1:T(8,128)(2,1)S(1)}, bf16[8,2,24,256]{3,0,2,1:T(8,128)(2,1)S(1)}, u32[]{:S(2)}, u32[]{:S(2)}) collective-permute-start(bf16[8,2,24,256]{3,0,2,1:T(8,128)(2,1)S(1)} %get-tuple-element.24), channel_id=1, source_target_pairs={{1,0},{2,1},{3,2},{4,3},{5,4},{6,5},{7,6},{8,7},{9,8},{10,9},{11,1... | collective-permute-start | bytes 589832 | tf_op jit(solution)/shard_map/ppermute | solution.py:65
  141.7 20.4 %collective-permute-start.2 = (bf16[8,2,24,256]{3,0,2,1:T(8,128)(2,1)S(1)}, bf16[8,2,24,256]{3,0,2,1:T(8,128)(2,1)S(1)}, u32[]{:S(2)}, u32[]{:S(2)}) collective-permute-start(bf16[8,2,24,256]{3,0,2,1:T(8,128)(2,1)S(1)} %get-tuple-element.23), channel_id=1, source_target_pairs={{0,1},{1,2},{2,3},{3,4},{4,5},{5,6},{6,7},{7,8},{8,9},{9,10},{10,1... | collective-permute-start | bytes 589832 | tf_op jit(solution)/shard_map/ppermute | solution.py:63
  144.3 4.6 %collective-permute-start.14 = (f32[8,128]{1,0:T(8,128)S(1)}, f32[8,128]{1,0:T(8,128)S(1)}, u32[]{:S(2)}, u32[]{:S(2)}) collective-permute-start(f32[8,128]{1,0:T(8,128)S(1)} %fusion.48), channel_id=1, source_target_pairs={{0,4},{1,5},{2,6},{3,7},{4,0},{5,1},{6,2},{7,3},{8,12},{9,13},{10,... | collective-permute-start | bytes 12296 | tf_op jit(solution)/shard_map/ppermute | solution.py:51
  148.9 7.5 %collective-permute-start.15 = (f32[8,128]{1,0:T(8,128)S(1)}, f32[8,128]{1,0:T(8,128)S(1)}, u32[]{:S(2)}, u32[]{:S(2)}) collective-permute-start(f32[8,128]{1,0:T(8,128)S(1)} %add.127), channel_id=1, source_target_pairs={{0,8},{1,9},{2,10},{3,11},{4,12},{5,13},{6,14},{7,15},{8,0},{9,1},... | collective-permute-start | bytes 12296 | tf_op jit(solution)/shard_map/ppermute | solution.py:51
  156.4 3.6 %collective-permute-start.16 = (f32[8,128]{1,0:T(8,128)S(1)}, f32[8,128]{1,0:T(8,128)S(1)}, u32[]{:S(2)}, u32[]{:S(2)}) collective-permute-start(f32[8,128]{1,0:T(8,128)S(1)} %add.128), channel_id=1, source_target_pairs={{0,16},{1,17},{2,18},{3,19},{4,20},{5,21},{6,22},{7,23},{8,24},{9,... | collective-permute-start | bytes 12296 | tf_op jit(solution)/shard_map/ppermute | solution.py:51
  160.0 5.1 %collective-permute-start.17 = (f32[8,128]{1,0:T(8,128)S(1)}, f32[8,128]{1,0:T(8,128)S(1)}, u32[]{:S(2)}, u32[]{:S(2)}) collective-permute-start(f32[8,128]{1,0:T(8,128)S(1)} %add.129), channel_id=1, source_target_pairs={{0,32},{1,33},{2,34},{3,35},{4,36},{5,37},{6,38},{7,39},{8,40},{9,... | collective-permute-start | bytes 12296 | tf_op jit(solution)/shard_map/ppermute | solution.py:51

commit v5 on v3

--- a/solution.py
+++ b/solution.py
@@ -28,20 +28,34 @@
     return [b for b in preferred if b < bits] + [b for b in range(bits) if b not in preferred]
 
 
-def halving_sum(pieces, axis, bit_order):
+def tile_twins(count):
+    bits = count.bit_length() - 1
+    pairs = {1: 4, 4: 1, 2: 5, 5: 2}
+    return {b: t for b, t in pairs.items() if b < bits and t < bits}
+
+
+def halving_sum(pieces, axis, bit_order, twins):
     count = lax.axis_size(axis)
     me = lax.axis_index(axis)
     bits = axis_bits(axis)
     rest = pieces.shape[1:]
+    odd = (me & 1) == 1
     x = pieces.reshape((2,) * bits + rest)
-    for bit in bit_order:
+    for step, bit in enumerate(bit_order):
+        if step == 1 and twins:
+            order = list(range(x.ndim))
+            for b, t in twins.items():
+                order[bits - 1 - b] = bits - 1 - t
+            x = jnp.where(odd, jnp.transpose(x, order), x)
+        twin = twins.get(bit, bit) if step > 0 else bit
         dim = bits - 1 - bit
-        mine = (me >> bit) & 1
+        mine = jnp.where(odd, (me >> twin) & 1, (me >> bit) & 1)
         low = lax.index_in_dim(x, 0, dim, keepdims=True)
         high = lax.index_in_dim(x, 1, dim, keepdims=True)
         keep = jnp.where(mine == 1, high, low)
         send = jnp.where(mine == 1, low, high)
-        x = keep + lax.ppermute(send, axis, xor_pairs(count, bit))
+        pairs = [(i, i ^ (1 << (twin if i & 1 else bit))) for i in range(count)]
+        x = keep + lax.ppermute(send, axis, pairs)
     return x.reshape(rest)
 
 
@@ -190,10 +204,14 @@
     all_hot = (types[:, None] == jnp.arange(2)[None, :]).astype(bf16)
     flat_feats = warped.reshape(own_count, cell_count, channels)
     flat_grads = d_out.reshape(own_count, cell_count, channels)
-    all_feats, all_grads = (
-        lax.all_to_all(flat_feats, "agent", split_axis=1, concat_axis=0, tiled=True),
-        lax.all_to_all(flat_grads, "agent", split_axis=1, concat_axis=0, tiled=True),
-    )
+    both = lax.all_to_all(
+        jnp.concatenate([flat_feats, flat_grads], axis=-1),
+        "agent",
+        split_axis=1,
+        concat_axis=0,
+        tiled=True,
+    )
+    all_feats, all_grads = both[..., :channels], both[..., channels:]
     part_cells = all_feats.shape[1]
     pairs = agents * part_cells
     is_type1 = (types == 1)[None, :, None]
@@ -234,7 +252,7 @@
     tiles = lax.axis_size("tile")
     share_rows = channels // tiles
     pieces = raw_all.reshape(2, tiles, share_rows, 4 * channels).transpose(1, 0, 2, 3)
-    share_all = halving_sum(pieces, "tile", tile_bit_order(tiles))
+    share_all = halving_sum(pieces, "tile", tile_bit_order(tiles), tile_twins(tiles))
     share_all = doubling_sum(share_all, "agent", list(range(axis_bits("agent"))))
     square_sum = jnp.broadcast_to(jnp.sum(share_all * share_all), (8, 128))
     square_sum = doubling_sum(square_sum, "tile", list(range(axis_bits("tile"))))[0, 0]

time: 166 us -> 160 us (0.964)
  starting transfers between devices: 47.6 us -> 37.1 us
  waiting for transfers between devices: 61.6 us -> 66.1 us
  local copies, waits for them, and re-layouts: 16.5 us -> 14.3 us
  other arithmetic: 9.41 us -> 11.5 us
    ppermute x6, starting transfers between devices: 10.7 us -> 5.5 us  [halving_sum(): x = keep + lax.ppermute(send, axis, pairs)]
    ppermute x2, waiting for transfers between devices: 1.07 us -> 5.93 us  [with_halo(): lax.ppermute(tail, axis, [(i, (i + 1) % count) for i in range(ends)])]
    all_to_all x2 -> x1, starting transfers between devices: 7.92 us -> 4.46 us  [body(): lax.all_to_all(jnp.concatenate([flat_feats, flat_grads], axis=-1), 'agent...]
    unnamed x17 -> x15, local copies, waits for them, and re-layouts: 4.1 us -> 2.54 us
    all_to_all x2 -> x1, waiting for transfers between devices: 9.2 us -> 8.94 us  [body(): lax.all_to_all(jnp.concatenate([flat_feats, flat_grads], axis=-1), 'agent...]
  transfers between devices with their start and end apart: 21 -> 20, of which waited for: 15 -> 15; matrix products, arithmetic and copies ran while one was open for 9% -> 6% of each run, Pallas kernels for 0% -> 0%
where the time goes in v5:
time: 160 us; the launch traced here: 159 us
  waiting for transfers between devices  66.1 us (41%)
  starting transfers between devices  37.1 us (23%)
  Pallas kernels  19.5 us (12%)
  local copies, waits for them, and re-layouts  14.3 us (9%)
  other arithmetic  11.5 us (7%)
  matrix products  8.82 us (6%)
  between operations  1.88 us (1%)
    ppermute x6, waiting for transfers between devices, halving_sum(): x = keep + lax.ppermute(send, axis, pairs)  30.6 us
    ppermute x8, waiting for transfers between devices, doubling_sum(): x = x + lax.ppermute(x, axis, xor_pairs(count, bit))  19.7 us
    pallas_call x1, Pallas kernels, cell_attention(): pl.pallas_call(functools.partial(attention_kernel, block_size), grid=(cel...  19.5 us
    ppermute x2, starting transfers between devices, with_halo(): lax.ppermute(head, axis, [((i + 1) % count, i) for i in range(ends)])  11.8 us
    all_to_all x1, waiting for transfers between devices, body(): lax.all_to_all(jnp.concatenate([flat_feats, flat_grads], axis=-1), 'agent...  8.94 us
    ppermute x8, starting transfers between devices, doubling_sum(): x = x + lax.ppermute(x, axis, xor_pairs(count, bit))  8.04 us
    ppermute x2, waiting for transfers between devices, with_halo(): lax.ppermute(tail, axis, [(i, (i + 1) % count) for i in range(ends)])  5.93 us
    ppermute x6, starting transfers between devices, halving_sum(): x = keep + lax.ppermute(send, axis, pairs)  5.5 us
  transfers between devices with their start and end apart: 20, of which 15 were waited for; matrix products, arithmetic and copies ran while one was open for 6% of the time, Pallas kernels for 0%

profile of v5, /device:TPU:2, one launch (start us, length us, event | category | flops | bytes accessed | tf_op | source)
XLA Modules:
  0.0 159.2 jit_solution(18235597582366857154)
XLA Ops:
  0.7 1.3 copy.50
  2.0 7.2 %collective-permute-start.1 = (bf16[8,2,24,256]{3,0,2,1:T(8,128)(2,1)S(1)}, bf16[8,2,24,256]{3,0,2,1:T(8,128)(2,1)S(1)}, u32[]{:S(2)}, u32[]{:S(2)}) collective-permute-start(bf16[8,2,24,256]{3,0,2,1:T(8,128)(2,1)S(1)} %get-tuple-element.26), channel_id=1, source_target_pairs={{1,0},{2,1},{3,2},{4,3},{5,4},{6,5},{7,6},{8,7},{9,8},{10,9},{11,1... | collective-permute-start | bytes 589832 | tf_op jit(solution)/shard_map/ppermute | solution.py:79
  9.2 1.9 %collective-permute-start = (bf16[8,2,24,256]{3,0,2,1:T(8,128)(2,1)S(1)}, bf16[8,2,24,256]{3,0,2,1:T(8,128)(2,1)S(1)}, u32[]{:S(2)}, u32[]{:S(2)}) collective-permute-start(bf16[8,2,24,256]{3,0,2,1:T(8,128)(2,1)S(1)} %get-tuple-element.25), channel_id=1, source_target_pairs={{0,1},{1,2},{2,3},{3,4},{4,5},{5,6},{6,7},{7,8},{8,9},{9,10},{10,1... | collective-permute-start | bytes 589832 | tf_op jit(solution)/shard_map/ppermute | solution.py:77
  11.1 0.2 copy.53
  11.5 0.9 collective-permute-done.1
  12.4 5.9 %collective-permute-done = bf16[8,2,24,256]{3,0,2,1:T(8,128)(2,1)S(1)} collective-permute-done((bf16[8,2,24,256]{3,0,2,1:T(8,128)(2,1)S(1)}, bf16[8,2,24,256]{3,0,2,1:T(8,128)(2,1)S(1)}, u32[]{:S(2)}, u32[]{:S(2)}) %collective-permute-start) | collective-permute-done | bytes 196640 | tf_op jit(solution)/shard_map/ppermute | solution.py:77
  18.4 1.7 %gather_fusion = bf16[8,4,24,256]{3,0,2,1:T(8,128)(2,1)S(1)} fusion(bf16[8,8,28,256]{3,0,2,1:T(8,128)(2,1)S(1)} %fusion.18, s32[8]{0:T(128)S(1)} %get-tuple-element.28), kind=kCustom, calls=%fused_computation | custom fusion | bytes 786560 | tf_op jit(solution)/shard_map/vmap()/gather | solution.py:94
  20.1 1.0 pad_maximum_fusion.1
  21.1 4.5 %all-to-all-start = ((bf16[8,96,512]{2,0,1:T(8,128)(2,1)}), bf16[8,96,512]{2,0,1:T(8,128)(2,1)S(1)}, u32[]{:S(2)}, u32[]{:S(2)}) async-start(bf16[8,96,512]{2,0,1:T(8,128)(2,1)} %pad_maximum_fusion.1), calls=%async_computation | async-start | bytes 1572864 | tf_op jit(solution)/shard_map/all_to_all | solution.py:207
  25.6 0.5 fusion.37.valid_ref
  26.1 8.9 %all-to-all-done = bf16[8,96,512]{2,0,1:T(8,128)(2,1)S(1)} async-done(((bf16[8,96,512]{2,0,1:T(8,128)(2,1)}), bf16[8,96,512]{2,0,1:T(8,128)(2,1)S(1)}, u32[]{:S(2)}, u32[]{:S(2)}) %all-to-all-start) | async-done | bytes 786464 | tf_op jit(solution)/shard_map/all_to_all | solution.py:207
  35.2 0.8 convert_bitcast_fusion
  36.0 0.2 copy-done.2
  36.1 0.4 fusion.12
  36.5 1.2 fusion.13.qkv_ref
  37.7 0.8 fusion.29.da_ref
  38.6 19.5 %shard_map.94 = (bf16[24,32,256]{2,1,0:T(8,128)(2,1)}, bf16[2,24,32,768]{3,2,1,0:T(8,128)(2,1)}) custom-call(f32[1,32]{1,0:T(1,128)} %fusion.37.valid_ref, bf16[24,32,768]{2,1,0:T(8,128)(2,1)} %fusion.13.qkv_ref, bf16[24,32,256]{2,1,0:T(8,128)(2,1)} %fusion.29.da_ref), custom_call_target="tpu_custom_call" | custom-call | flops 2415919104 | bytes 4325376 | tf_op jit(solution)/shard_map/pallas_call | solution.py:167
  58.1 1.4 convolution_bitcast_fusion
  59.6 3.1 %fusion.7 = f32[2,2,256,768]{2,3,1,0:T(8,128)S(1)} fusion(bf16[2,24,32,768]{3,2,1,0:T(8,128)(2,1)} %get-tuple-element.5, pred[2,32]{1,0:T(4,128)(4,1)S(1)} %pad_add_fusion, bf16[24,32,256]{2,1,0:T(8,128)(2,1)S(1)} %slice_bitcast_fusion.7), kind=kOutput, calls=%fused_computation.11 | convolution fusion | flops 1208352768 | bytes 5898304 | tf_op jit(solution)/shard_map/tgac,sgae->stce/dot_general | solution.py:244
  62.7 0.2 fusion.11
  62.9 0.1 pad_maximum_fusion
  63.1 2.4 %copy.61 = f32[2,256,1024]{2,0,1:T(2,128)} copy(f32[2,256,1024]{1,2,0:T(8,128)S(1)} %pad_maximum_fusion) | data formatting | bytes 4194304 | tf_op jit(solution)/shard_map/concatenate | solution.py:251
  65.5 2.3 %fusion.45 = (f32[2,2,2,2,2,1,2,4,1024]{8,6,7,5,4,3,2,1,0:T(2,128)S(1)}, f32[2,2,2,2,2,1,2,4,1024]{8,6,7,5,4,3,2,1,0:T(2,128)S(1)}) fusion(f32[2,2,2,2,2,2,2,4,1024]{8,6,7,5,4,3,2,1,0:T(2,128)} %bitcast.124), kind=kLoop, calls=%fused_computation.92 | loop fusion | bytes 4194304 | tf_op jit(solution)/shard_map/slice | solution.py:54
  67.7 1.9 %copy_select_fusion.1 = f32[2,2,2,2,2,1,2,4,1024]{8,7,6,5,4,3,2,1,0:T(4,128)} fusion(f32[2,2,2,2,2,1,2,4,1024]{8,6,7,5,4,3,2,1,0:T(2,128)S(1)} %get-tuple-element.22, f32[2,2,2,2,2,1,2,4,1024]{8,6,7,5,4,3,2,1,0:T(2,128)S(1)} %get-tuple-element.21, pred[]{:T(512)S(6)} %eq.48), kind=kLoop, calls=%fused_computation.24 | loop fusion | flops 262144 | bytes 3145729 | tf_op jit(solution)/shard_map/jit(_where)/select_n | solution.py:56
  69.6 3.0 %collective-permute-done.4 = f32[2,2,2,2,2,1,2,4,1024]{8,7,6,5,4,3,2,1,0:T(4,128)} collective-permute-done((f32[2,2,2,2,2,1,2,4,1024]{8,7,6,5,4,3,2,1,0:T(4,128)}, f32[2,2,2,2,2,1,2,4,1024]{8,7,6,5,4,3,2,1,0:T(4,128)}, u32[]{:S(2)}, u32[]{:S(2)}) %collective-permute-start.4) | collective-permute-done | bytes 1048608 | tf_op jit(solution)/shard_map/ppermute | solution.py:58
  72.6 2.2 %select_add_fusion = f32[2,2,2,2,2,1,2,4,1024]{8,7,6,5,4,3,2,1,0:T(4,128)S(1)} fusion(f32[2,2,2,2,2,1,2,4,1024]{8,7,6,5,4,3,2,1,0:T(4,128)} %collective-permute-done.4, f32[2,2,2,2,2,1,2,4,1024]{8,6,7,5,4,3,2,1,0:T(2,128)S(1)} %get-tuple-element.22, f32[2,2,2,2,2,1,2,4,1024]{8,6,7,5,4,3,2,1,0:T(2,128)S(1)} %get-tuple-element.21, pred[]{:T(512)S(6)} %eq.48), kind=kLoop, calls=%fused_computation.23 | loop fusion | flops 524288 | bytes 4194305 | tf_op jit(solution)/shard_map/add | solution.py:58
  74.9 0.2 copy_select_fusion
  75.1 0.2 slice_select_fusion
  75.4 9.2 %collective-permute-done.5 = f32[2,2,2,2,1,1,2,4,1024]{8,7,6,5,4,3,2,1,0:T(4,128)S(1)} collective-permute-done((f32[2,2,2,2,1,1,2,4,1024]{8,7,6,5,4,3,2,1,0:T(4,128)S(1)}, f32[2,2,2,2,1,1,2,4,1024]{8,7,6,5,4,3,2,1,0:T(4,128)S(1)}, u32[]{:S(2)}, u32[]{:S(2)}) %collective-permute-start.5) | collective-permute-done | bytes 524320 | tf_op jit(solution)/shard_map/ppermute | solution.py:58
  84.5 0.3 select_add_fusion.1
  84.9 0.3 collective-permute-start.6
  85.2 6.3 %collective-permute-done.6 = f32[2,1,2,2,1,1,2,4,1024]{8,7,6,5,4,3,2,1,0:T(4,128)S(1)} collective-permute-done((f32[2,1,2,2,1,1,2,4,1024]{8,7,6,5,4,3,2,1,0:T(4,128)S(1)}, f32[2,1,2,2,1,1,2,4,1024]{8,7,6,5,4,3,2,1,0:T(4,128)S(1)}, u32[]{:S(2)}, u32[]{:S(2)}) %collective-permute-start.6) | collective-permute-done | bytes 262176 | tf_op jit(solution)/shard_map/ppermute | solution.py:58
  91.8 6.7 %collective-permute-done.7 = f32[2,1,2,1,1,1,2,4,1024]{8,7,6,5,4,3,2,1,0:T(4,128)S(1)} collective-permute-done((f32[2,1,2,1,1,1,2,4,1024]{8,7,6,5,4,3,2,1,0:T(4,128)S(1)}, f32[2,1,2,1,1,1,2,4,1024]{8,7,6,5,4,3,2,1,0:T(4,128)S(1)}, u32[]{:S(2)}, u32[]{:S(2)}) %collective-permute-start.7) | collective-permute-done | bytes 131104 | tf_op jit(solution)/shard_map/ppermute | solution.py:58
  98.6 2.5 %collective-permute-start.8 = (f32[1,1,2,1,1,1,2,4,1024]{8,7,6,5,4,3,2,1,0:T(4,128)S(1)}, f32[1,1,2,1,1,1,2,4,1024]{8,7,6,5,4,3,2,1,0:T(4,128)S(1)}, u32[]{:S(2)}, u32[]{:S(2)}) collective-permute-start(f32[1,1,2,1,1,1,2,4,1024]{8,7,6,5,4,3,2,1,0:T(4,128)S(1)} %slice_select_fusion.3), channel_id=1, source_target_pairs={{0,32},{1,5},{2,34},{3,7},{4,36},{5,1},{6,38},{7,3},{8,40},{9,13},... | collective-permute-start | bytes 196616 | tf_op jit(solution)/shard_map/ppermute | solution.py:58
  101.1 3.1 %fusion.4 = f32[2,2,24,32,256]{4,3,2,1,0:T(8,128)S(1)} fusion(bf16[2,24,32,768]{3,2,1,0:T(8,128)(2,1)} %get-tuple-element.5, bf16[2,256,768]{2,1,0:T(8,128)(2,1)S(1)} %copy-done), kind=kOutput, calls=%fused_computation.10 | convolution fusion | flops 1207959552 | bytes 6291456 | tf_op jit(solution)/shard_map/sgae,tce->stgac/dot_general | solution.py:235
  104.2 0.3 collective-permute-done.8
  104.5 2.5 %collective-permute-start.9 = (f32[1,1,1,1,1,1,2,4,1024]{8,7,6,5,4,3,2,1,0:T(4,128)S(1)}, f32[1,1,1,1,1,1,2,4,1024]{8,7,6,5,4,3,2,1,0:T(4,128)S(1)}, u32[]{:S(2)}, u32[]{:S(2)}) collective-permute-start(f32[1,1,1,1,1,1,2,4,1024]{8,7,6,5,4,3,2,1,0:T(4,128)S(1)} %slice_select_fusion.4), channel_id=1, source_target_pairs={{0,8},{1,9},{2,10},{3,11},{4,12},{5,13},{6,14},{7,15},{8,0},{9,1},... | collective-permute-start | bytes 98312 | tf_op jit(solution)/shard_map/ppermute | solution.py:58
  107.0 0.2 slice_add_fusion.1
  107.3 5.1 %collective-permute-done.9 = f32[1,1,1,1,1,1,2,4,1024]{8,7,6,5,4,3,2,1,0:T(4,128)S(1)} collective-permute-done((f32[1,1,1,1,1,1,2,4,1024]{8,7,6,5,4,3,2,1,0:T(4,128)S(1)}, f32[1,1,1,1,1,1,2,4,1024]{8,7,6,5,4,3,2,1,0:T(4,128)S(1)}, u32[]{:S(2)}, u32[]{:S(2)}) %collective-permute-start.9) | collective-permute-done | bytes 32800 | tf_op jit(solution)/shard_map/ppermute | solution.py:58
  112.4 0.7 collective-permute-start.10
  113.1 0.1 fusion.28
  113.2 1.0 copy.59
  114.2 3.5 %all-to-all-start.1 = ((bf16[32,24,256]{2,1,0:T(8,128)(2,1)}), bf16[32,24,256]{2,1,0:T(8,128)(2,1)S(1)}, u32[]{:S(2)}, u32[]{:S(2)}) async-start(bf16[32,24,256]{2,1,0:T(8,128)(2,1)} %copy.59), calls=%async_computation.1 | async-start | bytes 786432 | tf_op jit(solution)/shard_map/all_to_all | solution.py:241
  117.7 3.6 %collective-permute-start.11 = (f32[2,4,1024]{2,1,0:T(4,128)S(1)}, f32[2,4,1024]{2,1,0:T(4,128)S(1)}, u32[]{:S(2)}, u32[]{:S(2)}) collective-permute-start(f32[2,4,1024]{2,1,0:T(4,128)S(1)} %add.123), channel_id=1, source_target_pairs={{0,128},{64,192},{128,0},{192,64},{1,129},{65,193},{129,1},{193,65... | collective-permute-start | bytes 98312 | tf_op jit(solution)/shard_map/ppermute | solution.py:65
  121.2 4.1 %collective-permute-done.11 = f32[2,4,1024]{2,1,0:T(4,128)S(1)} collective-permute-done((f32[2,4,1024]{2,1,0:T(4,128)S(1)}, f32[2,4,1024]{2,1,0:T(4,128)S(1)}, u32[]{:S(2)}, u32[]{:S(2)}) %collective-permute-start.11) | collective-permute-done | bytes 32800 | tf_op jit(solution)/shard_map/ppermute | solution.py:65
  125.3 0.6 multiply_reduce_fusion
  125.9 0.6 broadcast_in_dim.68
  126.8 1.1 collective-permute-done.12
  127.9 0.6 broadcast_add_fusion
  128.6 4.7 %collective-permute-start.3 = (bf16[8,2,24,256]{3,0,2,1:T(8,128)(2,1)S(1)}, bf16[8,2,24,256]{3,0,2,1:T(8,128)(2,1)S(1)}, u32[]{:S(2)}, u32[]{:S(2)}) collective-permute-start(bf16[8,2,24,256]{3,0,2,1:T(8,128)(2,1)S(1)} %get-tuple-element.24), channel_id=1, source_target_pairs={{1,0},{2,1},{3,2},{4,3},{5,4},{6,5},{7,6},{8,7},{9,8},{10,9},{11,1... | collective-permute-start | bytes 589832 | tf_op jit(solution)/shard_map/ppermute | solution.py:79
  133.3 1.9 %collective-permute-start.2 = (bf16[8,2,24,256]{3,0,2,1:T(8,128)(2,1)S(1)}, bf16[8,2,24,256]{3,0,2,1:T(8,128)(2,1)S(1)}, u32[]{:S(2)}, u32[]{:S(2)}) collective-permute-start(bf16[8,2,24,256]{3,0,2,1:T(8,128)(2,1)S(1)} %get-tuple-element.23), channel_id=1, source_target_pairs={{0,1},{1,2},{2,3},{3,4},{4,5},{5,6},{6,7},{7,8},{8,9},{9,10},{10,1... | collective-permute-start | bytes 589832 | tf_op jit(solution)/shard_map/ppermute | solution.py:77
  135.3 0.7 fusion.48
  135.9 0.3 collective-permute-start.14
  136.2 4.3 %collective-permute-done.14 = f32[8,128]{1,0:T(8,128)S(1)} collective-permute-done((f32[8,128]{1,0:T(8,128)S(1)}, f32[8,128]{1,0:T(8,128)S(1)}, u32[]{:S(2)}, u32[]{:S(2)}) %collective-permute-start.14) | collective-permute-done | bytes 4128 | tf_op jit(solution)/shard_map/ppermute | solution.py:65
  140.5 1.3 collective-permute-start.15
  141.8 6.2 %collective-permute-done.15 = f32[8,128]{1,0:T(8,128)S(1)} collective-permute-done((f32[8,128]{1,0:T(8,128)S(1)}, f32[8,128]{1,0:T(8,128)S(1)}, u32[]{:S(2)}, u32[]{:S(2)}) %collective-permute-start.15) | collective-permute-done | bytes 4128 | tf_op jit(solution)/shard_map/ppermute | solution.py:65
  148.0 3.6 %collective-permute-done.16 = f32[8,128]{1,0:T(8,128)S(1)} collective-permute-done((f32[8,128]{1,0:T(8,128)S(1)}, f32[8,128]{1,0:T(8,128)S(1)}, u32[]{:S(2)}, u32[]{:S(2)}) %collective-permute-start.16) | collective-permute-done | bytes 4128 | tf_op jit(solution)/shard_map/ppermute | solution.py:65
  151.6 2.1 %collective-permute-start.17 = (f32[8,128]{1,0:T(8,128)S(1)}, f32[8,128]{1,0:T(8,128)S(1)}, u32[]{:S(2)}, u32[]{:S(2)}) collective-permute-start(f32[8,128]{1,0:T(8,128)S(1)} %add.129), channel_id=1, source_target_pairs={{0,32},{1,33},{2,34},{3,35},{4,36},{5,37},{6,38},{7,39},{8,40},{9,... | collective-permute-start | bytes 12296 | tf_op jit(solution)/shard_map/ppermute | solution.py:65
  153.8 1.7 %gather_fusion.1 = bf16[8,4,24,256]{3,0,2,1:T(8,128)(2,1)S(1)} fusion(bf16[8,8,28,256]{3,0,2,1:T(8,128)(2,1)S(1)} %select_maximum_fusion, s32[8]{0:T(128)S(1)} %get-tuple-element.27), kind=kCustom, calls=%fused_computation.1 | custom fusion | bytes 786560 | tf_op jit(solution)/shard_map/vmap()/gather | solution.py:94
  155.5 0.8 copy.65
  156.3 0.4 collective-permute-done.17
  156.8 0.5 slice.133
  158.0 0.6 slice.172
  158.6 0.6 slice.173
  (47 shorter events, 1.3 us)
Async XLA Ops:
  0.6 34.5 %copy-start = (bf16[2,256,768]{2,1,0:T(8,128)(2,1)S(1)}, bf16[2,256,768]{2,1,0:T(8,128)(2,1)}, u32[]{:S(2)}) copy-start(bf16[2,256,768]{2,1,0:T(8,128)(2,1)} %param.11) | copy-start | bytes 2359300
  0.6 10.5 %copy-start.1 = (bf16[8,4,24,256]{3,2,1,0:T(8,128)(2,1)S(1)}, bf16[8,4,24,256]{3,2,1,0:T(8,128)(2,1)}, u32[]{:S(2)}) copy-start(bf16[8,4,24,256]{3,2,1,0:T(8,128)(2,1)} %param.13) | copy-start | bytes 1179652
  0.7 10.7 %copy-start.3 = (s32[32,2]{0,1:T(2,128)S(1)}, s32[32,2]{0,1:T(2,128)}, u32[]{:S(2)}) copy-start(s32[32,2]{0,1:T(2,128)} %param.10) | copy-start | bytes 772
  2.0 10.3 %collective-permute-start.1 = (bf16[8,2,24,256]{3,0,2,1:T(8,128)(2,1)S(1)}, bf16[8,2,24,256]{3,0,2,1:T(8,128)(2,1)S(1)}, u32[]{:S(2)}, u32[]{:S(2)}) collective-permute-start(bf16[8,2,24,256]{3,0,2,1:T(8,128)(2,1)S(1)} %get-tuple-element.26), channel_id=1, source_target_pairs={{1,0},{2,1},{3,2},{4,3},{5,4},{6,5},{7,6},{8,7},{9,8},{10,9},{11,1... | collective-permute-start | bytes 589832 | tf_op jit(solution)/shard_map/ppermute | solution.py:79
  9.2 9.1 %collective-permute-start = (bf16[8,2,24,256]{3,0,2,1:T(8,128)(2,1)S(1)}, bf16[8,2,24,256]{3,0,2,1:T(8,128)(2,1)S(1)}, u32[]{:S(2)}, u32[]{:S(2)}) collective-permute-start(bf16[8,2,24,256]{3,0,2,1:T(8,128)(2,1)S(1)} %get-tuple-element.25), channel_id=1, source_target_pairs={{0,1},{1,2},{2,3},{3,4},{4,5},{5,6},{6,7},{7,8},{8,9},{9,10},{10,1... | collective-permute-start | bytes 589832 | tf_op jit(solution)/shard_map/ppermute | solution.py:77
  20.1 5.4 %copy-start.4 = (s32[32]{0:T(128)S(1)}, s32[32]{0:T(128)}, u32[]{:S(2)}) copy-start(s32[32]{0:T(128)} %param.8) | copy-start | bytes 388
  20.1 5.5 %copy-start.5 = (s32[32]{0:T(128)S(1)}, s32[32]{0:T(128)}, u32[]{:S(2)}) copy-start(s32[32]{0:T(128)} %param.9) | copy-start | bytes 388
  21.1 14.0 %all-to-all-start = ((bf16[8,96,512]{2,0,1:T(8,128)(2,1)}), bf16[8,96,512]{2,0,1:T(8,128)(2,1)S(1)}, u32[]{:S(2)}, u32[]{:S(2)}) async-start(bf16[8,96,512]{2,0,1:T(8,128)(2,1)} %pad_maximum_fusion.1), calls=%async_computation | async-start | bytes 1572864 | tf_op jit(solution)/shard_map/all_to_all | solution.py:207
  35.2 1.0 copy-start.2
  69.6 3.0 %collective-permute-start.4 = (f32[2,2,2,2,2,1,2,4,1024]{8,7,6,5,4,3,2,1,0:T(4,128)}, f32[2,2,2,2,2,1,2,4,1024]{8,7,6,5,4,3,2,1,0:T(4,128)}, u32[]{:S(2)}, u32[]{:S(2)}) collective-permute-start(f32[2,2,2,2,2,1,2,4,1024]{8,7,6,5,4,3,2,1,0:T(4,128)} %copy_select_fusion.1), channel_id=1, source_target_pairs={{0,1},{1,0},{2,3},{3,2},{4,5},{5,4},{6,7},{7,6},{8,9},{9,8},{10,11... | collective-permute-start | bytes 3145736 | tf_op jit(solution)/shard_map/ppermute | solution.py:58
  75.3 9.3 %collective-permute-start.5 = (f32[2,2,2,2,1,1,2,4,1024]{8,7,6,5,4,3,2,1,0:T(4,128)S(1)}, f32[2,2,2,2,1,1,2,4,1024]{8,7,6,5,4,3,2,1,0:T(4,128)S(1)}, u32[]{:S(2)}, u32[]{:S(2)}) collective-permute-start(f32[2,2,2,2,1,1,2,4,1024]{8,7,6,5,4,3,2,1,0:T(4,128)S(1)} %slice_select_fusion), channel_id=1, source_target_pairs={{0,2},{1,17},{2,0},{3,19},{4,6},{5,21},{6,4},{7,23},{8,10},{9,25},... | collective-permute-start | bytes 1572872 | tf_op jit(solution)/shard_map/ppermute | solution.py:58
  84.9 6.6 %collective-permute-start.6 = (f32[2,1,2,2,1,1,2,4,1024]{8,7,6,5,4,3,2,1,0:T(4,128)S(1)}, f32[2,1,2,2,1,1,2,4,1024]{8,7,6,5,4,3,2,1,0:T(4,128)S(1)}, u32[]{:S(2)}, u32[]{:S(2)}) collective-permute-start(f32[2,1,2,2,1,1,2,4,1024]{8,7,6,5,4,3,2,1,0:T(4,128)S(1)} %slice_select_fusion.1), channel_id=1, source_target_pairs={{0,16},{1,3},{2,18},{3,1},{4,20},{5,7},{6,22},{7,5},{8,24},{9,11},... | collective-permute-start | bytes 786440 | tf_op jit(solution)/shard_map/ppermute | solution.py:58
  91.7 6.8 %collective-permute-start.7 = (f32[2,1,2,1,1,1,2,4,1024]{8,7,6,5,4,3,2,1,0:T(4,128)S(1)}, f32[2,1,2,1,1,1,2,4,1024]{8,7,6,5,4,3,2,1,0:T(4,128)S(1)}, u32[]{:S(2)}, u32[]{:S(2)}) collective-permute-start(f32[2,1,2,1,1,1,2,4,1024]{8,7,6,5,4,3,2,1,0:T(4,128)S(1)} %slice_select_fusion.2), channel_id=1, source_target_pairs={{0,4},{1,33},{2,6},{3,35},{4,0},{5,37},{6,2},{7,39},{8,12},{9,41},... | collective-permute-start | bytes 393224 | tf_op jit(solution)/shard_map/ppermute | solution.py:58
  98.6 5.9 %collective-permute-start.8 = (f32[1,1,2,1,1,1,2,4,1024]{8,7,6,5,4,3,2,1,0:T(4,128)S(1)}, f32[1,1,2,1,1,1,2,4,1024]{8,7,6,5,4,3,2,1,0:T(4,128)S(1)}, u32[]{:S(2)}, u32[]{:S(2)}) collective-permute-start(f32[1,1,2,1,1,1,2,4,1024]{8,7,6,5,4,3,2,1,0:T(4,128)S(1)} %slice_select_fusion.3), channel_id=1, source_target_pairs={{0,32},{1,5},{2,34},{3,7},{4,36},{5,1},{6,38},{7,3},{8,40},{9,13},... | collective-permute-start | bytes 196616 | tf_op jit(solution)/shard_map/ppermute | solution.py:58
  104.5 7.9 %collective-permute-start.9 = (f32[1,1,1,1,1,1,2,4,1024]{8,7,6,5,4,3,2,1,0:T(4,128)S(1)}, f32[1,1,1,1,1,1,2,4,1024]{8,7,6,5,4,3,2,1,0:T(4,128)S(1)}, u32[]{:S(2)}, u32[]{:S(2)}) collective-permute-start(f32[1,1,1,1,1,1,2,4,1024]{8,7,6,5,4,3,2,1,0:T(4,128)S(1)} %slice_select_fusion.4), channel_id=1, source_target_pairs={{0,8},{1,9},{2,10},{3,11},{4,12},{5,13},{6,14},{7,15},{8,0},{9,1},... | collective-permute-start | bytes 98312 | tf_op jit(solution)/shard_map/ppermute | solution.py:58
  112.4 5.2 %collective-permute-start.10 = (f32[2,4,1024]{2,1,0:T(4,128)S(1)}, f32[2,4,1024]{2,1,0:T(4,128)S(1)}, u32[]{:S(2)}, u32[]{:S(2)}) collective-permute-start(f32[2,4,1024]{2,1,0:T(4,128)S(1)} %add_bitcast_fusion), channel_id=1, source_target_pairs={{0,64},{64,0},{128,192},{192,128},{1,65},{65,1},{129,193},{193,129... | collective-permute-start | bytes 98312 | tf_op jit(solution)/shard_map/ppermute | solution.py:65
  114.2 12.5 %all-to-all-start.1 = ((bf16[32,24,256]{2,1,0:T(8,128)(2,1)}), bf16[32,24,256]{2,1,0:T(8,128)(2,1)S(1)}, u32[]{:S(2)}, u32[]{:S(2)}) async-start(bf16[32,24,256]{2,1,0:T(8,128)(2,1)} %copy.59), calls=%async_computation.1 | async-start | bytes 786432 | tf_op jit(solution)/shard_map/all_to_all | solution.py:241
  117.7 7.7 %collective-permute-start.11 = (f32[2,4,1024]{2,1,0:T(4,128)S(1)}, f32[2,4,1024]{2,1,0:T(4,128)S(1)}, u32[]{:S(2)}, u32[]{:S(2)}) collective-permute-start(f32[2,4,1024]{2,1,0:T(4,128)S(1)} %add.123), channel_id=1, source_target_pairs={{0,128},{64,192},{128,0},{192,64},{1,129},{65,193},{129,1},{193,65... | collective-permute-start | bytes 98312 | tf_op jit(solution)/shard_map/ppermute | solution.py:65
  126.6 1.3 collective-permute-start.12
  128.5 6.7 %collective-permute-start.13 = (f32[8,128]{1,0:T(8,128)S(1)}, f32[8,128]{1,0:T(8,128)S(1)}, u32[]{:S(2)}, u32[]{:S(2)}) collective-permute-start(f32[8,128]{1,0:T(8,128)S(1)} %broadcast_add_fusion), channel_id=1, source_target_pairs={{0,2},{1,3},{2,0},{3,1},{4,6},{5,7},{6,4},{7,5},{8,10},{9,11},{10,... | collective-permute-start | bytes 12296 | tf_op jit(solution)/shard_map/ppermute | solution.py:65
  128.6 25.1 %collective-permute-start.3 = (bf16[8,2,24,256]{3,0,2,1:T(8,128)(2,1)S(1)}, bf16[8,2,24,256]{3,0,2,1:T(8,128)(2,1)S(1)}, u32[]{:S(2)}, u32[]{:S(2)}) collective-permute-start(bf16[8,2,24,256]{3,0,2,1:T(8,128)(2,1)S(1)} %get-tuple-element.24), channel_id=1, source_target_pairs={{1,0},{2,1},{3,2},{4,3},{5,4},{6,5},{7,6},{8,7},{9,8},{10,9},{11,1... | collective-permute-start | bytes 589832 | tf_op jit(solution)/shard_map/ppermute | solution.py:79
  133.3 20.4 %collective-permute-start.2 = (bf16[8,2,24,256]{3,0,2,1:T(8,128)(2,1)S(1)}, bf16[8,2,24,256]{3,0,2,1:T(8,128)(2,1)S(1)}, u32[]{:S(2)}, u32[]{:S(2)}) collective-permute-start(bf16[8,2,24,256]{3,0,2,1:T(8,128)(2,1)S(1)} %get-tuple-element.23), channel_id=1, source_target_pairs={{0,1},{1,2},{2,3},{3,4},{4,5},{5,6},{6,7},{7,8},{8,9},{9,10},{10,1... | collective-permute-start | bytes 589832 | tf_op jit(solution)/shard_map/ppermute | solution.py:77
  135.9 4.6 %collective-permute-start.14 = (f32[8,128]{1,0:T(8,128)S(1)}, f32[8,128]{1,0:T(8,128)S(1)}, u32[]{:S(2)}, u32[]{:S(2)}) collective-permute-start(f32[8,128]{1,0:T(8,128)S(1)} %fusion.48), channel_id=1, source_target_pairs={{0,4},{1,5},{2,6},{3,7},{4,0},{5,1},{6,2},{7,3},{8,12},{9,13},{10,... | collective-permute-start | bytes 12296 | tf_op jit(solution)/shard_map/ppermute | solution.py:65
  140.5 7.5 %collective-permute-start.15 = (f32[8,128]{1,0:T(8,128)S(1)}, f32[8,128]{1,0:T(8,128)S(1)}, u32[]{:S(2)}, u32[]{:S(2)}) collective-permute-start(f32[8,128]{1,0:T(8,128)S(1)} %add.127), channel_id=1, source_target_pairs={{0,8},{1,9},{2,10},{3,11},{4,12},{5,13},{6,14},{7,15},{8,0},{9,1},... | collective-permute-start | bytes 12296 | tf_op jit(solution)/shard_map/ppermute | solution.py:65
  148.0 3.6 %collective-permute-start.16 = (f32[8,128]{1,0:T(8,128)S(1)}, f32[8,128]{1,0:T(8,128)S(1)}, u32[]{:S(2)}, u32[]{:S(2)}) collective-permute-start(f32[8,128]{1,0:T(8,128)S(1)} %add.128), channel_id=1, source_target_pairs={{0,16},{1,17},{2,18},{3,19},{4,20},{5,21},{6,22},{7,23},{8,24},{9,... | collective-permute-start | bytes 12296 | tf_op jit(solution)/shard_map/ppermute | solution.py:65
  151.6 5.1 %collective-permute-start.17 = (f32[8,128]{1,0:T(8,128)S(1)}, f32[8,128]{1,0:T(8,128)S(1)}, u32[]{:S(2)}, u32[]{:S(2)}) collective-permute-start(f32[8,128]{1,0:T(8,128)S(1)} %add.129), channel_id=1, source_target_pairs={{0,32},{1,33},{2,34},{3,35},{4,36},{5,37},{6,38},{7,39},{8,40},{9,... | collective-permute-start | bytes 12296 | tf_op jit(solution)/shard_map/ppermute | solution.py:65

commit v6 on v5

--- a/solution.py
+++ b/solution.py
@@ -57,6 +57,16 @@
         pairs = [(i, i ^ (1 << (twin if i & 1 else bit))) for i in range(count)]
         x = keep + lax.ppermute(send, axis, pairs)
     return x.reshape(rest)
+
+
+def gather_sum(x, axis):
+    count = lax.axis_size(axis)
+    copies = jnp.broadcast_to(x[None], (count,) + x.shape)
+    held = lax.all_to_all(copies, axis, 0, 0, tiled=True)
+    total = held[0]
+    for i in range(1, count):
+        total = total + held[i]
+    return total
 
 
 def doubling_sum(x, axis, bit_order):
@@ -253,9 +263,9 @@
     share_rows = channels // tiles
     pieces = raw_all.reshape(2, tiles, share_rows, 4 * channels).transpose(1, 0, 2, 3)
     share_all = halving_sum(pieces, "tile", tile_bit_order(tiles), tile_twins(tiles))
-    share_all = doubling_sum(share_all, "agent", list(range(axis_bits("agent"))))
-    square_sum = jnp.broadcast_to(jnp.sum(share_all * share_all), (8, 128))
-    square_sum = doubling_sum(square_sum, "tile", list(range(axis_bits("tile"))))[0, 0]
+    share_all = gather_sum(share_all, "agent")
+    square_sum = jnp.sum(share_all * share_all).reshape(1, 1)
+    square_sum = gather_sum(jnp.broadcast_to(square_sum, (1, 128)), "tile")[0, 0]
     factor = norm_limit / jnp.maximum(jnp.sqrt(square_sum), norm_limit)
     scaled = share_all * factor
     return (d_feats, scaled[..., : 3 * channels], scaled[..., 3 * channels :])

time: 160 us -> 146 us (0.912); the launches traced: 159 us -> 143 us
  waiting for transfers between devices: 66.1 us -> 52.4 us
  matrix products: 8.82 us -> 7.18 us
    ppermute x8 -> x0, waiting for transfers between devices: 19.7 us -> none  [doubling_sum(): x = x + lax.ppermute(x, axis, xor_pairs(count, bit))]
    all_to_all x0 -> x2, starting transfers between devices: none -> 11.1 us  [gather_sum(): held = lax.all_to_all(copies, axis, 0, 0, tiled=True)]
    ppermute x8 -> x0, starting transfers between devices: 8.04 us -> none  [doubling_sum(): x = x + lax.ppermute(x, axis, xor_pairs(count, bit))]
    all_to_all x0 -> x2, waiting for transfers between devices: none -> 7.57 us  [gather_sum(): held = lax.all_to_all(copies, axis, 0, 0, tiled=True)]
    ppermute x6, waiting for transfers between devices: 30.6 us -> 24.1 us  [halving_sum(): x = keep + lax.ppermute(send, axis, pairs)]
    all_to_all x1, waiting for transfers between devices: 0.01 us -> 5.01 us  [body(): lax.all_to_all(d_part, 'agent', split_axis=0, concat_axis=1, tiled=True)]
    slice x2 -> x0, local copies, waits for them, and re-layouts: 2.79 us -> none  [the longest x1 2.27 us: halving_sum(): high = lax.index_in_dim(x, 1, dim, keepdims=True)]
    ppermute x2, starting transfers between devices: 11.8 us -> 9.1 us  [with_halo(): lax.ppermute(head, axis, [((i + 1) % count, i) for i in range(ends)])]
  transfers between devices with their start and end apart: 20 -> 14, of which waited for: 15 -> 11; matrix products, arithmetic and copies ran while one was open for 6% -> 6% of each run, Pallas kernels for 0% -> 0%
where the time goes in v6:
time: 146 us; the launch traced here: 143 us
  waiting for transfers between devices  52.4 us (36%)
  starting transfers between devices  37.6 us (26%)
  Pallas kernels  19.5 us (13%)
  local copies, waits for them, and re-layouts  13.3 us (9%)
  other arithmetic  12.1 us (8%)
  matrix products  7.18 us (5%)
    ppermute x6, waiting for transfers between devices, halving_sum(): x = keep + lax.ppermute(send, axis, pairs)  24.1 us
    pallas_call x1, Pallas kernels, cell_attention(): pl.pallas_call(functools.partial(attention_kernel, block_size), grid=(cel...  19.5 us
    all_to_all x2, starting transfers between devices, gather_sum(): held = lax.all_to_all(copies, axis, 0, 0, tiled=True)  11.1 us
    ppermute x2, starting transfers between devices, with_halo(): lax.ppermute(head, axis, [((i + 1) % count, i) for i in range(ends)])  9.1 us
    all_to_all x1, waiting for transfers between devices, body(): lax.all_to_all(jnp.concatenate([flat_feats, flat_grads], axis=-1), 'agent...  8.94 us
    all_to_all x2, waiting for transfers between devices, gather_sum(): held = lax.all_to_all(copies, axis, 0, 0, tiled=True)  7.57 us
    ppermute x2, waiting for transfers between devices, with_halo(): lax.ppermute(tail, axis, [(i, (i + 1) % count) for i in range(ends)])  5.93 us
    ppermute x6, starting transfers between devices, halving_sum(): x = keep + lax.ppermute(send, axis, pairs)  5.2 us
  transfers between devices with their start and end apart: 14, of which 11 were waited for; matrix products, arithmetic and copies ran while one was open for 6% of the time, Pallas kernels for 0%

profile of v6, /device:TPU:2, one launch (start us, length us, event | category | flops | bytes accessed | tf_op | source)
XLA Modules:
  0.0 143.4 jit_solution(13102668068001162707)
XLA Ops:
  0.7 1.3 copy.49
  2.0 7.2 %collective-permute-start.1 = (bf16[8,2,24,256]{3,0,2,1:T(8,128)(2,1)S(1)}, bf16[8,2,24,256]{3,0,2,1:T(8,128)(2,1)S(1)}, u32[]{:S(2)}, u32[]{:S(2)}) collective-permute-start(bf16[8,2,24,256]{3,0,2,1:T(8,128)(2,1)S(1)} %get-tuple-element.24), channel_id=1, source_target_pairs={{1,0},{2,1},{3,2},{4,3},{5,4},{6,5},{7,6},{8,7},{9,8},{10,9},{11,1... | collective-permute-start | bytes 589832 | tf_op jit(solution)/shard_map/ppermute | solution.py:89
  9.2 1.9 %collective-permute-start = (bf16[8,2,24,256]{3,0,2,1:T(8,128)(2,1)S(1)}, bf16[8,2,24,256]{3,0,2,1:T(8,128)(2,1)S(1)}, u32[]{:S(2)}, u32[]{:S(2)}) collective-permute-start(bf16[8,2,24,256]{3,0,2,1:T(8,128)(2,1)S(1)} %get-tuple-element.23), channel_id=1, source_target_pairs={{0,1},{1,2},{2,3},{3,4},{4,5},{5,6},{6,7},{7,8},{8,9},{9,10},{10,1... | collective-permute-start | bytes 589832 | tf_op jit(solution)/shard_map/ppermute | solution.py:87
  11.1 0.2 copy.52
  11.4 0.1 constant_dynamic-slice_fusion
  11.5 0.9 collective-permute-done.1
  12.4 5.9 %collective-permute-done = bf16[8,2,24,256]{3,0,2,1:T(8,128)(2,1)S(1)} collective-permute-done((bf16[8,2,24,256]{3,0,2,1:T(8,128)(2,1)S(1)}, bf16[8,2,24,256]{3,0,2,1:T(8,128)(2,1)S(1)}, u32[]{:S(2)}, u32[]{:S(2)}) %collective-permute-start) | collective-permute-done | bytes 196640 | tf_op jit(solution)/shard_map/ppermute | solution.py:87
  18.4 1.7 %gather_fusion = bf16[8,4,24,256]{3,0,2,1:T(8,128)(2,1)S(1)} fusion(bf16[8,8,28,256]{3,0,2,1:T(8,128)(2,1)S(1)} %fusion.18, s32[8]{0:T(128)S(1)} %get-tuple-element.26), kind=kCustom, calls=%fused_computation | custom fusion | bytes 786560 | tf_op jit(solution)/shard_map/vmap()/gather | solution.py:104
  20.1 1.0 pad_maximum_fusion.1
  21.1 4.5 %all-to-all-start = ((bf16[8,96,512]{2,0,1:T(8,128)(2,1)}), bf16[8,96,512]{2,0,1:T(8,128)(2,1)S(1)}, u32[]{:S(2)}, u32[]{:S(2)}) async-start(bf16[8,96,512]{2,0,1:T(8,128)(2,1)} %pad_maximum_fusion.1), calls=%async_computation | async-start | bytes 1572864 | tf_op jit(solution)/shard_map/all_to_all | solution.py:217
  25.6 0.5 fusion.37.valid_ref
  26.1 8.9 %all-to-all-done = bf16[8,96,512]{2,0,1:T(8,128)(2,1)S(1)} async-done(((bf16[8,96,512]{2,0,1:T(8,128)(2,1)}), bf16[8,96,512]{2,0,1:T(8,128)(2,1)S(1)}, u32[]{:S(2)}, u32[]{:S(2)}) %all-to-all-start) | async-done | bytes 786464 | tf_op jit(solution)/shard_map/all_to_all | solution.py:217
  35.0 0.1 copy.77
  35.2 0.8 convert_bitcast_fusion
  36.0 0.2 copy-done.2
  36.1 0.4 fusion.12
  36.5 1.2 fusion.13.qkv_ref
  37.7 0.8 fusion.29.da_ref
  38.6 19.5 %shard_map.94 = (bf16[24,32,256]{2,1,0:T(8,128)(2,1)}, bf16[2,24,32,768]{3,2,1,0:T(8,128)(2,1)}) custom-call(f32[1,32]{1,0:T(1,128)} %fusion.37.valid_ref, bf16[24,32,768]{2,1,0:T(8,128)(2,1)} %fusion.13.qkv_ref, bf16[24,32,256]{2,1,0:T(8,128)(2,1)} %fusion.29.da_ref), custom_call_target="tpu_custom_call" | custom-call | flops 2415919104 | bytes 4325376 | tf_op jit(solution)/shard_map/pallas_call | solution.py:177
  58.1 1.4 %convolution_bitcast_fusion = f32[2,256,256]{1,2,0:T(8,128)S(1)} fusion(pred[2,32]{1,0:T(4,128)(4,1)S(1)} %pad_add_fusion, bf16[24,32,256]{2,1,0:T(8,128)(2,1)} %get-tuple-element.6, bf16[32,24,512]{2,0,1:T(8,128)(2,1)S(1)} %bitcast.413), kind=kOutput, calls=%fused_computation.18 | convolution fusion | flops 201719808 | bytes 1311232 | tf_op jit(solution)/shard_map/tgac,gae->tce/dot_general | solution.py:242
  59.6 3.1 %fusion.7 = f32[2,2,256,768]{2,3,1,0:T(8,128)S(1)} fusion(bf16[2,24,32,768]{3,2,1,0:T(8,128)(2,1)} %get-tuple-element.5, pred[2,32]{1,0:T(4,128)(4,1)S(1)} %pad_add_fusion, bf16[24,32,256]{2,1,0:T(8,128)(2,1)S(1)} %slice_bitcast_fusion.7), kind=kOutput, calls=%fused_computation.11 | convolution fusion | flops 1208352768 | bytes 5898304 | tf_op jit(solution)/shard_map/tgac,sgae->stce/dot_general | solution.py:254
  62.7 0.2 fusion.11
  62.9 1.5 %pad_maximum_fusion = f32[2,256,1024]{1,2,0:T(8,128)} fusion(f32[2,256,256]{1,2,0:T(8,128)S(1)} %convolution_bitcast_fusion, f32[2,256,768]{1,2,0:T(8,128)S(1)} %fusion.11), kind=kLoop, calls=%fused_computation.9 | loop fusion | flops 524288 | bytes 4194304 | tf_op jit(solution)/shard_map/concatenate | solution.py:261
  64.4 2.9 %copy.60 = f32[2,256,1024]{2,0,1:T(2,128)S(1)} copy(f32[2,256,1024]{1,2,0:T(8,128)} %pad_maximum_fusion) | data formatting | bytes 4194304 | tf_op jit(solution)/shard_map/concatenate | solution.py:261
  67.3 1.6 %broadcast_select_fusion = f32[2,2,2,2,2,1,2,4,1024]{8,6,7,5,4,3,2,1,0:T(2,128)} fusion(pred[]{:T(512)S(6)} %eq.48, f32[2,2,2,2,2,2,2,4,1024]{8,6,7,5,4,3,2,1,0:T(2,128)S(1)} %bitcast.408), kind=kLoop, calls=%fused_computation.24 | loop fusion | flops 262144 | bytes 3145729 | tf_op jit(solution)/shard_map/jit(_where)/select_n | solution.py:56
  68.9 3.0 %collective-permute-done.4 = f32[2,2,2,2,2,1,2,4,1024]{8,6,7,5,4,3,2,1,0:T(2,128)} collective-permute-done((f32[2,2,2,2,2,1,2,4,1024]{8,6,7,5,4,3,2,1,0:T(2,128)}, f32[2,2,2,2,2,1,2,4,1024]{8,6,7,5,4,3,2,1,0:T(2,128)}, u32[]{:S(2)}, u32[]{:S(2)}) %collective-permute-start.4) | collective-permute-done | bytes 1048608 | tf_op jit(solution)/shard_map/ppermute | solution.py:58
  71.9 2.2 %select_add_fusion = f32[2,2,2,2,2,1,2,4,1024]{8,6,7,5,4,3,2,1,0:T(2,128)S(1)} fusion(f32[2,2,2,2,2,1,2,4,1024]{8,6,7,5,4,3,2,1,0:T(2,128)} %collective-permute-done.4, pred[]{:T(512)S(6)} %eq.48, f32[2,2,2,2,2,2,2,4,1024]{8,6,7,5,4,3,2,1,0:T(2,128)S(1)} %bitcast.409), kind=kLoop, calls=%fused_computation.23 | loop fusion | flops 524288 | bytes 4194305 | tf_op jit(solution)/shard_map/add | solution.py:58
  74.1 0.5 bitcast_select_fusion
  74.7 0.3 broadcast_select_fusion.1
  75.0 0.1 collective-permute-start.5
  75.1 9.1 %collective-permute-done.5 = f32[2,2,2,2,1,1,2,4,1024]{8,6,7,5,4,3,2,1,0:T(2,128)S(1)} collective-permute-done((f32[2,2,2,2,1,1,2,4,1024]{8,6,7,5,4,3,2,1,0:T(2,128)S(1)}, f32[2,2,2,2,1,1,2,4,1024]{8,6,7,5,4,3,2,1,0:T(2,128)S(1)}, u32[]{:S(2)}, u32[]{:S(2)}) %collective-permute-start.5) | collective-permute-done | bytes 524320 | tf_op jit(solution)/shard_map/ppermute | solution.py:58
  84.3 0.4 select_add_fusion.1
  84.7 0.1 broadcast_select_fusion.2
  84.8 0.3 collective-permute-start.6
  85.1 1.4 fusion.4
  86.5 4.9 %collective-permute-done.6 = f32[2,1,2,2,1,1,2,4,1024]{8,6,7,5,4,3,2,1,0:T(2,128)S(1)} collective-permute-done((f32[2,1,2,2,1,1,2,4,1024]{8,6,7,5,4,3,2,1,0:T(2,128)S(1)}, f32[2,1,2,2,1,1,2,4,1024]{8,6,7,5,4,3,2,1,0:T(2,128)S(1)}, u32[]{:S(2)}, u32[]{:S(2)}) %collective-permute-start.6) | collective-permute-done | bytes 262176 | tf_op jit(solution)/shard_map/ppermute | solution.py:58
  91.5 0.2 select_add_fusion.2
  91.7 0.1 broadcast_select_fusion.3
  91.7 0.1 collective-permute-start.7
  91.8 0.3 slice_add_fusion.1
  92.1 6.4 %collective-permute-done.7 = f32[2,1,2,1,1,1,2,4,1024]{8,6,7,5,4,3,2,1,0:T(2,128)S(1)} collective-permute-done((f32[2,1,2,1,1,1,2,4,1024]{8,6,7,5,4,3,2,1,0:T(2,128)S(1)}, f32[2,1,2,1,1,1,2,4,1024]{8,6,7,5,4,3,2,1,0:T(2,128)S(1)}, u32[]{:S(2)}, u32[]{:S(2)}) %collective-permute-start.7) | collective-permute-done | bytes 131104 | tf_op jit(solution)/shard_map/ppermute | solution.py:58
  98.5 0.1 select_add_fusion.3
  98.7 2.5 %collective-permute-start.8 = (f32[1,1,2,1,1,1,2,4,1024]{8,6,7,5,4,3,2,1,0:T(2,128)S(1)}, f32[1,1,2,1,1,1,2,4,1024]{8,6,7,5,4,3,2,1,0:T(2,128)S(1)}, u32[]{:S(2)}, u32[]{:S(2)}) collective-permute-start(f32[1,1,2,1,1,1,2,4,1024]{8,6,7,5,4,3,2,1,0:T(2,128)S(1)} %broadcast_select_fusion.4), channel_id=1, source_target_pairs={{0,32},{1,5},{2,34},{3,7},{4,36},{5,1},{6,38},{7,3},{8,40},{9,13},... | collective-permute-start | bytes 196616 | tf_op jit(solution)/shard_map/ppermute | solution.py:58
  101.2 0.1 fusion.28
  101.3 1.0 copy.58
  102.3 3.5 %all-to-all-start.1 = ((bf16[32,24,256]{2,1,0:T(8,128)(2,1)}), bf16[32,24,256]{2,1,0:T(8,128)(2,1)S(1)}, u32[]{:S(2)}, u32[]{:S(2)}) async-start(bf16[32,24,256]{2,1,0:T(8,128)(2,1)} %copy.58), calls=%async_computation.1 | async-start | bytes 786432 | tf_op jit(solution)/shard_map/all_to_all | solution.py:251
  105.8 2.2 %collective-permute-start.9 = (f32[1,1,1,1,1,1,2,4,1024]{8,6,7,5,4,3,2,1,0:T(2,128)S(1)}, f32[1,1,1,1,1,1,2,4,1024]{8,6,7,5,4,3,2,1,0:T(2,128)S(1)}, u32[]{:S(2)}, u32[]{:S(2)}) collective-permute-start(f32[1,1,1,1,1,1,2,4,1024]{8,6,7,5,4,3,2,1,0:T(2,128)S(1)} %broadcast_select_fusion.5), channel_id=1, source_target_pairs={{0,8},{1,9},{2,10},{3,11},{4,12},{5,13},{6,14},{7,15},{8,0},{9,1},... | collective-permute-start | bytes 98312 | tf_op jit(solution)/shard_map/ppermute | solution.py:58
  108.1 5.0 %all-to-all-done.1 = bf16[32,24,256]{2,1,0:T(8,128)(2,1)S(1)} async-done(((bf16[32,24,256]{2,1,0:T(8,128)(2,1)}), bf16[32,24,256]{2,1,0:T(8,128)(2,1)S(1)}, u32[]{:S(2)}, u32[]{:S(2)}) %all-to-all-start.1) | async-done | bytes 393248 | tf_op jit(solution)/shard_map/all_to_all | solution.py:251
  113.1 0.1 copy.78
  113.1 0.6 collective-permute-done.9
  113.8 0.7 broadcast_in_dim.73
  114.5 4.7 %all-to-all-start.2 = ((f32[4,2,4,1024]{3,2,1,0:T(4,128)}), f32[4,2,4,1024]{3,2,1,0:T(4,128)S(1)}, u32[]{:S(2)}, u32[]{:S(2)}) async-start(f32[4,2,4,1024]{3,2,1,0:T(4,128)} %broadcast_in_dim.73), calls=%async_computation.2 | async-start | bytes 262144 | tf_op jit(solution)/shard_map/all_to_all | solution.py:65
  119.2 1.9 %collective-permute-start.3 = (bf16[8,2,24,256]{3,0,2,1:T(8,128)(2,1)S(1)}, bf16[8,2,24,256]{3,0,2,1:T(8,128)(2,1)S(1)}, u32[]{:S(2)}, u32[]{:S(2)}) collective-permute-start(bf16[8,2,24,256]{3,0,2,1:T(8,128)(2,1)S(1)} %get-tuple-element.22), channel_id=1, source_target_pairs={{1,0},{2,1},{3,2},{4,3},{5,4},{6,5},{7,6},{8,7},{9,8},{10,9},{11,1... | collective-permute-start | bytes 589832 | tf_op jit(solution)/shard_map/ppermute | solution.py:89
  121.2 2.4 %collective-permute-start.2 = (bf16[8,2,24,256]{3,0,2,1:T(8,128)(2,1)S(1)}, bf16[8,2,24,256]{3,0,2,1:T(8,128)(2,1)S(1)}, u32[]{:S(2)}, u32[]{:S(2)}) collective-permute-start(bf16[8,2,24,256]{3,0,2,1:T(8,128)(2,1)S(1)} %get-tuple-element.21), channel_id=1, source_target_pairs={{0,1},{1,2},{2,3},{3,4},{4,5},{5,6},{6,7},{7,8},{8,9},{9,10},{10,1... | collective-permute-start | bytes 589832 | tf_op jit(solution)/shard_map/ppermute | solution.py:87
  123.6 1.6 %all-to-all-done.2 = f32[4,2,4,1024]{3,2,1,0:T(4,128)S(1)} async-done(((f32[4,2,4,1024]{3,2,1,0:T(4,128)}), f32[4,2,4,1024]{3,2,1,0:T(4,128)S(1)}, u32[]{:S(2)}, u32[]{:S(2)}) %all-to-all-start.2) | async-done | bytes 131104 | tf_op jit(solution)/shard_map/all_to_all | solution.py:65
  125.2 0.6 multiply_reduce_fusion
  125.8 1.3 broadcast_in_dim_broadcast_in_dim_broadcast_in_dim.2
  127.1 6.3 %all-to-all-start.3 = ((f32[64,1,128]{2,1,0:T(1,128)}), f32[64,1,128]{2,1,0:T(1,128)S(1)}, u32[]{:S(2)}, u32[]{:S(2)}) async-start(f32[64,1,128]{2,1,0:T(1,128)} %broadcast_in_dim_broadcast_in_dim_broadcast_in_dim.2), calls=%async_computation.3 | async-start | bytes 65536 | tf_op jit(solution)/shard_map/all_to_all | solution.py:65
  133.5 1.7 %gather_fusion.1 = bf16[8,4,24,256]{3,0,2,1:T(8,128)(2,1)S(1)} fusion(bf16[8,8,28,256]{3,0,2,1:T(8,128)(2,1)S(1)} %select_maximum_fusion, s32[8]{0:T(128)S(1)} %get-tuple-element.25), kind=kCustom, calls=%fused_computation.1 | custom fusion | bytes 786560 | tf_op jit(solution)/shard_map/vmap()/gather | solution.py:104
  135.2 0.8 copy.63
  136.0 6.0 %all-to-all-done.3 = f32[64,1,128]{2,1,0:T(1,128)S(1)} async-done(((f32[64,1,128]{2,1,0:T(1,128)}), f32[64,1,128]{2,1,0:T(1,128)S(1)}, u32[]{:S(2)}, u32[]{:S(2)}) %all-to-all-start.3) | async-done | bytes 32800 | tf_op jit(solution)/shard_map/all_to_all | solution.py:65
  142.0 0.1 fusion.42
  142.2 0.6 slice.512
  142.8 0.6 slice.513
  (31 shorter events, 0.5 us)
Async XLA Ops:
  0.6 34.5 %copy-start = (bf16[2,256,768]{2,1,0:T(8,128)(2,1)S(1)}, bf16[2,256,768]{2,1,0:T(8,128)(2,1)}, u32[]{:S(2)}) copy-start(bf16[2,256,768]{2,1,0:T(8,128)(2,1)} %param.11) | copy-start | bytes 2359300
  0.6 10.5 %copy-start.1 = (bf16[8,4,24,256]{3,2,1,0:T(8,128)(2,1)S(1)}, bf16[8,4,24,256]{3,2,1,0:T(8,128)(2,1)}, u32[]{:S(2)}) copy-start(bf16[8,4,24,256]{3,2,1,0:T(8,128)(2,1)} %param.13) | copy-start | bytes 1179652
  0.7 10.7 %copy-start.3 = (s32[32,2]{0,1:T(2,128)S(1)}, s32[32,2]{0,1:T(2,128)}, u32[]{:S(2)}) copy-start(s32[32,2]{0,1:T(2,128)} %param.10) | copy-start | bytes 772
  2.0 10.3 %collective-permute-start.1 = (bf16[8,2,24,256]{3,0,2,1:T(8,128)(2,1)S(1)}, bf16[8,2,24,256]{3,0,2,1:T(8,128)(2,1)S(1)}, u32[]{:S(2)}, u32[]{:S(2)}) collective-permute-start(bf16[8,2,24,256]{3,0,2,1:T(8,128)(2,1)S(1)} %get-tuple-element.24), channel_id=1, source_target_pairs={{1,0},{2,1},{3,2},{4,3},{5,4},{6,5},{7,6},{8,7},{9,8},{10,9},{11,1... | collective-permute-start | bytes 589832 | tf_op jit(solution)/shard_map/ppermute | solution.py:89
  9.2 9.1 %collective-permute-start = (bf16[8,2,24,256]{3,0,2,1:T(8,128)(2,1)S(1)}, bf16[8,2,24,256]{3,0,2,1:T(8,128)(2,1)S(1)}, u32[]{:S(2)}, u32[]{:S(2)}) collective-permute-start(bf16[8,2,24,256]{3,0,2,1:T(8,128)(2,1)S(1)} %get-tuple-element.23), channel_id=1, source_target_pairs={{0,1},{1,2},{2,3},{3,4},{4,5},{5,6},{6,7},{7,8},{8,9},{9,10},{10,1... | collective-permute-start | bytes 589832 | tf_op jit(solution)/shard_map/ppermute | solution.py:87
  20.1 5.4 %copy-start.4 = (s32[32]{0:T(128)S(1)}, s32[32]{0:T(128)}, u32[]{:S(2)}) copy-start(s32[32]{0:T(128)} %param.8) | copy-start | bytes 388
  20.1 5.5 %copy-start.5 = (s32[32]{0:T(128)S(1)}, s32[32]{0:T(128)}, u32[]{:S(2)}) copy-start(s32[32]{0:T(128)} %param.9) | copy-start | bytes 388
  21.1 14.0 %all-to-all-start = ((bf16[8,96,512]{2,0,1:T(8,128)(2,1)}), bf16[8,96,512]{2,0,1:T(8,128)(2,1)S(1)}, u32[]{:S(2)}, u32[]{:S(2)}) async-start(bf16[8,96,512]{2,0,1:T(8,128)(2,1)} %pad_maximum_fusion.1), calls=%async_computation | async-start | bytes 1572864 | tf_op jit(solution)/shard_map/all_to_all | solution.py:217
  35.2 1.0 copy-start.2
  68.9 3.0 %collective-permute-start.4 = (f32[2,2,2,2,2,1,2,4,1024]{8,6,7,5,4,3,2,1,0:T(2,128)}, f32[2,2,2,2,2,1,2,4,1024]{8,6,7,5,4,3,2,1,0:T(2,128)}, u32[]{:S(2)}, u32[]{:S(2)}) collective-permute-start(f32[2,2,2,2,2,1,2,4,1024]{8,6,7,5,4,3,2,1,0:T(2,128)} %broadcast_select_fusion), channel_id=1, source_target_pairs={{0,1},{1,0},{2,3},{3,2},{4,5},{5,4},{6,7},{7,6},{8,9},{9,8},{10,11... | collective-permute-start | bytes 3145736 | tf_op jit(solution)/shard_map/ppermute | solution.py:58
  75.0 9.3 %collective-permute-start.5 = (f32[2,2,2,2,1,1,2,4,1024]{8,6,7,5,4,3,2,1,0:T(2,128)S(1)}, f32[2,2,2,2,1,1,2,4,1024]{8,6,7,5,4,3,2,1,0:T(2,128)S(1)}, u32[]{:S(2)}, u32[]{:S(2)}) collective-permute-start(f32[2,2,2,2,1,1,2,4,1024]{8,6,7,5,4,3,2,1,0:T(2,128)S(1)} %broadcast_select_fusion.1), channel_id=1, source_target_pairs={{0,2},{1,17},{2,0},{3,19},{4,6},{5,21},{6,4},{7,23},{8,10},{9,25},... | collective-permute-start | bytes 1572872 | tf_op jit(solution)/shard_map/ppermute | solution.py:58
  75.1 10.0 %copy-start.6 = (bf16[2,24,32,768]{3,2,1,0:T(8,128)(2,1)S(1)}, bf16[2,24,32,768]{3,2,1,0:T(8,128)(2,1)}, u32[]{:S(2)}) copy-start(bf16[2,24,32,768]{3,2,1,0:T(8,128)(2,1)} %get-tuple-element.5) | copy-start | bytes 7077892
  84.8 6.6 %collective-permute-start.6 = (f32[2,1,2,2,1,1,2,4,1024]{8,6,7,5,4,3,2,1,0:T(2,128)S(1)}, f32[2,1,2,2,1,1,2,4,1024]{8,6,7,5,4,3,2,1,0:T(2,128)S(1)}, u32[]{:S(2)}, u32[]{:S(2)}) collective-permute-start(f32[2,1,2,2,1,1,2,4,1024]{8,6,7,5,4,3,2,1,0:T(2,128)S(1)} %broadcast_select_fusion.2), channel_id=1, source_target_pairs={{0,16},{1,3},{2,18},{3,1},{4,20},{5,7},{6,22},{7,5},{8,24},{9,11},... | collective-permute-start | bytes 786440 | tf_op jit(solution)/shard_map/ppermute | solution.py:58
  91.7 6.8 %collective-permute-start.7 = (f32[2,1,2,1,1,1,2,4,1024]{8,6,7,5,4,3,2,1,0:T(2,128)S(1)}, f32[2,1,2,1,1,1,2,4,1024]{8,6,7,5,4,3,2,1,0:T(2,128)S(1)}, u32[]{:S(2)}, u32[]{:S(2)}) collective-permute-start(f32[2,1,2,1,1,1,2,4,1024]{8,6,7,5,4,3,2,1,0:T(2,128)S(1)} %broadcast_select_fusion.3), channel_id=1, source_target_pairs={{0,4},{1,33},{2,6},{3,35},{4,0},{5,37},{6,2},{7,39},{8,12},{9,41},... | collective-permute-start | bytes 393224 | tf_op jit(solution)/shard_map/ppermute | solution.py:58
  98.7 7.0 %collective-permute-start.8 = (f32[1,1,2,1,1,1,2,4,1024]{8,6,7,5,4,3,2,1,0:T(2,128)S(1)}, f32[1,1,2,1,1,1,2,4,1024]{8,6,7,5,4,3,2,1,0:T(2,128)S(1)}, u32[]{:S(2)}, u32[]{:S(2)}) collective-permute-start(f32[1,1,2,1,1,1,2,4,1024]{8,6,7,5,4,3,2,1,0:T(2,128)S(1)} %broadcast_select_fusion.4), channel_id=1, source_target_pairs={{0,32},{1,5},{2,34},{3,7},{4,36},{5,1},{6,38},{7,3},{8,40},{9,13},... | collective-permute-start | bytes 196616 | tf_op jit(solution)/shard_map/ppermute | solution.py:58
  102.3 10.8 %all-to-all-start.1 = ((bf16[32,24,256]{2,1,0:T(8,128)(2,1)}), bf16[32,24,256]{2,1,0:T(8,128)(2,1)S(1)}, u32[]{:S(2)}, u32[]{:S(2)}) async-start(bf16[32,24,256]{2,1,0:T(8,128)(2,1)} %copy.58), calls=%async_computation.1 | async-start | bytes 786432 | tf_op jit(solution)/shard_map/all_to_all | solution.py:251
  105.8 7.9 %collective-permute-start.9 = (f32[1,1,1,1,1,1,2,4,1024]{8,6,7,5,4,3,2,1,0:T(2,128)S(1)}, f32[1,1,1,1,1,1,2,4,1024]{8,6,7,5,4,3,2,1,0:T(2,128)S(1)}, u32[]{:S(2)}, u32[]{:S(2)}) collective-permute-start(f32[1,1,1,1,1,1,2,4,1024]{8,6,7,5,4,3,2,1,0:T(2,128)S(1)} %broadcast_select_fusion.5), channel_id=1, source_target_pairs={{0,8},{1,9},{2,10},{3,11},{4,12},{5,13},{6,14},{7,15},{8,0},{9,1},... | collective-permute-start | bytes 98312 | tf_op jit(solution)/shard_map/ppermute | solution.py:58
  114.5 10.7 %all-to-all-start.2 = ((f32[4,2,4,1024]{3,2,1,0:T(4,128)}), f32[4,2,4,1024]{3,2,1,0:T(4,128)S(1)}, u32[]{:S(2)}, u32[]{:S(2)}) async-start(f32[4,2,4,1024]{3,2,1,0:T(4,128)} %broadcast_in_dim.73), calls=%async_computation.2 | async-start | bytes 262144 | tf_op jit(solution)/shard_map/all_to_all | solution.py:65
  119.2 14.2 %collective-permute-start.3 = (bf16[8,2,24,256]{3,0,2,1:T(8,128)(2,1)S(1)}, bf16[8,2,24,256]{3,0,2,1:T(8,128)(2,1)S(1)}, u32[]{:S(2)}, u32[]{:S(2)}) collective-permute-start(bf16[8,2,24,256]{3,0,2,1:T(8,128)(2,1)S(1)} %get-tuple-element.22), channel_id=1, source_target_pairs={{1,0},{2,1},{3,2},{4,3},{5,4},{6,5},{7,6},{8,7},{9,8},{10,9},{11,1... | collective-permute-start | bytes 589832 | tf_op jit(solution)/shard_map/ppermute | solution.py:89
  121.2 12.3 %collective-permute-start.2 = (bf16[8,2,24,256]{3,0,2,1:T(8,128)(2,1)S(1)}, bf16[8,2,24,256]{3,0,2,1:T(8,128)(2,1)S(1)}, u32[]{:S(2)}, u32[]{:S(2)}) collective-permute-start(bf16[8,2,24,256]{3,0,2,1:T(8,128)(2,1)S(1)} %get-tuple-element.21), channel_id=1, source_target_pairs={{0,1},{1,2},{2,3},{3,4},{4,5},{5,6},{6,7},{7,8},{8,9},{9,10},{10,1... | collective-permute-start | bytes 589832 | tf_op jit(solution)/shard_map/ppermute | solution.py:87
  127.1 14.9 %all-to-all-start.3 = ((f32[64,1,128]{2,1,0:T(1,128)}), f32[64,1,128]{2,1,0:T(1,128)S(1)}, u32[]{:S(2)}, u32[]{:S(2)}) async-start(f32[64,1,128]{2,1,0:T(1,128)} %broadcast_in_dim_broadcast_in_dim_broadcast_in_dim.2), calls=%async_computation.3 | async-start | bytes 65536 | tf_op jit(solution)/shard_map/all_to_all | solution.py:65

commit v7 on v6

--- a/solution.py
+++ b/solution.py
@@ -240,7 +240,7 @@
     attended, d_split = cell_attention(valid_row, qkv, d_attended, own_count)
     attended_typed = jnp.where(type_mask, attended[None], jnp.zeros((), bf16))
     raw_out = jnp.einsum(
-        "tgac,gae->tce", attended_typed, grads_cm, preferred_element_type=f32
+        "tgac,gae->cte", attended_typed, grads_cm, preferred_element_type=f32
     )
     d_part_terms = jnp.einsum(
         "sgae,tce->stgac", d_split, w_qkv, preferred_element_type=f32
@@ -252,7 +252,7 @@
     d_warped = returned.reshape(own_count, row_count, col_count, channels)
     feats_typed = jnp.where(type_mask, feats_cm[None], jnp.zeros((), bf16))
     qkv_terms = jnp.einsum(
-        "tgac,sgae->stce", feats_typed, d_split, preferred_element_type=f32
+        "tgac,sgae->scte", feats_typed, d_split, preferred_element_type=f32
     )
     raw_qkv = qkv_terms[0] + qkv_terms[1]
     rimmed_grad = with_halo(d_warped, (("tile", 1),), MAXOFF)
@@ -261,13 +261,14 @@
     raw_all = jnp.concatenate([raw_qkv, raw_out], axis=-1)
     tiles = lax.axis_size("tile")
     share_rows = channels // tiles
-    pieces = raw_all.reshape(2, tiles, share_rows, 4 * channels).transpose(1, 0, 2, 3)
+    pieces = raw_all.reshape(tiles, share_rows, 2, 4 * channels)
     share_all = halving_sum(pieces, "tile", tile_bit_order(tiles), tile_twins(tiles))
     share_all = gather_sum(share_all, "agent")
     square_sum = jnp.sum(share_all * share_all).reshape(1, 1)
     square_sum = gather_sum(jnp.broadcast_to(square_sum, (1, 128)), "tile")[0, 0]
     factor = norm_limit / jnp.maximum(jnp.sqrt(square_sum), norm_limit)
     scaled = share_all * factor
+    scaled = jnp.transpose(scaled, (1, 0, 2))
     return (d_feats, scaled[..., : 3 * channels], scaled[..., 3 * channels :])
 
 

time: 146 us -> 144 us (0.986)
  matrix products: 7.18 us -> 5.65 us
    dot_general x2, matrix products: 4.58 us -> 3.06 us  [the longest x1 1.58 us: body(): jnp.einsum('tgac,gae->cte', attended_typed, grads_cm, preferred_element_t...]
where the time goes in v7:
time: 144 us; the launch traced here: 142 us
  waiting for transfers between devices  52.4 us (36%)
  starting transfers between devices  37.6 us (26%)
  Pallas kernels  19.5 us (14%)
  local copies, waits for them, and re-layouts  13.5 us (9%)
  other arithmetic  12.1 us (8%)
  matrix products  5.65 us (4%)
    ppermute x6, waiting for transfers between devices, halving_sum(): x = keep + lax.ppermute(send, axis, pairs)  24.1 us
    pallas_call x1, Pallas kernels, cell_attention(): pl.pallas_call(functools.partial(attention_kernel, block_size), grid=(cel...  19.5 us
    all_to_all x2, starting transfers between devices, gather_sum(): held = lax.all_to_all(copies, axis, 0, 0, tiled=True)  11.1 us
    ppermute x2, starting transfers between devices, with_halo(): lax.ppermute(head, axis, [((i + 1) % count, i) for i in range(ends)])  9.1 us
    all_to_all x1, waiting for transfers between devices, body(): lax.all_to_all(jnp.concatenate([flat_feats, flat_grads], axis=-1), 'agent...  8.94 us
    all_to_all x2, waiting for transfers between devices, gather_sum(): held = lax.all_to_all(copies, axis, 0, 0, tiled=True)  7.58 us
    ppermute x2, waiting for transfers between devices, with_halo(): lax.ppermute(tail, axis, [(i, (i + 1) % count) for i in range(ends)])  5.93 us
    ppermute x6, starting transfers between devices, halving_sum(): x = keep + lax.ppermute(send, axis, pairs)  5.2 us
  transfers between devices with their start and end apart: 14, of which 11 were waited for; matrix products, arithmetic and copies ran while one was open for 6% of the time, Pallas kernels for 0%

profile of v7, /device:TPU:2, one launch (start us, length us, event | category | flops | bytes accessed | tf_op | source)
XLA Modules:
  0.0 142.1 jit_solution(7536121531750538014)
XLA Ops:
  0.7 1.3 copy.48
  2.0 7.2 %collective-permute-start.1 = (bf16[8,2,24,256]{3,0,2,1:T(8,128)(2,1)S(1)}, bf16[8,2,24,256]{3,0,2,1:T(8,128)(2,1)S(1)}, u32[]{:S(2)}, u32[]{:S(2)}) collective-permute-start(bf16[8,2,24,256]{3,0,2,1:T(8,128)(2,1)S(1)} %get-tuple-element.24), channel_id=1, source_target_pairs={{1,0},{2,1},{3,2},{4,3},{5,4},{6,5},{7,6},{8,7},{9,8},{10,9},{11,1... | collective-permute-start | bytes 589832 | tf_op jit(solution)/shard_map/ppermute | solution.py:89
  9.2 1.9 %collective-permute-start = (bf16[8,2,24,256]{3,0,2,1:T(8,128)(2,1)S(1)}, bf16[8,2,24,256]{3,0,2,1:T(8,128)(2,1)S(1)}, u32[]{:S(2)}, u32[]{:S(2)}) collective-permute-start(bf16[8,2,24,256]{3,0,2,1:T(8,128)(2,1)S(1)} %get-tuple-element.23), channel_id=1, source_target_pairs={{0,1},{1,2},{2,3},{3,4},{4,5},{5,6},{6,7},{7,8},{8,9},{9,10},{10,1... | collective-permute-start | bytes 589832 | tf_op jit(solution)/shard_map/ppermute | solution.py:87
  11.1 0.2 copy.51
  11.4 0.1 constant_dynamic-slice_fusion
  11.5 0.9 collective-permute-done.1
  12.4 5.9 %collective-permute-done = bf16[8,2,24,256]{3,0,2,1:T(8,128)(2,1)S(1)} collective-permute-done((bf16[8,2,24,256]{3,0,2,1:T(8,128)(2,1)S(1)}, bf16[8,2,24,256]{3,0,2,1:T(8,128)(2,1)S(1)}, u32[]{:S(2)}, u32[]{:S(2)}) %collective-permute-start) | collective-permute-done | bytes 196640 | tf_op jit(solution)/shard_map/ppermute | solution.py:87
  18.4 1.7 %gather_fusion = bf16[8,4,24,256]{3,0,2,1:T(8,128)(2,1)S(1)} fusion(bf16[8,8,28,256]{3,0,2,1:T(8,128)(2,1)S(1)} %fusion.18, s32[8]{0:T(128)S(1)} %get-tuple-element.26), kind=kCustom, calls=%fused_computation | custom fusion | bytes 786560 | tf_op jit(solution)/shard_map/vmap()/gather | solution.py:104
  20.1 1.0 pad_maximum_fusion.1
  21.1 4.5 %all-to-all-start = ((bf16[8,96,512]{2,0,1:T(8,128)(2,1)}), bf16[8,96,512]{2,0,1:T(8,128)(2,1)S(1)}, u32[]{:S(2)}, u32[]{:S(2)}) async-start(bf16[8,96,512]{2,0,1:T(8,128)(2,1)} %pad_maximum_fusion.1), calls=%async_computation | async-start | bytes 1572864 | tf_op jit(solution)/shard_map/all_to_all | solution.py:217
  25.6 0.5 fusion.37.valid_ref
  26.1 8.9 %all-to-all-done = bf16[8,96,512]{2,0,1:T(8,128)(2,1)S(1)} async-done(((bf16[8,96,512]{2,0,1:T(8,128)(2,1)}), bf16[8,96,512]{2,0,1:T(8,128)(2,1)S(1)}, u32[]{:S(2)}, u32[]{:S(2)}) %all-to-all-start) | async-done | bytes 786464 | tf_op jit(solution)/shard_map/all_to_all | solution.py:217
  35.0 0.1 copy.76
  35.2 0.8 convert_bitcast_fusion
  35.9 0.2 copy-done.2
  36.1 0.4 fusion.12
  36.5 1.2 fusion.13.qkv_ref
  37.7 0.8 fusion.29.da_ref
  38.5 19.5 %shard_map.94 = (bf16[24,32,256]{2,1,0:T(8,128)(2,1)}, bf16[2,24,32,768]{3,2,1,0:T(8,128)(2,1)}) custom-call(f32[1,32]{1,0:T(1,128)} %fusion.37.valid_ref, bf16[24,32,768]{2,1,0:T(8,128)(2,1)} %fusion.13.qkv_ref, bf16[24,32,256]{2,1,0:T(8,128)(2,1)} %fusion.29.da_ref), custom_call_target="tpu_custom_call" | custom-call | flops 2415919104 | bytes 4325376 | tf_op jit(solution)/shard_map/pallas_call | solution.py:177
  58.1 1.6 %convolution_bitcast_fusion = f32[256,2,256]{0,2,1:T(8,128)S(1)} fusion(pred[2,32]{1,0:T(4,128)(4,1)S(1)} %pad_add_fusion, bf16[24,32,256]{2,1,0:T(8,128)(2,1)} %get-tuple-element.6, bf16[32,24,512]{2,0,1:T(8,128)(2,1)S(1)} %bitcast.413), kind=kOutput, calls=%fused_computation.18 | convolution fusion | flops 201719808 | bytes 1311232 | tf_op jit(solution)/shard_map/tgac,gae->cte/dot_general | solution.py:242
  59.7 0.2 copy-done.6
  59.8 1.5 %fusion.7 = f32[2,256,2,768]{1,3,2,0:T(8,128)S(1)} fusion(bf16[2,24,32,768]{3,2,1,0:T(8,128)(2,1)S(1)} %copy-done.6, pred[2,32]{1,0:T(4,128)(4,1)S(1)} %pad_add_fusion, bf16[24,32,256]{2,1,0:T(8,128)(2,1)S(1)} %slice_bitcast_fusion.7), kind=kOutput, calls=%fused_computation.11 | convolution fusion | flops 1208352768 | bytes 5898304 | tf_op jit(solution)/shard_map/tgac,sgae->scte/dot_general | solution.py:254
  61.3 0.2 fusion.11
  61.5 1.5 %pad_maximum_fusion = f32[256,2,1024]{0,2,1:T(8,128)} fusion(f32[256,2,256]{0,2,1:T(8,128)S(1)} %convolution_bitcast_fusion, f32[256,2,768]{0,2,1:T(8,128)S(1)} %fusion.11), kind=kLoop, calls=%fused_computation.9 | loop fusion | flops 524288 | bytes 4194304 | tf_op jit(solution)/shard_map/concatenate | solution.py:261
  63.0 2.9 %copy.59 = f32[256,2,1024]{2,1,0:T(2,128)S(1)} copy(f32[256,2,1024]{0,2,1:T(8,128)} %pad_maximum_fusion) | data formatting | bytes 4194304 | tf_op jit(solution)/shard_map/concatenate | solution.py:261
  65.9 1.6 %broadcast_select_fusion = f32[2,2,2,2,2,1,4,2,1024]{8,7,6,5,4,3,2,1,0:T(2,128)} fusion(pred[]{:T(512)S(6)} %eq.48, f32[2,2,2,2,2,2,4,2,1024]{8,7,6,5,4,3,2,1,0:T(2,128)S(1)} %bitcast.408), kind=kLoop, calls=%fused_computation.24 | loop fusion | flops 262144 | bytes 3145729 | tf_op jit(solution)/shard_map/jit(_where)/select_n | solution.py:56
  67.5 3.0 %collective-permute-done.4 = f32[2,2,2,2,2,1,4,2,1024]{8,7,6,5,4,3,2,1,0:T(2,128)} collective-permute-done((f32[2,2,2,2,2,1,4,2,1024]{8,7,6,5,4,3,2,1,0:T(2,128)}, f32[2,2,2,2,2,1,4,2,1024]{8,7,6,5,4,3,2,1,0:T(2,128)}, u32[]{:S(2)}, u32[]{:S(2)}) %collective-permute-start.4) | collective-permute-done | bytes 1048608 | tf_op jit(solution)/shard_map/ppermute | solution.py:58
  70.5 2.2 %select_add_fusion = f32[2,2,2,2,2,1,4,2,1024]{8,7,6,5,4,3,2,1,0:T(2,128)S(1)} fusion(f32[2,2,2,2,2,1,4,2,1024]{8,7,6,5,4,3,2,1,0:T(2,128)} %collective-permute-done.4, pred[]{:T(512)S(6)} %eq.48, f32[2,2,2,2,2,2,4,2,1024]{8,7,6,5,4,3,2,1,0:T(2,128)S(1)} %bitcast.409), kind=kLoop, calls=%fused_computation.23 | loop fusion | flops 524288 | bytes 4194305 | tf_op jit(solution)/shard_map/add | solution.py:58
  72.8 0.5 bitcast_select_fusion
  73.3 0.3 broadcast_select_fusion.1
  73.7 0.1 collective-permute-start.5
  73.8 9.1 %collective-permute-done.5 = f32[2,2,2,2,1,1,4,2,1024]{8,7,6,5,4,3,2,1,0:T(2,128)S(1)} collective-permute-done((f32[2,2,2,2,1,1,4,2,1024]{8,7,6,5,4,3,2,1,0:T(2,128)S(1)}, f32[2,2,2,2,1,1,4,2,1024]{8,7,6,5,4,3,2,1,0:T(2,128)S(1)}, u32[]{:S(2)}, u32[]{:S(2)}) %collective-permute-start.5) | collective-permute-done | bytes 524320 | tf_op jit(solution)/shard_map/ppermute | solution.py:58
  82.9 0.4 select_add_fusion.1
  83.3 0.1 broadcast_select_fusion.2
  83.5 0.3 collective-permute-start.6
  83.8 1.4 %fusion.4 = f32[2,2,24,32,256]{4,3,2,1,0:T(8,128)S(1)} fusion(bf16[2,24,32,768]{3,2,1,0:T(8,128)(2,1)S(1)} %copy-done.7, bf16[2,256,768]{2,1,0:T(8,128)(2,1)S(1)} %copy-done), kind=kOutput, calls=%fused_computation.10 | convolution fusion | flops 1207959552 | bytes 6291456 | tf_op jit(solution)/shard_map/sgae,tce->stgac/dot_general | solution.py:245
  85.2 4.9 %collective-permute-done.6 = f32[2,1,2,2,1,1,4,2,1024]{8,7,6,5,4,3,2,1,0:T(2,128)S(1)} collective-permute-done((f32[2,1,2,2,1,1,4,2,1024]{8,7,6,5,4,3,2,1,0:T(2,128)S(1)}, f32[2,1,2,2,1,1,4,2,1024]{8,7,6,5,4,3,2,1,0:T(2,128)S(1)}, u32[]{:S(2)}, u32[]{:S(2)}) %collective-permute-start.6) | collective-permute-done | bytes 262176 | tf_op jit(solution)/shard_map/ppermute | solution.py:58
  90.1 0.2 select_add_fusion.2
  90.3 0.1 broadcast_select_fusion.3
  90.4 0.1 collective-permute-start.7
  90.5 0.3 slice_add_fusion.1
  90.7 6.4 %collective-permute-done.7 = f32[2,1,2,1,1,1,4,2,1024]{8,7,6,5,4,3,2,1,0:T(2,128)S(1)} collective-permute-done((f32[2,1,2,1,1,1,4,2,1024]{8,7,6,5,4,3,2,1,0:T(2,128)S(1)}, f32[2,1,2,1,1,1,4,2,1024]{8,7,6,5,4,3,2,1,0:T(2,128)S(1)}, u32[]{:S(2)}, u32[]{:S(2)}) %collective-permute-start.7) | collective-permute-done | bytes 131104 | tf_op jit(solution)/shard_map/ppermute | solution.py:58
  97.2 0.1 select_add_fusion.3
  97.3 2.5 %collective-permute-start.8 = (f32[1,1,2,1,1,1,4,2,1024]{8,7,6,5,4,3,2,1,0:T(2,128)S(1)}, f32[1,1,2,1,1,1,4,2,1024]{8,7,6,5,4,3,2,1,0:T(2,128)S(1)}, u32[]{:S(2)}, u32[]{:S(2)}) collective-permute-start(f32[1,1,2,1,1,1,4,2,1024]{8,7,6,5,4,3,2,1,0:T(2,128)S(1)} %broadcast_select_fusion.4), channel_id=1, source_target_pairs={{0,32},{1,5},{2,34},{3,7},{4,36},{5,1},{6,38},{7,3},{8,40},{9,13},... | collective-permute-start | bytes 196616 | tf_op jit(solution)/shard_map/ppermute | solution.py:58
  99.8 0.1 fusion.28
  100.0 1.0 copy.57
  100.9 3.5 %all-to-all-start.1 = ((bf16[32,24,256]{2,1,0:T(8,128)(2,1)}), bf16[32,24,256]{2,1,0:T(8,128)(2,1)S(1)}, u32[]{:S(2)}, u32[]{:S(2)}) async-start(bf16[32,24,256]{2,1,0:T(8,128)(2,1)} %copy.57), calls=%async_computation.1 | async-start | bytes 786432 | tf_op jit(solution)/shard_map/all_to_all | solution.py:251
  104.5 2.2 %collective-permute-start.9 = (f32[1,1,1,1,1,1,4,2,1024]{8,7,6,5,4,3,2,1,0:T(2,128)S(1)}, f32[1,1,1,1,1,1,4,2,1024]{8,7,6,5,4,3,2,1,0:T(2,128)S(1)}, u32[]{:S(2)}, u32[]{:S(2)}) collective-permute-start(f32[1,1,1,1,1,1,4,2,1024]{8,7,6,5,4,3,2,1,0:T(2,128)S(1)} %broadcast_select_fusion.5), channel_id=1, source_target_pairs={{0,8},{1,9},{2,10},{3,11},{4,12},{5,13},{6,14},{7,15},{8,0},{9,1},... | collective-permute-start | bytes 98312 | tf_op jit(solution)/shard_map/ppermute | solution.py:58
  106.7 5.0 %all-to-all-done.1 = bf16[32,24,256]{2,1,0:T(8,128)(2,1)S(1)} async-done(((bf16[32,24,256]{2,1,0:T(8,128)(2,1)}), bf16[32,24,256]{2,1,0:T(8,128)(2,1)S(1)}, u32[]{:S(2)}, u32[]{:S(2)}) %all-to-all-start.1) | async-done | bytes 393248 | tf_op jit(solution)/shard_map/all_to_all | solution.py:251
  111.7 0.1 copy.77
  111.8 0.6 collective-permute-done.9
  112.4 0.7 broadcast_in_dim.73
  113.1 4.7 %all-to-all-start.2 = ((f32[4,4,2,1024]{3,1,2,0:T(4,128)}), f32[4,4,2,1024]{3,1,2,0:T(4,128)S(1)}, u32[]{:S(2)}, u32[]{:S(2)}) async-start(f32[4,4,2,1024]{3,1,2,0:T(4,128)} %broadcast_in_dim.73), calls=%async_computation.2 | async-start | bytes 262144 | tf_op jit(solution)/shard_map/all_to_all | solution.py:65
  117.9 1.9 %collective-permute-start.3 = (bf16[8,2,24,256]{3,0,2,1:T(8,128)(2,1)S(1)}, bf16[8,2,24,256]{3,0,2,1:T(8,128)(2,1)S(1)}, u32[]{:S(2)}, u32[]{:S(2)}) collective-permute-start(bf16[8,2,24,256]{3,0,2,1:T(8,128)(2,1)S(1)} %get-tuple-element.22), channel_id=1, source_target_pairs={{1,0},{2,1},{3,2},{4,3},{5,4},{6,5},{7,6},{8,7},{9,8},{10,9},{11,1... | collective-permute-start | bytes 589832 | tf_op jit(solution)/shard_map/ppermute | solution.py:89
  119.8 2.4 %collective-permute-start.2 = (bf16[8,2,24,256]{3,0,2,1:T(8,128)(2,1)S(1)}, bf16[8,2,24,256]{3,0,2,1:T(8,128)(2,1)S(1)}, u32[]{:S(2)}, u32[]{:S(2)}) collective-permute-start(bf16[8,2,24,256]{3,0,2,1:T(8,128)(2,1)S(1)} %get-tuple-element.21), channel_id=1, source_target_pairs={{0,1},{1,2},{2,3},{3,4},{4,5},{5,6},{6,7},{7,8},{8,9},{9,10},{10,1... | collective-permute-start | bytes 589832 | tf_op jit(solution)/shard_map/ppermute | solution.py:87
  122.2 1.6 %all-to-all-done.2 = f32[4,4,2,1024]{3,1,2,0:T(4,128)S(1)} async-done(((f32[4,4,2,1024]{3,1,2,0:T(4,128)}), f32[4,4,2,1024]{3,1,2,0:T(4,128)S(1)}, u32[]{:S(2)}, u32[]{:S(2)}) %all-to-all-start.2) | async-done | bytes 131104 | tf_op jit(solution)/shard_map/all_to_all | solution.py:65
  123.8 0.6 multiply_reduce_fusion
  124.5 1.3 broadcast_in_dim_broadcast_in_dim_broadcast_in_dim.2
  125.7 6.3 %all-to-all-start.3 = ((f32[64,1,128]{2,1,0:T(1,128)}), f32[64,1,128]{2,1,0:T(1,128)S(1)}, u32[]{:S(2)}, u32[]{:S(2)}) async-start(f32[64,1,128]{2,1,0:T(1,128)} %broadcast_in_dim_broadcast_in_dim_broadcast_in_dim.2), calls=%async_computation.3 | async-start | bytes 65536 | tf_op jit(solution)/shard_map/all_to_all | solution.py:65
  132.2 1.7 %gather_fusion.1 = bf16[8,4,24,256]{3,0,2,1:T(8,128)(2,1)S(1)} fusion(bf16[8,8,28,256]{3,0,2,1:T(8,128)(2,1)S(1)} %select_maximum_fusion, s32[8]{0:T(128)S(1)} %get-tuple-element.25), kind=kCustom, calls=%fused_computation.1 | custom fusion | bytes 786560 | tf_op jit(solution)/shard_map/vmap()/gather | solution.py:104
  133.9 0.8 copy.62
  134.7 6.0 %all-to-all-done.3 = f32[64,1,128]{2,1,0:T(1,128)S(1)} async-done(((f32[64,1,128]{2,1,0:T(1,128)}), f32[64,1,128]{2,1,0:T(1,128)S(1)}, u32[]{:S(2)}, u32[]{:S(2)}) %all-to-all-start.3) | async-done | bytes 32800 | tf_op jit(solution)/shard_map/all_to_all | solution.py:65
  140.9 0.6 slice.512
  141.5 0.6 slice.513
  (33 shorter events, 0.5 us)
Async XLA Ops:
  0.6 34.5 %copy-start = (bf16[2,256,768]{2,1,0:T(8,128)(2,1)S(1)}, bf16[2,256,768]{2,1,0:T(8,128)(2,1)}, u32[]{:S(2)}) copy-start(bf16[2,256,768]{2,1,0:T(8,128)(2,1)} %param.11) | copy-start | bytes 2359300
  0.6 10.5 %copy-start.1 = (bf16[8,4,24,256]{3,2,1,0:T(8,128)(2,1)S(1)}, bf16[8,4,24,256]{3,2,1,0:T(8,128)(2,1)}, u32[]{:S(2)}) copy-start(bf16[8,4,24,256]{3,2,1,0:T(8,128)(2,1)} %param.13) | copy-start | bytes 1179652
  0.7 10.7 %copy-start.3 = (s32[32,2]{0,1:T(2,128)S(1)}, s32[32,2]{0,1:T(2,128)}, u32[]{:S(2)}) copy-start(s32[32,2]{0,1:T(2,128)} %param.10) | copy-start | bytes 772
  2.0 10.3 %collective-permute-start.1 = (bf16[8,2,24,256]{3,0,2,1:T(8,128)(2,1)S(1)}, bf16[8,2,24,256]{3,0,2,1:T(8,128)(2,1)S(1)}, u32[]{:S(2)}, u32[]{:S(2)}) collective-permute-start(bf16[8,2,24,256]{3,0,2,1:T(8,128)(2,1)S(1)} %get-tuple-element.24), channel_id=1, source_target_pairs={{1,0},{2,1},{3,2},{4,3},{5,4},{6,5},{7,6},{8,7},{9,8},{10,9},{11,1... | collective-permute-start | bytes 589832 | tf_op jit(solution)/shard_map/ppermute | solution.py:89
  9.2 9.1 %collective-permute-start = (bf16[8,2,24,256]{3,0,2,1:T(8,128)(2,1)S(1)}, bf16[8,2,24,256]{3,0,2,1:T(8,128)(2,1)S(1)}, u32[]{:S(2)}, u32[]{:S(2)}) collective-permute-start(bf16[8,2,24,256]{3,0,2,1:T(8,128)(2,1)S(1)} %get-tuple-element.23), channel_id=1, source_target_pairs={{0,1},{1,2},{2,3},{3,4},{4,5},{5,6},{6,7},{7,8},{8,9},{9,10},{10,1... | collective-permute-start | bytes 589832 | tf_op jit(solution)/shard_map/ppermute | solution.py:87
  20.1 5.4 %copy-start.4 = (s32[32]{0:T(128)S(1)}, s32[32]{0:T(128)}, u32[]{:S(2)}) copy-start(s32[32]{0:T(128)} %param.8) | copy-start | bytes 388
  20.1 5.5 %copy-start.5 = (s32[32]{0:T(128)S(1)}, s32[32]{0:T(128)}, u32[]{:S(2)}) copy-start(s32[32]{0:T(128)} %param.9) | copy-start | bytes 388
  21.1 14.0 %all-to-all-start = ((bf16[8,96,512]{2,0,1:T(8,128)(2,1)}), bf16[8,96,512]{2,0,1:T(8,128)(2,1)S(1)}, u32[]{:S(2)}, u32[]{:S(2)}) async-start(bf16[8,96,512]{2,0,1:T(8,128)(2,1)} %pad_maximum_fusion.1), calls=%async_computation | async-start | bytes 1572864 | tf_op jit(solution)/shard_map/all_to_all | solution.py:217
  35.1 1.0 copy-start.2
  58.1 1.8 %copy-start.6 = (bf16[2,24,32,768]{3,2,1,0:T(8,128)(2,1)S(1)}, bf16[2,24,32,768]{3,2,1,0:T(8,128)(2,1)}, u32[]{:S(2)}) copy-start(bf16[2,24,32,768]{3,2,1,0:T(8,128)(2,1)} %get-tuple-element.5) | copy-start | bytes 7077892
  67.5 3.0 %collective-permute-start.4 = (f32[2,2,2,2,2,1,4,2,1024]{8,7,6,5,4,3,2,1,0:T(2,128)}, f32[2,2,2,2,2,1,4,2,1024]{8,7,6,5,4,3,2,1,0:T(2,128)}, u32[]{:S(2)}, u32[]{:S(2)}) collective-permute-start(f32[2,2,2,2,2,1,4,2,1024]{8,7,6,5,4,3,2,1,0:T(2,128)} %broadcast_select_fusion), channel_id=1, source_target_pairs={{0,1},{1,0},{2,3},{3,2},{4,5},{5,4},{6,7},{7,6},{8,9},{9,8},{10,11... | collective-permute-start | bytes 3145736 | tf_op jit(solution)/shard_map/ppermute | solution.py:58
  73.7 9.3 %collective-permute-start.5 = (f32[2,2,2,2,1,1,4,2,1024]{8,7,6,5,4,3,2,1,0:T(2,128)S(1)}, f32[2,2,2,2,1,1,4,2,1024]{8,7,6,5,4,3,2,1,0:T(2,128)S(1)}, u32[]{:S(2)}, u32[]{:S(2)}) collective-permute-start(f32[2,2,2,2,1,1,4,2,1024]{8,7,6,5,4,3,2,1,0:T(2,128)S(1)} %broadcast_select_fusion.1), channel_id=1, source_target_pairs={{0,2},{1,17},{2,0},{3,19},{4,6},{5,21},{6,4},{7,23},{8,10},{9,25},... | collective-permute-start | bytes 1572872 | tf_op jit(solution)/shard_map/ppermute | solution.py:58
  73.8 10.0 %copy-start.7 = (bf16[2,24,32,768]{3,2,1,0:T(8,128)(2,1)S(1)}, bf16[2,24,32,768]{3,2,1,0:T(8,128)(2,1)}, u32[]{:S(2)}) copy-start(bf16[2,24,32,768]{3,2,1,0:T(8,128)(2,1)} %get-tuple-element.5) | copy-start | bytes 7077892
  83.5 6.6 %collective-permute-start.6 = (f32[2,1,2,2,1,1,4,2,1024]{8,7,6,5,4,3,2,1,0:T(2,128)S(1)}, f32[2,1,2,2,1,1,4,2,1024]{8,7,6,5,4,3,2,1,0:T(2,128)S(1)}, u32[]{:S(2)}, u32[]{:S(2)}) collective-permute-start(f32[2,1,2,2,1,1,4,2,1024]{8,7,6,5,4,3,2,1,0:T(2,128)S(1)} %broadcast_select_fusion.2), channel_id=1, source_target_pairs={{0,16},{1,3},{2,18},{3,1},{4,20},{5,7},{6,22},{7,5},{8,24},{9,11},... | collective-permute-start | bytes 786440 | tf_op jit(solution)/shard_map/ppermute | solution.py:58
  90.4 6.8 %collective-permute-start.7 = (f32[2,1,2,1,1,1,4,2,1024]{8,7,6,5,4,3,2,1,0:T(2,128)S(1)}, f32[2,1,2,1,1,1,4,2,1024]{8,7,6,5,4,3,2,1,0:T(2,128)S(1)}, u32[]{:S(2)}, u32[]{:S(2)}) collective-permute-start(f32[2,1,2,1,1,1,4,2,1024]{8,7,6,5,4,3,2,1,0:T(2,128)S(1)} %broadcast_select_fusion.3), channel_id=1, source_target_pairs={{0,4},{1,33},{2,6},{3,35},{4,0},{5,37},{6,2},{7,39},{8,12},{9,41},... | collective-permute-start | bytes 393224 | tf_op jit(solution)/shard_map/ppermute | solution.py:58
  97.3 7.1 %collective-permute-start.8 = (f32[1,1,2,1,1,1,4,2,1024]{8,7,6,5,4,3,2,1,0:T(2,128)S(1)}, f32[1,1,2,1,1,1,4,2,1024]{8,7,6,5,4,3,2,1,0:T(2,128)S(1)}, u32[]{:S(2)}, u32[]{:S(2)}) collective-permute-start(f32[1,1,2,1,1,1,4,2,1024]{8,7,6,5,4,3,2,1,0:T(2,128)S(1)} %broadcast_select_fusion.4), channel_id=1, source_target_pairs={{0,32},{1,5},{2,34},{3,7},{4,36},{5,1},{6,38},{7,3},{8,40},{9,13},... | collective-permute-start | bytes 196616 | tf_op jit(solution)/shard_map/ppermute | solution.py:58
  100.9 10.8 %all-to-all-start.1 = ((bf16[32,24,256]{2,1,0:T(8,128)(2,1)}), bf16[32,24,256]{2,1,0:T(8,128)(2,1)S(1)}, u32[]{:S(2)}, u32[]{:S(2)}) async-start(bf16[32,24,256]{2,1,0:T(8,128)(2,1)} %copy.57), calls=%async_computation.1 | async-start | bytes 786432 | tf_op jit(solution)/shard_map/all_to_all | solution.py:251
  104.5 7.9 %collective-permute-start.9 = (f32[1,1,1,1,1,1,4,2,1024]{8,7,6,5,4,3,2,1,0:T(2,128)S(1)}, f32[1,1,1,1,1,1,4,2,1024]{8,7,6,5,4,3,2,1,0:T(2,128)S(1)}, u32[]{:S(2)}, u32[]{:S(2)}) collective-permute-start(f32[1,1,1,1,1,1,4,2,1024]{8,7,6,5,4,3,2,1,0:T(2,128)S(1)} %broadcast_select_fusion.5), channel_id=1, source_target_pairs={{0,8},{1,9},{2,10},{3,11},{4,12},{5,13},{6,14},{7,15},{8,0},{9,1},... | collective-permute-start | bytes 98312 | tf_op jit(solution)/shard_map/ppermute | solution.py:58
  113.1 10.7 %all-to-all-start.2 = ((f32[4,4,2,1024]{3,1,2,0:T(4,128)}), f32[4,4,2,1024]{3,1,2,0:T(4,128)S(1)}, u32[]{:S(2)}, u32[]{:S(2)}) async-start(f32[4,4,2,1024]{3,1,2,0:T(4,128)} %broadcast_in_dim.73), calls=%async_computation.2 | async-start | bytes 262144 | tf_op jit(solution)/shard_map/all_to_all | solution.py:65
  117.9 14.2 %collective-permute-start.3 = (bf16[8,2,24,256]{3,0,2,1:T(8,128)(2,1)S(1)}, bf16[8,2,24,256]{3,0,2,1:T(8,128)(2,1)S(1)}, u32[]{:S(2)}, u32[]{:S(2)}) collective-permute-start(bf16[8,2,24,256]{3,0,2,1:T(8,128)(2,1)S(1)} %get-tuple-element.22), channel_id=1, source_target_pairs={{1,0},{2,1},{3,2},{4,3},{5,4},{6,5},{7,6},{8,7},{9,8},{10,9},{11,1... | collective-permute-start | bytes 589832 | tf_op jit(solution)/shard_map/ppermute | solution.py:89
  119.8 12.3 %collective-permute-start.2 = (bf16[8,2,24,256]{3,0,2,1:T(8,128)(2,1)S(1)}, bf16[8,2,24,256]{3,0,2,1:T(8,128)(2,1)S(1)}, u32[]{:S(2)}, u32[]{:S(2)}) collective-permute-start(bf16[8,2,24,256]{3,0,2,1:T(8,128)(2,1)S(1)} %get-tuple-element.21), channel_id=1, source_target_pairs={{0,1},{1,2},{2,3},{3,4},{4,5},{5,6},{6,7},{7,8},{8,9},{9,10},{10,1... | collective-permute-start | bytes 589832 | tf_op jit(solution)/shard_map/ppermute | solution.py:87
  125.7 14.9 %all-to-all-start.3 = ((f32[64,1,128]{2,1,0:T(1,128)}), f32[64,1,128]{2,1,0:T(1,128)S(1)}, u32[]{:S(2)}, u32[]{:S(2)}) async-start(f32[64,1,128]{2,1,0:T(1,128)} %broadcast_in_dim_broadcast_in_dim_broadcast_in_dim.2), calls=%async_computation.3 | async-start | bytes 65536 | tf_op jit(solution)/shard_map/all_to_all | solution.py:65

commit v8 on v7

--- a/solution.py
+++ b/solution.py
@@ -5,9 +5,10 @@
 import jax.numpy as jnp
 from jax import lax
 from jax.experimental import pallas as pl
-from jax.sharding import PartitionSpec as P
+from jax.sharding import Mesh, PartitionSpec as P
 
 HEADS = 8
+TILE = ("x", "z", "core")
 MAXOFF = 2
 
 
@@ -206,7 +207,7 @@
     agents = own_count * lax.axis_size("agent")
     first_agent = lax.axis_index("agent") * own_count
     own_offsets = lax.dynamic_slice_in_dim(offsets, first_agent, own_count, 0)
-    rimmed = with_halo(feats, (("tile", 1),), MAXOFF)
+    rimmed = with_halo(feats, ((TILE, 1),), MAXOFF)
     warped = relocate(rimmed, own_offsets, 1)
     cell_count = row_count * col_count
     head_size = channels // HEADS
@@ -255,17 +256,27 @@
         "tgac,sgae->scte", feats_typed, d_split, preferred_element_type=f32
     )
     raw_qkv = qkv_terms[0] + qkv_terms[1]
-    rimmed_grad = with_halo(d_warped, (("tile", 1),), MAXOFF)
+    rimmed_grad = with_halo(d_warped, ((TILE, 1),), MAXOFF)
     d_feats = relocate(rimmed_grad, own_offsets, -1)
     norm_limit = math.sqrt(8.0 * channels * channels)
     raw_all = jnp.concatenate([raw_qkv, raw_out], axis=-1)
-    tiles = lax.axis_size("tile")
-    share_rows = channels // tiles
-    pieces = raw_all.reshape(tiles, share_rows, 2, 4 * channels)
-    share_all = halving_sum(pieces, "tile", tile_bit_order(tiles), tile_twins(tiles))
+    sizes = [lax.axis_size(name) for name in TILE]
+    share_rows = channels // math.prod(sizes)
+    pieces = raw_all.reshape(*sizes, share_rows, 2, 4 * channels)
+    core_at = len(sizes) - 1
+    mine = lax.axis_index("core")
+    keep = lax.dynamic_index_in_dim(pieces, mine, core_at, keepdims=False)
+    send = lax.dynamic_index_in_dim(pieces, 1 - mine, core_at, keepdims=False)
+    share_all = keep + lax.ppermute(send, "core", [(0, 1), (1, 0)])
+    for dim, name in ((0, "x"), (0, "z")):
+        held = lax.all_to_all(share_all, name, dim, dim, tiled=True)
+        total = held[0]
+        for i in range(1, held.shape[0]):
+            total = total + held[i]
+        share_all = total
     share_all = gather_sum(share_all, "agent")
     square_sum = jnp.sum(share_all * share_all).reshape(1, 1)
-    square_sum = gather_sum(jnp.broadcast_to(square_sum, (1, 128)), "tile")[0, 0]
+    square_sum = gather_sum(jnp.broadcast_to(square_sum, (1, 128)), TILE)[0, 0]
     factor = norm_limit / jnp.maximum(jnp.sqrt(square_sum), norm_limit)
     scaled = share_all * factor
     scaled = jnp.transpose(scaled, (1, 0, 2))
@@ -273,19 +284,25 @@
 
 
 def solution(mesh):
+    agents_n, tiles = mesh.devices.shape
+    cores = 2
+    zs = min(8, tiles // cores)
+    fine = Mesh(
+        mesh.devices.reshape(agents_n, tiles // (cores * zs), zs, cores), ("agent",) + TILE
+    )
     placed = (
-        P("agent", "tile", None, None),
-        P(),
-        P(),
-        P(),
-        P(),
-        P(),
-        P("agent", "tile", None, None),
+        P("agent", TILE, None, None),
+        P(),
+        P(),
+        P(),
+        P(),
+        P(),
+        P("agent", TILE, None, None),
     )
     return jax.shard_map(
         body,
-        mesh=mesh,
+        mesh=fine,
         in_specs=placed,
-        out_specs=(P("agent", "tile", None, None), P(None, "tile", None), P(None, "tile", None)),
+        out_specs=(P("agent", TILE, None, None), P(None, TILE, None), P(None, TILE, None)),
         check_vma=False,
     )

time: 144 us -> 146 us (1.014)
  other arithmetic: 12.1 us -> 8.19 us
  local copies, waits for them, and re-layouts: 13.5 us -> 15.8 us
  starting transfers between devices: 37.6 us -> 39.6 us
  matrix products: 5.65 us -> 7.32 us
    ppermute x6 -> x1, waiting for transfers between devices: 24.1 us -> 2.65 us  [body(): share_all = keep + lax.ppermute(send, 'core', [(0, 1), (1, 0)])]
    all_to_all x0 -> x2, waiting for transfers between devices: none -> 19.9 us  [body(): held = lax.all_to_all(share_all, name, dim, dim, tiled=True)]
    all_to_all x0 -> x2, starting transfers between devices: none -> 8.75 us  [body(): held = lax.all_to_all(share_all, name, dim, dim, tiled=True)]
    ppermute x6 -> x1, starting transfers between devices: 5.2 us -> 0.09 us  [body(): share_all = keep + lax.ppermute(send, 'core', [(0, 1), (1, 0)])]
    select_n x7 -> x0, other arithmetic: 2.71 us -> none  [the longest x6 2.16 us: halving_sum(): send = jnp.where(mine == 1, low, high)]
    all_to_all x2, starting transfers between devices: 11.1 us -> 9.22 us  [gather_sum(): held = lax.all_to_all(copies, axis, 0, 0, tiled=True)]
    dot_general x1, matrix products: 1.42 us -> 3.08 us  [body(): jnp.einsum('sgae,tce->stgac', d_split, w_qkv, preferred_element_type=f32)]
    add x5 -> x2, other arithmetic: 2.98 us -> 1.74 us  [the longest x1 1.69 us: body(): share_all = keep + lax.ppermute(send, 'core', [(0, 1), (1, 0)])]
  transfers between devices with their start and end apart: 14 -> 11, of which waited for: 11 -> 9; matrix products, arithmetic and copies ran while one was open for 6% -> 8% of each run, Pallas kernels for 0% -> 0%
where the time goes in v8:
time: 146 us; the launch traced here: 144 us
  waiting for transfers between devices  52.2 us (36%)
  starting transfers between devices  39.6 us (27%)
  Pallas kernels  19.6 us (13%)
  local copies, waits for them, and re-layouts  15.8 us (11%)
  other arithmetic  8.19 us (6%)
  matrix products  7.32 us (5%)
    all_to_all x2, waiting for transfers between devices, body(): held = lax.all_to_all(share_all, name, dim, dim, tiled=True)  19.9 us
    pallas_call x1, Pallas kernels, cell_attention(): pl.pallas_call(functools.partial(attention_kernel, block_size), grid=(cel...  19.6 us
    all_to_all x2, starting transfers between devices, gather_sum(): held = lax.all_to_all(copies, axis, 0, 0, tiled=True)  9.22 us
    ppermute x2, starting transfers between devices, with_halo(): lax.ppermute(head, axis, [((i + 1) % count, i) for i in range(ends)])  9.1 us
    all_to_all x1, waiting for transfers between devices, body(): lax.all_to_all(jnp.concatenate([flat_feats, flat_grads], axis=-1), 'agent...  8.94 us
    all_to_all x2, starting transfers between devices, body(): held = lax.all_to_all(share_all, name, dim, dim, tiled=True)  8.75 us
    all_to_all x2, waiting for transfers between devices, gather_sum(): held = lax.all_to_all(copies, axis, 0, 0, tiled=True)  7.35 us
    all_to_all x1, waiting for transfers between devices, body(): lax.all_to_all(d_part, 'agent', split_axis=0, concat_axis=1, tiled=True)  6.49 us
  transfers between devices with their start and end apart: 11, of which 9 were waited for; matrix products, arithmetic and copies ran while one was open for 8% of the time, Pallas kernels for 0%

profile of v8, /device:TPU:2, one launch (start us, length us, event | category | flops | bytes accessed | tf_op | source)
XLA Modules:
  0.0 143.7 jit_solution(7812706953610747929)
XLA Ops:
  0.6 0.0 copy-start
  0.7 1.3 copy.49
  2.0 7.2 %collective-permute-start.1 = (bf16[8,2,24,256]{3,0,2,1:T(8,128)(2,1)S(1)}, bf16[8,2,24,256]{3,0,2,1:T(8,128)(2,1)S(1)}, u32[]{:S(2)}, u32[]{:S(2)}) collective-permute-start(bf16[8,2,24,256]{3,0,2,1:T(8,128)(2,1)S(1)} %get-tuple-element.26), channel_id=1, source_target_pairs={{1,0},{2,1},{3,2},{4,3},{5,4},{6,5},{7,6},{8,7},{9,8},{10,9},{11,1... | collective-permute-start | bytes 589832 | tf_op jit(solution)/shard_map/ppermute | solution.py:90
  9.2 1.9 %collective-permute-start = (bf16[8,2,24,256]{3,0,2,1:T(8,128)(2,1)S(1)}, bf16[8,2,24,256]{3,0,2,1:T(8,128)(2,1)S(1)}, u32[]{:S(2)}, u32[]{:S(2)}) collective-permute-start(bf16[8,2,24,256]{3,0,2,1:T(8,128)(2,1)S(1)} %get-tuple-element.25), channel_id=1, source_target_pairs={{0,1},{1,2},{2,3},{3,4},{4,5},{5,6},{6,7},{7,8},{8,9},{9,10},{10,1... | collective-permute-start | bytes 589832 | tf_op jit(solution)/shard_map/ppermute | solution.py:88
  11.1 0.2 copy.52
  11.4 0.1 constant_dynamic-slice_fusion.2
  11.5 0.9 collective-permute-done.1
  12.4 5.9 %collective-permute-done = bf16[8,2,24,256]{3,0,2,1:T(8,128)(2,1)S(1)} collective-permute-done((bf16[8,2,24,256]{3,0,2,1:T(8,128)(2,1)S(1)}, bf16[8,2,24,256]{3,0,2,1:T(8,128)(2,1)S(1)}, u32[]{:S(2)}, u32[]{:S(2)}) %collective-permute-start) | collective-permute-done | bytes 196640 | tf_op jit(solution)/shard_map/ppermute | solution.py:88
  18.3 0.1 fusion.18
  18.4 1.7 %gather_fusion = bf16[8,4,24,256]{3,0,2,1:T(8,128)(2,1)S(1)} fusion(bf16[8,8,28,256]{3,0,2,1:T(8,128)(2,1)S(1)} %fusion.18, s32[8]{0:T(128)S(1)} %get-tuple-element.28), kind=kCustom, calls=%fused_computation | custom fusion | bytes 786560 | tf_op jit(solution)/shard_map/vmap()/gather | solution.py:105
  20.1 0.0 copy-start.4
  20.1 0.0 copy-start.5
  20.1 1.0 pad_maximum_fusion.1
  21.1 4.5 %all-to-all-start = ((bf16[8,96,512]{2,0,1:T(8,128)(2,1)}), bf16[8,96,512]{2,0,1:T(8,128)(2,1)S(1)}, u32[]{:S(2)}, u32[]{:S(2)}) async-start(bf16[8,96,512]{2,0,1:T(8,128)(2,1)} %pad_maximum_fusion.1), calls=%async_computation | async-start | bytes 1572864 | tf_op jit(solution)/shard_map/all_to_all | solution.py:218
  25.6 0.5 fusion.39.valid_ref
  26.1 8.9 %all-to-all-done = bf16[8,96,512]{2,0,1:T(8,128)(2,1)S(1)} async-done(((bf16[8,96,512]{2,0,1:T(8,128)(2,1)}), bf16[8,96,512]{2,0,1:T(8,128)(2,1)S(1)}, u32[]{:S(2)}, u32[]{:S(2)}) %all-to-all-start) | async-done | bytes 786464 | tf_op jit(solution)/shard_map/all_to_all | solution.py:218
  35.0 0.1 copy.81
  35.1 0.0 copy-start.2
  35.2 0.8 convert_bitcast_fusion
  35.9 0.2 copy-done.2
  36.1 0.4 fusion.12
  36.5 1.2 fusion.13.qkv_ref
  37.7 0.8 fusion.29.da_ref
  38.5 19.6 %shard_map.94 = (bf16[24,32,256]{2,1,0:T(8,128)(2,1)}, bf16[2,24,32,768]{3,2,1,0:T(8,128)(2,1)}) custom-call(f32[1,32]{1,0:T(1,128)} %fusion.39.valid_ref, bf16[24,32,768]{2,1,0:T(8,128)(2,1)} %fusion.13.qkv_ref, bf16[24,32,256]{2,1,0:T(8,128)(2,1)} %fusion.29.da_ref), custom_call_target="tpu_custom_call" | custom-call | flops 2415919104 | bytes 4325376 | tf_op jit(solution)/shard_map/pallas_call | solution.py:178
  58.1 1.6 %convolution_bitcast_fusion = f32[256,2,256]{0,2,1:T(8,128)S(1)} fusion(pred[2,32]{1,0:T(4,128)(4,1)S(1)} %pad_add_fusion, bf16[24,32,256]{2,1,0:T(8,128)(2,1)} %get-tuple-element.6, bf16[32,24,512]{2,0,1:T(8,128)(2,1)S(1)} %bitcast.417), kind=kOutput, calls=%fused_computation.18 | convolution fusion | flops 201719808 | bytes 1311232 | tf_op jit(solution)/shard_map/tgac,gae->cte/dot_general | solution.py:243
  59.7 0.2 copy-done.6
  59.9 1.5 %fusion.7 = f32[2,256,2,768]{1,3,2,0:T(8,128)S(1)} fusion(bf16[2,24,32,768]{3,2,1,0:T(8,128)(2,1)S(1)} %copy-done.6, pred[2,32]{1,0:T(4,128)(4,1)S(1)} %pad_add_fusion, bf16[24,32,256]{2,1,0:T(8,128)(2,1)S(1)} %slice_bitcast_fusion.7), kind=kOutput, calls=%fused_computation.11 | convolution fusion | flops 1208352768 | bytes 5898304 | tf_op jit(solution)/shard_map/tgac,sgae->scte/dot_general | solution.py:255
  61.4 0.2 fusion.11
  61.6 1.5 %pad_maximum_fusion = f32[256,2,1024]{0,2,1:T(8,128)} fusion(f32[256,2,256]{0,2,1:T(8,128)S(1)} %convolution_bitcast_fusion, f32[256,2,768]{0,2,1:T(8,128)S(1)} %fusion.11), kind=kLoop, calls=%fused_computation.9 | loop fusion | flops 524288 | bytes 4194304 | tf_op jit(solution)/shard_map/concatenate | solution.py:262
  63.0 2.9 %copy.60 = f32[256,2,1024]{2,1,0:T(2,128)S(1)} copy(f32[256,2,1024]{0,2,1:T(8,128)} %pad_maximum_fusion) | data formatting | bytes 4194304 | tf_op jit(solution)/shard_map/concatenate | solution.py:262
  66.0 0.7 constant_dynamic-slice_fusion.1
  66.7 0.6 copy.80
  67.3 0.1 collective-permute-start.4
  67.4 2.6 %collective-permute-done.4 = f32[4,8,4,2,1024]{4,1,3,2,0:T(8,128)S(1)} collective-permute-done((f32[4,8,4,2,1024]{4,1,3,2,0:T(8,128)S(1)}, f32[4,8,4,2,1024]{4,1,3,2,0:T(8,128)S(1)}, u32[]{:S(2)}, u32[]{:S(2)}) %collective-permute-start.4) | collective-permute-done | bytes 1048608 | tf_op jit(solution)/shard_map/ppermute | solution.py:270
  70.1 1.7 %bitcast_add_fusion = f32[4,8,4,2,1024]{4,1,3,2,0:T(8,128)} fusion(f32[4,8,4,2,1024]{4,1,3,2,0:T(8,128)S(1)} %collective-permute-done.4, f32[4,8,1,4,2,1024]{5,4,3,2,1,0:T(2,128)S(1)} %get-tuple-element.21), kind=kLoop, calls=%fused_computation.22 | loop fusion | flops 262144 | bytes 3145728 | tf_op jit(solution)/shard_map/add | solution.py:270
  71.8 4.9 %all-to-all-start.2 = ((f32[4,8,4,2,1024]{4,1,3,2,0:T(8,128)}), f32[4,8,4,2,1024]{4,1,3,2,0:T(8,128)S(1)}, u32[]{:S(2)}, u32[]{:S(2)}) async-start(f32[4,8,4,2,1024]{4,1,3,2,0:T(8,128)} %bitcast_add_fusion), calls=%async_computation.2 | async-start | bytes 2097152 | tf_op jit(solution)/shard_map/all_to_all | solution.py:272
  76.6 3.1 %fusion.4 = f32[2,2,24,32,256]{4,3,2,1,0:T(8,128)S(1)} fusion(bf16[2,24,32,768]{3,2,1,0:T(8,128)(2,1)} %get-tuple-element.5, bf16[2,256,768]{2,1,0:T(8,128)(2,1)S(1)} %copy-done), kind=kOutput, calls=%fused_computation.10 | convolution fusion | flops 1207959552 | bytes 6291456 | tf_op jit(solution)/shard_map/sgae,tce->stgac/dot_general | solution.py:246
  79.7 0.2 slice_add_fusion.1
  80.0 0.1 fusion.28
  80.1 1.0 copy.58
  81.0 9.5 %all-to-all-done.2 = f32[4,8,4,2,1024]{4,1,3,2,0:T(8,128)S(1)} async-done(((f32[4,8,4,2,1024]{4,1,3,2,0:T(8,128)}), f32[4,8,4,2,1024]{4,1,3,2,0:T(8,128)S(1)}, u32[]{:S(2)}, u32[]{:S(2)}) %all-to-all-start.2) | async-done | bytes 1048608 | tf_op jit(solution)/shard_map/all_to_all | solution.py:272
  90.6 3.5 %all-to-all-start.1 = ((bf16[32,24,256]{2,1,0:T(8,128)(2,1)}), bf16[32,24,256]{2,1,0:T(8,128)(2,1)S(1)}, u32[]{:S(2)}, u32[]{:S(2)}) async-start(bf16[32,24,256]{2,1,0:T(8,128)(2,1)} %copy.58), calls=%async_computation.1 | async-start | bytes 786432 | tf_op jit(solution)/shard_map/all_to_all | solution.py:252
  94.0 0.1 fusion.36
  94.1 0.9 copy.63
  95.0 6.5 %all-to-all-done.1 = bf16[32,24,256]{2,1,0:T(8,128)(2,1)S(1)} async-done(((bf16[32,24,256]{2,1,0:T(8,128)(2,1)}), bf16[32,24,256]{2,1,0:T(8,128)(2,1)S(1)}, u32[]{:S(2)}, u32[]{:S(2)}) %all-to-all-start.1) | async-done | bytes 393248 | tf_op jit(solution)/shard_map/all_to_all | solution.py:252
  101.5 3.9 %all-to-all-start.3 = ((f32[8,4,2,1024]{3,2,1,0:T(2,128)}), f32[8,4,2,1024]{3,2,1,0:T(2,128)S(1)}, u32[]{:S(2)}, u32[]{:S(2)}) async-start(f32[8,4,2,1024]{3,2,1,0:T(2,128)} %copy.63), calls=%async_computation.3 | async-start | bytes 524288 | tf_op jit(solution)/shard_map/all_to_all | solution.py:272
  105.4 0.1 copy.82
  105.5 10.4 %all-to-all-done.3 = f32[8,4,2,1024]{3,2,1,0:T(2,128)S(1)} async-done(((f32[8,4,2,1024]{3,2,1,0:T(2,128)}), f32[8,4,2,1024]{3,2,1,0:T(2,128)S(1)}, u32[]{:S(2)}, u32[]{:S(2)}) %all-to-all-start.3) | async-done | bytes 262176 | tf_op jit(solution)/shard_map/all_to_all | solution.py:272
  115.9 0.1 fusion.38
  116.0 0.7 broadcast_in_dim.74
  116.6 3.3 %all-to-all-start.4 = ((f32[4,4,2,1024]{3,1,2,0:T(4,128)}), f32[4,4,2,1024]{3,1,2,0:T(4,128)S(1)}, u32[]{:S(2)}, u32[]{:S(2)}) async-start(f32[4,4,2,1024]{3,1,2,0:T(4,128)} %broadcast_in_dim.74), calls=%async_computation.4 | async-start | bytes 262144 | tf_op jit(solution)/shard_map/all_to_all | solution.py:66
  120.0 1.9 %collective-permute-start.3 = (bf16[8,2,24,256]{3,0,2,1:T(8,128)(2,1)S(1)}, bf16[8,2,24,256]{3,0,2,1:T(8,128)(2,1)S(1)}, u32[]{:S(2)}, u32[]{:S(2)}) collective-permute-start(bf16[8,2,24,256]{3,0,2,1:T(8,128)(2,1)S(1)} %get-tuple-element.24), channel_id=1, source_target_pairs={{1,0},{2,1},{3,2},{4,3},{5,4},{6,5},{7,6},{8,7},{9,8},{10,9},{11,1... | collective-permute-start | bytes 589832 | tf_op jit(solution)/shard_map/ppermute | solution.py:90
  121.9 2.6 %collective-permute-start.2 = (bf16[8,2,24,256]{3,0,2,1:T(8,128)(2,1)S(1)}, bf16[8,2,24,256]{3,0,2,1:T(8,128)(2,1)S(1)}, u32[]{:S(2)}, u32[]{:S(2)}) collective-permute-start(bf16[8,2,24,256]{3,0,2,1:T(8,128)(2,1)S(1)} %get-tuple-element.23), channel_id=1, source_target_pairs={{0,1},{1,2},{2,3},{3,4},{4,5},{5,6},{6,7},{7,8},{8,9},{9,10},{10,1... | collective-permute-start | bytes 589832 | tf_op jit(solution)/shard_map/ppermute | solution.py:88
  124.5 1.4 all-to-all-done.4
  125.9 0.6 multiply_reduce_fusion
  126.5 1.3 broadcast_in_dim_broadcast_in_dim_broadcast_in_dim.2
  127.8 5.9 %all-to-all-start.5 = ((f32[64,1,128]{2,1,0:T(1,128)}), f32[64,1,128]{2,1,0:T(1,128)S(1)}, u32[]{:S(2)}, u32[]{:S(2)}) async-start(f32[64,1,128]{2,1,0:T(1,128)} %broadcast_in_dim_broadcast_in_dim_broadcast_in_dim.2), calls=%async_computation.5 | async-start | bytes 65536 | tf_op jit(solution)/shard_map/all_to_all | solution.py:66
  133.7 0.1 select_maximum_fusion
  133.8 1.7 %gather_fusion.1 = bf16[8,4,24,256]{3,0,2,1:T(8,128)(2,1)S(1)} fusion(bf16[8,8,28,256]{3,0,2,1:T(8,128)(2,1)S(1)} %select_maximum_fusion, s32[8]{0:T(128)S(1)} %get-tuple-element.27), kind=kCustom, calls=%fused_computation.1 | custom fusion | bytes 786560 | tf_op jit(solution)/shard_map/vmap()/gather | solution.py:105
  135.5 0.8 copy.65
  136.3 6.0 %all-to-all-done.5 = f32[64,1,128]{2,1,0:T(1,128)S(1)} async-done(((f32[64,1,128]{2,1,0:T(1,128)}), f32[64,1,128]{2,1,0:T(1,128)S(1)}, u32[]{:S(2)}, u32[]{:S(2)}) %all-to-all-start.5) | async-done | bytes 32800 | tf_op jit(solution)/shard_map/all_to_all | solution.py:66
  142.3 0.1 fusion.44
  142.5 0.6 slice.512
  143.1 0.6 slice.513
  (18 shorter events, 0.2 us)
Async XLA Ops:
  0.6 34.5 %copy-start = (bf16[2,256,768]{2,1,0:T(8,128)(2,1)S(1)}, bf16[2,256,768]{2,1,0:T(8,128)(2,1)}, u32[]{:S(2)}) copy-start(bf16[2,256,768]{2,1,0:T(8,128)(2,1)} %param.11) | copy-start | bytes 2359300
  0.6 10.5 %copy-start.1 = (bf16[8,4,24,256]{3,2,1,0:T(8,128)(2,1)S(1)}, bf16[8,4,24,256]{3,2,1,0:T(8,128)(2,1)}, u32[]{:S(2)}) copy-start(bf16[8,4,24,256]{3,2,1,0:T(8,128)(2,1)} %param.13) | copy-start | bytes 1179652
  0.7 10.7 %copy-start.3 = (s32[32,2]{0,1:T(2,128)S(1)}, s32[32,2]{0,1:T(2,128)}, u32[]{:S(2)}) copy-start(s32[32,2]{0,1:T(2,128)} %param.10) | copy-start | bytes 772
  2.0 10.3 %collective-permute-start.1 = (bf16[8,2,24,256]{3,0,2,1:T(8,128)(2,1)S(1)}, bf16[8,2,24,256]{3,0,2,1:T(8,128)(2,1)S(1)}, u32[]{:S(2)}, u32[]{:S(2)}) collective-permute-start(bf16[8,2,24,256]{3,0,2,1:T(8,128)(2,1)S(1)} %get-tuple-element.26), channel_id=1, source_target_pairs={{1,0},{2,1},{3,2},{4,3},{5,4},{6,5},{7,6},{8,7},{9,8},{10,9},{11,1... | collective-permute-start | bytes 589832 | tf_op jit(solution)/shard_map/ppermute | solution.py:90
  9.2 9.1 %collective-permute-start = (bf16[8,2,24,256]{3,0,2,1:T(8,128)(2,1)S(1)}, bf16[8,2,24,256]{3,0,2,1:T(8,128)(2,1)S(1)}, u32[]{:S(2)}, u32[]{:S(2)}) collective-permute-start(bf16[8,2,24,256]{3,0,2,1:T(8,128)(2,1)S(1)} %get-tuple-element.25), channel_id=1, source_target_pairs={{0,1},{1,2},{2,3},{3,4},{4,5},{5,6},{6,7},{7,8},{8,9},{9,10},{10,1... | collective-permute-start | bytes 589832 | tf_op jit(solution)/shard_map/ppermute | solution.py:88
  20.1 5.4 %copy-start.4 = (s32[32]{0:T(128)S(1)}, s32[32]{0:T(128)}, u32[]{:S(2)}) copy-start(s32[32]{0:T(128)} %param.8) | copy-start | bytes 388
  20.1 5.5 %copy-start.5 = (s32[32]{0:T(128)S(1)}, s32[32]{0:T(128)}, u32[]{:S(2)}) copy-start(s32[32]{0:T(128)} %param.9) | copy-start | bytes 388
  21.1 14.0 %all-to-all-start = ((bf16[8,96,512]{2,0,1:T(8,128)(2,1)}), bf16[8,96,512]{2,0,1:T(8,128)(2,1)S(1)}, u32[]{:S(2)}, u32[]{:S(2)}) async-start(bf16[8,96,512]{2,0,1:T(8,128)(2,1)} %pad_maximum_fusion.1), calls=%async_computation | async-start | bytes 1572864 | tf_op jit(solution)/shard_map/all_to_all | solution.py:218
  35.1 1.0 copy-start.2
  58.1 1.8 %copy-start.6 = (bf16[2,24,32,768]{3,2,1,0:T(8,128)(2,1)S(1)}, bf16[2,24,32,768]{3,2,1,0:T(8,128)(2,1)}, u32[]{:S(2)}) copy-start(bf16[2,24,32,768]{3,2,1,0:T(8,128)(2,1)} %get-tuple-element.5) | copy-start | bytes 7077892
  67.3 2.7 %collective-permute-start.4 = (f32[4,8,4,2,1024]{4,1,3,2,0:T(8,128)S(1)}, f32[4,8,4,2,1024]{4,1,3,2,0:T(8,128)S(1)}, u32[]{:S(2)}, u32[]{:S(2)}) collective-permute-start(f32[4,8,4,2,1024]{4,1,3,2,0:T(8,128)S(1)} %bitcast.424), channel_id=1, source_target_pairs={{0,1},{1,0},{2,3},{3,2},{4,5},{5,4},{6,7},{7,6},{8,9},{9,8},{10,11... | collective-permute-start | bytes 3145736 | tf_op jit(solution)/shard_map/ppermute | solution.py:270
  71.8 18.8 %all-to-all-start.2 = ((f32[4,8,4,2,1024]{4,1,3,2,0:T(8,128)}), f32[4,8,4,2,1024]{4,1,3,2,0:T(8,128)S(1)}, u32[]{:S(2)}, u32[]{:S(2)}) async-start(f32[4,8,4,2,1024]{4,1,3,2,0:T(8,128)} %bitcast_add_fusion), calls=%async_computation.2 | async-start | bytes 2097152 | tf_op jit(solution)/shard_map/all_to_all | solution.py:272
  90.6 10.9 %all-to-all-start.1 = ((bf16[32,24,256]{2,1,0:T(8,128)(2,1)}), bf16[32,24,256]{2,1,0:T(8,128)(2,1)S(1)}, u32[]{:S(2)}, u32[]{:S(2)}) async-start(bf16[32,24,256]{2,1,0:T(8,128)(2,1)} %copy.58), calls=%async_computation.1 | async-start | bytes 786432 | tf_op jit(solution)/shard_map/all_to_all | solution.py:252
  101.5 14.4 %all-to-all-start.3 = ((f32[8,4,2,1024]{3,2,1,0:T(2,128)}), f32[8,4,2,1024]{3,2,1,0:T(2,128)S(1)}, u32[]{:S(2)}, u32[]{:S(2)}) async-start(f32[8,4,2,1024]{3,2,1,0:T(2,128)} %copy.63), calls=%async_computation.3 | async-start | bytes 524288 | tf_op jit(solution)/shard_map/all_to_all | solution.py:272
  116.6 9.3 %all-to-all-start.4 = ((f32[4,4,2,1024]{3,1,2,0:T(4,128)}), f32[4,4,2,1024]{3,1,2,0:T(4,128)S(1)}, u32[]{:S(2)}, u32[]{:S(2)}) async-start(f32[4,4,2,1024]{3,1,2,0:T(4,128)} %broadcast_in_dim.74), calls=%async_computation.4 | async-start | bytes 262144 | tf_op jit(solution)/shard_map/all_to_all | solution.py:66
  120.0 13.7 %collective-permute-start.3 = (bf16[8,2,24,256]{3,0,2,1:T(8,128)(2,1)S(1)}, bf16[8,2,24,256]{3,0,2,1:T(8,128)(2,1)S(1)}, u32[]{:S(2)}, u32[]{:S(2)}) collective-permute-start(bf16[8,2,24,256]{3,0,2,1:T(8,128)(2,1)S(1)} %get-tuple-element.24), channel_id=1, source_target_pairs={{1,0},{2,1},{3,2},{4,3},{5,4},{6,5},{7,6},{8,7},{9,8},{10,9},{11,1... | collective-permute-start | bytes 589832 | tf_op jit(solution)/shard_map/ppermute | solution.py:90
  121.9 11.8 %collective-permute-start.2 = (bf16[8,2,24,256]{3,0,2,1:T(8,128)(2,1)S(1)}, bf16[8,2,24,256]{3,0,2,1:T(8,128)(2,1)S(1)}, u32[]{:S(2)}, u32[]{:S(2)}) collective-permute-start(bf16[8,2,24,256]{3,0,2,1:T(8,128)(2,1)S(1)} %get-tuple-element.23), channel_id=1, source_target_pairs={{0,1},{1,2},{2,3},{3,4},{4,5},{5,6},{6,7},{7,8},{8,9},{9,10},{10,1... | collective-permute-start | bytes 589832 | tf_op jit(solution)/shard_map/ppermute | solution.py:88
  127.8 14.5 %all-to-all-start.5 = ((f32[64,1,128]{2,1,0:T(1,128)}), f32[64,1,128]{2,1,0:T(1,128)S(1)}, u32[]{:S(2)}, u32[]{:S(2)}) async-start(f32[64,1,128]{2,1,0:T(1,128)} %broadcast_in_dim_broadcast_in_dim_broadcast_in_dim.2), calls=%async_computation.5 | async-start | bytes 65536 | tf_op jit(solution)/shard_map/all_to_all | solution.py:66

commit v9 on v7

--- a/solution.py
+++ b/solution.py
@@ -5,9 +5,10 @@
 import jax.numpy as jnp
 from jax import lax
 from jax.experimental import pallas as pl
-from jax.sharding import PartitionSpec as P
+from jax.sharding import Mesh, PartitionSpec as P
 
 HEADS = 8
+TILE = ("x2", "x1", "z4", "z2", "z1", "core")
 MAXOFF = 2
 
 
@@ -34,7 +35,7 @@
     return {b: t for b, t in pairs.items() if b < bits and t < bits}
 
 
-def halving_sum(pieces, axis, bit_order, twins):
+def halving_sum(pieces, axis, bit_order, twins, keep_bits=False):
     count = lax.axis_size(axis)
     me = lax.axis_index(axis)
     bits = axis_bits(axis)
@@ -56,7 +57,7 @@
         send = jnp.where(mine == 1, low, high)
         pairs = [(i, i ^ (1 << (twin if i & 1 else bit))) for i in range(count)]
         x = keep + lax.ppermute(send, axis, pairs)
-    return x.reshape(rest)
+    return x if keep_bits else x.reshape(rest)
 
 
 def gather_sum(x, axis):
@@ -198,7 +199,7 @@
     )(valid_row, qkv, d_attended)
 
 
-def body(feats, types, valid, offsets, w_qkv, w_out, d_out):
+def body(TILE, feats, types, valid, offsets, w_qkv, w_out, d_out):
     f32 = jnp.float32
     bf16 = jnp.bfloat16
     highest = lax.Precision.HIGHEST
@@ -206,7 +207,7 @@
     agents = own_count * lax.axis_size("agent")
     first_agent = lax.axis_index("agent") * own_count
     own_offsets = lax.dynamic_slice_in_dim(offsets, first_agent, own_count, 0)
-    rimmed = with_halo(feats, (("tile", 1),), MAXOFF)
+    rimmed = with_halo(feats, ((TILE, 1),), MAXOFF)
     warped = relocate(rimmed, own_offsets, 1)
     cell_count = row_count * col_count
     head_size = channels // HEADS
@@ -255,17 +256,36 @@
         "tgac,sgae->scte", feats_typed, d_split, preferred_element_type=f32
     )
     raw_qkv = qkv_terms[0] + qkv_terms[1]
-    rimmed_grad = with_halo(d_warped, (("tile", 1),), MAXOFF)
+    rimmed_grad = with_halo(d_warped, ((TILE, 1),), MAXOFF)
     d_feats = relocate(rimmed_grad, own_offsets, -1)
     norm_limit = math.sqrt(8.0 * channels * channels)
     raw_all = jnp.concatenate([raw_qkv, raw_out], axis=-1)
-    tiles = lax.axis_size("tile")
+    tiles = lax.axis_size(TILE)
     share_rows = channels // tiles
     pieces = raw_all.reshape(tiles, share_rows, 2, 4 * channels)
-    share_all = halving_sum(pieces, "tile", tile_bit_order(tiles), tile_twins(tiles))
+    order = tile_bit_order(tiles)
+    twins = tile_twins(tiles)
+    head = order[:3]
+    tail = sorted(order[3:], reverse=True)
+    share_all = halving_sum(pieces, TILE, head, twins, keep_bits=True)
+    if tail:
+        bits = axis_bits(TILE)
+        odd = (lax.axis_index(TILE) & 1) == 1
+        back = list(range(share_all.ndim))
+        for b, t in twins.items():
+            back[bits - 1 - b] = bits - 1 - t
+        share_all = jnp.where(odd, jnp.transpose(share_all, back), share_all)
+        share_all = share_all.reshape((1 << len(tail),) + pieces.shape[1:])
+        held = lax.all_to_all(share_all, tuple(TILE[len(TILE) - 1 - b] for b in tail), 0, 0, tiled=True)
+        total = held[0]
+        for i in range(1, held.shape[0]):
+            total = total + held[i]
+        share_all = total
+    else:
+        share_all = share_all.reshape(pieces.shape[1:])
     share_all = gather_sum(share_all, "agent")
     square_sum = jnp.sum(share_all * share_all).reshape(1, 1)
-    square_sum = gather_sum(jnp.broadcast_to(square_sum, (1, 128)), "tile")[0, 0]
+    square_sum = gather_sum(jnp.broadcast_to(square_sum, (1, 128)), TILE)[0, 0]
     factor = norm_limit / jnp.maximum(jnp.sqrt(square_sum), norm_limit)
     scaled = share_all * factor
     scaled = jnp.transpose(scaled, (1, 0, 2))
@@ -273,19 +293,24 @@
 
 
 def solution(mesh):
+    agents_n, tiles = mesh.devices.shape
+    bits = tiles.bit_length() - 1
+    names = TILE[len(TILE) - bits :]
+    fine = Mesh(mesh.devices.reshape((agents_n,) + (2,) * bits), ("agent",) + names)
+    tile = names
     placed = (
-        P("agent", "tile", None, None),
-        P(),
-        P(),
-        P(),
-        P(),
-        P(),
-        P("agent", "tile", None, None),
+        P("agent", tile, None, None),
+        P(),
+        P(),
+        P(),
+        P(),
+        P(),
+        P("agent", tile, None, None),
     )
     return jax.shard_map(
-        body,
-        mesh=mesh,
+        functools.partial(body, tile),
+        mesh=fine,
         in_specs=placed,
-        out_specs=(P("agent", "tile", None, None), P(None, "tile", None), P(None, "tile", None)),
+        out_specs=(P("agent", tile, None, None), P(None, tile, None), P(None, tile, None)),
         check_vma=False,
     )

time: 144 us -> 145 us (level)
  matrix products: 5.65 us -> 7.32 us
    ppermute x6 -> x3, waiting for transfers between devices: 24.1 us -> 10.6 us  [halving_sum(): x = keep + lax.ppermute(send, axis, pairs)]
    all_to_all x0 -> x1, waiting for transfers between devices: none -> 12.3 us  [body(): lax.all_to_all(share_all, tuple((TILE[len(TILE) - 1 - b] for b in tail)),...]
    all_to_all x0 -> x1, starting transfers between devices: none -> 5.45 us  [body(): lax.all_to_all(share_all, tuple((TILE[len(TILE) - 1 - b] for b in tail)),...]
    ppermute x6 -> x3, starting transfers between devices: 5.2 us -> 0.37 us  [halving_sum(): x = keep + lax.ppermute(send, axis, pairs)]
    dot_general x1, matrix products: 1.42 us -> 3.09 us  [body(): jnp.einsum('sgae,tce->stgac', d_split, w_qkv, preferred_element_type=f32)]
    add x5 -> x3, other arithmetic: 2.98 us -> 2.65 us  [halving_sum(): x = keep + lax.ppermute(send, axis, pairs)]
  transfers between devices with their start and end apart: 14 -> 12, of which waited for: 11 -> 10; matrix products, arithmetic and copies ran while one was open for 6% -> 8% of each run, Pallas kernels for 0% -> 0%
where the time goes in v9:
time: 145 us; the launch traced here: 143 us
  waiting for transfers between devices  51.4 us (35%)
  starting transfers between devices  37.7 us (26%)
  Pallas kernels  19.5 us (13%)
  local copies, waits for them, and re-layouts  13.5 us (9%)
  other arithmetic  12.3 us (8%)
  matrix products  7.32 us (5%)
    pallas_call x1, Pallas kernels, cell_attention(): pl.pallas_call(functools.partial(attention_kernel, block_size), grid=(cel...  19.5 us
    all_to_all x1, waiting for transfers between devices, body(): lax.all_to_all(share_all, tuple((TILE[len(TILE) - 1 - b] for b in tail)),...  12.3 us
    ppermute x3, waiting for transfers between devices, halving_sum(): x = keep + lax.ppermute(send, axis, pairs)  10.6 us
    all_to_all x2, starting transfers between devices, gather_sum(): held = lax.all_to_all(copies, axis, 0, 0, tiled=True)  10.5 us
    ppermute x2, starting transfers between devices, with_halo(): lax.ppermute(head, axis, [((i + 1) % count, i) for i in range(ends)])  9.1 us
    all_to_all x1, waiting for transfers between devices, body(): lax.all_to_all(jnp.concatenate([flat_feats, flat_grads], axis=-1), 'agent...  8.94 us
    all_to_all x2, waiting for transfers between devices, gather_sum(): held = lax.all_to_all(copies, axis, 0, 0, tiled=True)  7.55 us
    ppermute x2, waiting for transfers between devices, with_halo(): lax.ppermute(tail, axis, [(i, (i + 1) % count) for i in range(ends)])  5.93 us
  transfers between devices with their start and end apart: 12, of which 10 were waited for; matrix products, arithmetic and copies ran while one was open for 8% of the time, Pallas kernels for 0%

profile of v9, /device:TPU:2, one launch (start us, length us, event | category | flops | bytes accessed | tf_op | source)
XLA Modules:
  0.0 143.0 jit_solution(10703072581167269311)
XLA Ops:
  0.7 1.3 copy.51
  2.0 7.2 %collective-permute-start.1 = (bf16[8,2,24,256]{3,0,2,1:T(8,128)(2,1)S(1)}, bf16[8,2,24,256]{3,0,2,1:T(8,128)(2,1)S(1)}, u32[]{:S(2)}, u32[]{:S(2)}) collective-permute-start(bf16[8,2,24,256]{3,0,2,1:T(8,128)(2,1)S(1)} %get-tuple-element.24), channel_id=1, source_target_pairs={{1,0},{2,1},{3,2},{4,3},{5,4},{6,5},{7,6},{8,7},{9,8},{10,9},{11,1... | collective-permute-start | bytes 589832 | tf_op jit(solution)/shard_map/ppermute | solution.py:90
  9.2 1.9 %collective-permute-start = (bf16[8,2,24,256]{3,0,2,1:T(8,128)(2,1)S(1)}, bf16[8,2,24,256]{3,0,2,1:T(8,128)(2,1)S(1)}, u32[]{:S(2)}, u32[]{:S(2)}) collective-permute-start(bf16[8,2,24,256]{3,0,2,1:T(8,128)(2,1)S(1)} %get-tuple-element.23), channel_id=1, source_target_pairs={{0,1},{1,2},{2,3},{3,4},{4,5},{5,6},{6,7},{7,8},{8,9},{9,10},{10,1... | collective-permute-start | bytes 589832 | tf_op jit(solution)/shard_map/ppermute | solution.py:88
  11.1 0.2 copy.54
  11.4 0.1 constant_dynamic-slice_fusion
  11.5 0.9 collective-permute-done.1
  12.4 5.9 %collective-permute-done = bf16[8,2,24,256]{3,0,2,1:T(8,128)(2,1)S(1)} collective-permute-done((bf16[8,2,24,256]{3,0,2,1:T(8,128)(2,1)S(1)}, bf16[8,2,24,256]{3,0,2,1:T(8,128)(2,1)S(1)}, u32[]{:S(2)}, u32[]{:S(2)}) %collective-permute-start) | collective-permute-done | bytes 196640 | tf_op jit(solution)/shard_map/ppermute | solution.py:88
  18.3 0.1 fusion.18
  18.4 1.7 %gather_fusion = bf16[8,4,24,256]{3,0,2,1:T(8,128)(2,1)S(1)} fusion(bf16[8,8,28,256]{3,0,2,1:T(8,128)(2,1)S(1)} %fusion.18, s32[8]{0:T(128)S(1)} %get-tuple-element.26), kind=kCustom, calls=%fused_computation | custom fusion | bytes 786560 | tf_op jit(solution)/shard_map/vmap()/gather | solution.py:105
  20.1 0.9 pad_maximum_fusion.1
  21.0 4.5 %all-to-all-start = ((bf16[8,96,512]{2,0,1:T(8,128)(2,1)}), bf16[8,96,512]{2,0,1:T(8,128)(2,1)S(1)}, u32[]{:S(2)}, u32[]{:S(2)}) async-start(bf16[8,96,512]{2,0,1:T(8,128)(2,1)} %pad_maximum_fusion.1), calls=%async_computation | async-start | bytes 1572864 | tf_op jit(solution)/shard_map/all_to_all | solution.py:218
  25.5 0.5 fusion.38.valid_ref
  26.1 8.9 %all-to-all-done = bf16[8,96,512]{2,0,1:T(8,128)(2,1)S(1)} async-done(((bf16[8,96,512]{2,0,1:T(8,128)(2,1)}), bf16[8,96,512]{2,0,1:T(8,128)(2,1)S(1)}, u32[]{:S(2)}, u32[]{:S(2)}) %all-to-all-start) | async-done | bytes 786464 | tf_op jit(solution)/shard_map/all_to_all | solution.py:218
  35.0 0.1 copy.81
  35.1 0.8 convert_bitcast_fusion
  35.9 0.2 copy-done.2
  36.1 0.4 fusion.12
  36.5 1.2 fusion.13.qkv_ref
  37.7 0.8 fusion.29.da_ref
  38.5 19.5 %shard_map.94 = (bf16[24,32,256]{2,1,0:T(8,128)(2,1)}, bf16[2,24,32,768]{3,2,1,0:T(8,128)(2,1)}) custom-call(f32[1,32]{1,0:T(1,128)} %fusion.38.valid_ref, bf16[24,32,768]{2,1,0:T(8,128)(2,1)} %fusion.13.qkv_ref, bf16[24,32,256]{2,1,0:T(8,128)(2,1)} %fusion.29.da_ref), custom_call_target="tpu_custom_call" | custom-call | flops 2415919104 | bytes 4325376 | tf_op jit(solution)/shard_map/pallas_call | solution.py:178
  58.1 1.6 %convolution_bitcast_fusion = f32[256,2,256]{0,2,1:T(8,128)S(1)} fusion(pred[2,32]{1,0:T(4,128)(4,1)S(1)} %pad_add_fusion, bf16[24,32,256]{2,1,0:T(8,128)(2,1)} %get-tuple-element.6, bf16[32,24,512]{2,0,1:T(8,128)(2,1)S(1)} %bitcast.416), kind=kOutput, calls=%fused_computation.18 | convolution fusion | flops 201719808 | bytes 1311232 | tf_op jit(solution)/shard_map/tgac,gae->cte/dot_general | solution.py:243
  59.7 0.2 copy-done.6
  59.9 1.5 %fusion.7 = f32[2,256,2,768]{1,3,2,0:T(8,128)S(1)} fusion(bf16[2,24,32,768]{3,2,1,0:T(8,128)(2,1)S(1)} %copy-done.6, pred[2,32]{1,0:T(4,128)(4,1)S(1)} %pad_add_fusion, bf16[24,32,256]{2,1,0:T(8,128)(2,1)S(1)} %slice_bitcast_fusion.7), kind=kOutput, calls=%fused_computation.11 | convolution fusion | flops 1208352768 | bytes 5898304 | tf_op jit(solution)/shard_map/tgac,sgae->scte/dot_general | solution.py:255
  61.3 0.2 fusion.11
  61.6 1.5 %pad_maximum_fusion = f32[256,2,1024]{0,2,1:T(8,128)} fusion(f32[256,2,256]{0,2,1:T(8,128)S(1)} %convolution_bitcast_fusion, f32[256,2,768]{0,2,1:T(8,128)S(1)} %fusion.11), kind=kLoop, calls=%fused_computation.9 | loop fusion | flops 524288 | bytes 4194304 | tf_op jit(solution)/shard_map/concatenate | solution.py:262
  63.0 2.9 %copy.62 = f32[256,2,1024]{2,1,0:T(2,128)S(1)} copy(f32[256,2,1024]{0,2,1:T(8,128)} %pad_maximum_fusion) | data formatting | bytes 4194304 | tf_op jit(solution)/shard_map/concatenate | solution.py:262
  65.9 1.6 %broadcast_select_fusion = f32[2,2,2,2,2,1,4,2,1024]{8,7,6,5,4,3,2,1,0:T(2,128)} fusion(pred[]{:T(512)S(6)} %eq.34, f32[2,2,2,2,2,2,4,2,1024]{8,7,6,5,4,3,2,1,0:T(2,128)S(1)} %bitcast.411), kind=kLoop, calls=%fused_computation.24 | loop fusion | flops 262144 | bytes 3145729 | tf_op jit(solution)/shard_map/jit(_where)/select_n | solution.py:57
  67.5 3.0 %collective-permute-done.4 = f32[2,2,2,2,2,1,4,2,1024]{8,7,6,5,4,3,2,1,0:T(2,128)} collective-permute-done((f32[2,2,2,2,2,1,4,2,1024]{8,7,6,5,4,3,2,1,0:T(2,128)}, f32[2,2,2,2,2,1,4,2,1024]{8,7,6,5,4,3,2,1,0:T(2,128)}, u32[]{:S(2)}, u32[]{:S(2)}) %collective-permute-start.4) | collective-permute-done | bytes 1048608 | tf_op jit(solution)/shard_map/ppermute | solution.py:59
  70.5 2.0 %select_add_fusion = f32[2,2,2,2,2,1,4,2,1024]{8,7,6,5,4,3,2,1,0:T(2,128)S(1)} fusion(f32[2,2,2,2,2,1,4,2,1024]{8,7,6,5,4,3,2,1,0:T(2,128)} %collective-permute-done.4, pred[]{:T(512)S(6)} %eq.34, f32[2,2,2,2,2,2,4,2,1024]{8,7,6,5,4,3,2,1,0:T(2,128)S(1)} %bitcast.412), kind=kLoop, calls=%fused_computation.23 | loop fusion | flops 524288 | bytes 4194305 | tf_op jit(solution)/shard_map/add | solution.py:59
  72.5 0.4 bitcast_select_fusion
  73.0 0.3 broadcast_select_fusion.1
  73.3 0.1 collective-permute-start.5
  73.4 3.1 %fusion.4 = f32[2,2,24,32,256]{4,3,2,1,0:T(8,128)S(1)} fusion(bf16[2,24,32,768]{3,2,1,0:T(8,128)(2,1)} %get-tuple-element.5, bf16[2,256,768]{2,1,0:T(8,128)(2,1)S(1)} %copy-done), kind=kOutput, calls=%fused_computation.10 | convolution fusion | flops 1207959552 | bytes 6291456 | tf_op jit(solution)/shard_map/sgae,tce->stgac/dot_general | solution.py:246
  76.5 6.1 %collective-permute-done.5 = f32[2,2,2,2,1,1,4,2,1024]{8,7,6,5,4,3,2,1,0:T(2,128)S(1)} collective-permute-done((f32[2,2,2,2,1,1,4,2,1024]{8,7,6,5,4,3,2,1,0:T(2,128)S(1)}, f32[2,2,2,2,1,1,4,2,1024]{8,7,6,5,4,3,2,1,0:T(2,128)S(1)}, u32[]{:S(2)}, u32[]{:S(2)}) %collective-permute-start.5) | collective-permute-done | bytes 524320 | tf_op jit(solution)/shard_map/ppermute | solution.py:59
  82.6 0.4 select_add_fusion.1
  83.0 0.1 broadcast_select_fusion.2
  83.2 0.3 collective-permute-start.6
  83.4 0.2 slice_add_fusion.1
  83.7 0.1 fusion.28
  83.8 1.0 copy.60
  84.8 3.5 %all-to-all-start.1 = ((bf16[32,24,256]{2,1,0:T(8,128)(2,1)}), bf16[32,24,256]{2,1,0:T(8,128)(2,1)S(1)}, u32[]{:S(2)}, u32[]{:S(2)}) async-start(bf16[32,24,256]{2,1,0:T(8,128)(2,1)} %copy.60), calls=%async_computation.1 | async-start | bytes 786432 | tf_op jit(solution)/shard_map/all_to_all | solution.py:252
  88.2 1.6 %collective-permute-done.6 = f32[2,1,2,2,1,1,4,2,1024]{8,7,6,5,4,3,2,1,0:T(2,128)S(1)} collective-permute-done((f32[2,1,2,2,1,1,4,2,1024]{8,7,6,5,4,3,2,1,0:T(2,128)S(1)}, f32[2,1,2,2,1,1,4,2,1024]{8,7,6,5,4,3,2,1,0:T(2,128)S(1)}, u32[]{:S(2)}, u32[]{:S(2)}) %collective-permute-start.6) | collective-permute-done | bytes 262176 | tf_op jit(solution)/shard_map/ppermute | solution.py:59
  89.8 0.2 select_add_fusion.2
  90.0 0.8 bitcast_select_fusion.1
  90.8 5.2 %all-to-all-done.1 = bf16[32,24,256]{2,1,0:T(8,128)(2,1)S(1)} async-done(((bf16[32,24,256]{2,1,0:T(8,128)(2,1)}), bf16[32,24,256]{2,1,0:T(8,128)(2,1)S(1)}, u32[]{:S(2)}, u32[]{:S(2)}) %all-to-all-start.1) | async-done | bytes 393248 | tf_op jit(solution)/shard_map/all_to_all | solution.py:252
  96.0 5.5 %all-to-all-start.2 = ((f32[8,4,2,1024]{3,2,1,0:T(2,128)}), f32[8,4,2,1024]{3,2,1,0:T(2,128)S(1)}, u32[]{:S(2)}, u32[]{:S(2)}) async-start(f32[8,4,2,1024]{3,2,1,0:T(2,128)} %bitcast.49), calls=%async_computation.2 | async-start | bytes 524288 | tf_op jit(solution)/shard_map/all_to_all | solution.py:279
  101.5 0.1 copy.82
  101.5 12.3 %all-to-all-done.2 = f32[8,4,2,1024]{3,2,1,0:T(2,128)S(1)} async-done(((f32[8,4,2,1024]{3,2,1,0:T(2,128)}), f32[8,4,2,1024]{3,2,1,0:T(2,128)S(1)}, u32[]{:S(2)}, u32[]{:S(2)}) %all-to-all-start.2) | async-done | bytes 262176 | tf_op jit(solution)/shard_map/all_to_all | solution.py:279
  113.8 0.1 fusion.37
  113.9 0.7 broadcast_in_dim.74
  114.6 3.3 %all-to-all-start.3 = ((f32[4,4,2,1024]{3,1,2,0:T(4,128)}), f32[4,4,2,1024]{3,1,2,0:T(4,128)S(1)}, u32[]{:S(2)}, u32[]{:S(2)}) async-start(f32[4,4,2,1024]{3,1,2,0:T(4,128)} %broadcast_in_dim.74), calls=%async_computation.3 | async-start | bytes 262144 | tf_op jit(solution)/shard_map/all_to_all | solution.py:66
  118.0 1.9 %collective-permute-start.3 = (bf16[8,2,24,256]{3,0,2,1:T(8,128)(2,1)S(1)}, bf16[8,2,24,256]{3,0,2,1:T(8,128)(2,1)S(1)}, u32[]{:S(2)}, u32[]{:S(2)}) collective-permute-start(bf16[8,2,24,256]{3,0,2,1:T(8,128)(2,1)S(1)} %get-tuple-element.22), channel_id=1, source_target_pairs={{1,0},{2,1},{3,2},{4,3},{5,4},{6,5},{7,6},{8,7},{9,8},{10,9},{11,1... | collective-permute-start | bytes 589832 | tf_op jit(solution)/shard_map/ppermute | solution.py:90
  119.9 2.4 %collective-permute-start.2 = (bf16[8,2,24,256]{3,0,2,1:T(8,128)(2,1)S(1)}, bf16[8,2,24,256]{3,0,2,1:T(8,128)(2,1)S(1)}, u32[]{:S(2)}, u32[]{:S(2)}) collective-permute-start(bf16[8,2,24,256]{3,0,2,1:T(8,128)(2,1)S(1)} %get-tuple-element.21), channel_id=1, source_target_pairs={{0,1},{1,2},{2,3},{3,4},{4,5},{5,6},{6,7},{7,8},{8,9},{9,10},{10,1... | collective-permute-start | bytes 589832 | tf_op jit(solution)/shard_map/ppermute | solution.py:88
  122.3 1.6 %all-to-all-done.3 = f32[4,4,2,1024]{3,1,2,0:T(4,128)S(1)} async-done(((f32[4,4,2,1024]{3,1,2,0:T(4,128)}), f32[4,4,2,1024]{3,1,2,0:T(4,128)S(1)}, u32[]{:S(2)}, u32[]{:S(2)}) %all-to-all-start.3) | async-done | bytes 131104 | tf_op jit(solution)/shard_map/all_to_all | solution.py:66
  123.9 0.6 multiply_reduce_fusion
  124.5 1.3 broadcast_in_dim_broadcast_in_dim_broadcast_in_dim.2
  125.7 7.2 %all-to-all-start.4 = ((f32[64,1,128]{2,1,0:T(1,128)}), f32[64,1,128]{2,1,0:T(1,128)S(1)}, u32[]{:S(2)}, u32[]{:S(2)}) async-start(f32[64,1,128]{2,1,0:T(1,128)} %broadcast_in_dim_broadcast_in_dim_broadcast_in_dim.2), calls=%async_computation.4 | async-start | bytes 65536 | tf_op jit(solution)/shard_map/all_to_all | solution.py:66
  133.0 0.1 select_maximum_fusion
  133.1 1.7 %gather_fusion.1 = bf16[8,4,24,256]{3,0,2,1:T(8,128)(2,1)S(1)} fusion(bf16[8,8,28,256]{3,0,2,1:T(8,128)(2,1)S(1)} %select_maximum_fusion, s32[8]{0:T(128)S(1)} %get-tuple-element.25), kind=kCustom, calls=%fused_computation.1 | custom fusion | bytes 786560 | tf_op jit(solution)/shard_map/vmap()/gather | solution.py:105
  134.8 0.8 copy.66
  135.6 6.0 %all-to-all-done.4 = f32[64,1,128]{2,1,0:T(1,128)S(1)} async-done(((f32[64,1,128]{2,1,0:T(1,128)}), f32[64,1,128]{2,1,0:T(1,128)S(1)}, u32[]{:S(2)}, u32[]{:S(2)}) %all-to-all-start.4) | async-done | bytes 32800 | tf_op jit(solution)/shard_map/all_to_all | solution.py:66
  141.6 0.1 fusion.43
  141.8 0.6 slice.522
  142.4 0.6 slice.523
  (23 shorter events, 0.2 us)
Async XLA Ops:
  0.6 34.5 %copy-start = (bf16[2,256,768]{2,1,0:T(8,128)(2,1)S(1)}, bf16[2,256,768]{2,1,0:T(8,128)(2,1)}, u32[]{:S(2)}) copy-start(bf16[2,256,768]{2,1,0:T(8,128)(2,1)} %param.11) | copy-start | bytes 2359300
  0.6 10.5 %copy-start.1 = (bf16[8,4,24,256]{3,2,1,0:T(8,128)(2,1)S(1)}, bf16[8,4,24,256]{3,2,1,0:T(8,128)(2,1)}, u32[]{:S(2)}) copy-start(bf16[8,4,24,256]{3,2,1,0:T(8,128)(2,1)} %param.13) | copy-start | bytes 1179652
  0.7 10.7 %copy-start.3 = (s32[32,2]{0,1:T(2,128)S(1)}, s32[32,2]{0,1:T(2,128)}, u32[]{:S(2)}) copy-start(s32[32,2]{0,1:T(2,128)} %param.10) | copy-start | bytes 772
  2.0 10.3 %collective-permute-start.1 = (bf16[8,2,24,256]{3,0,2,1:T(8,128)(2,1)S(1)}, bf16[8,2,24,256]{3,0,2,1:T(8,128)(2,1)S(1)}, u32[]{:S(2)}, u32[]{:S(2)}) collective-permute-start(bf16[8,2,24,256]{3,0,2,1:T(8,128)(2,1)S(1)} %get-tuple-element.24), channel_id=1, source_target_pairs={{1,0},{2,1},{3,2},{4,3},{5,4},{6,5},{7,6},{8,7},{9,8},{10,9},{11,1... | collective-permute-start | bytes 589832 | tf_op jit(solution)/shard_map/ppermute | solution.py:90
  9.2 9.1 %collective-permute-start = (bf16[8,2,24,256]{3,0,2,1:T(8,128)(2,1)S(1)}, bf16[8,2,24,256]{3,0,2,1:T(8,128)(2,1)S(1)}, u32[]{:S(2)}, u32[]{:S(2)}) collective-permute-start(bf16[8,2,24,256]{3,0,2,1:T(8,128)(2,1)S(1)} %get-tuple-element.23), channel_id=1, source_target_pairs={{0,1},{1,2},{2,3},{3,4},{4,5},{5,6},{6,7},{7,8},{8,9},{9,10},{10,1... | collective-permute-start | bytes 589832 | tf_op jit(solution)/shard_map/ppermute | solution.py:88
  20.1 5.4 %copy-start.4 = (s32[32]{0:T(128)S(1)}, s32[32]{0:T(128)}, u32[]{:S(2)}) copy-start(s32[32]{0:T(128)} %param.8) | copy-start | bytes 388
  20.1 5.5 %copy-start.5 = (s32[32]{0:T(128)S(1)}, s32[32]{0:T(128)}, u32[]{:S(2)}) copy-start(s32[32]{0:T(128)} %param.9) | copy-start | bytes 388
  21.0 14.0 %all-to-all-start = ((bf16[8,96,512]{2,0,1:T(8,128)(2,1)}), bf16[8,96,512]{2,0,1:T(8,128)(2,1)S(1)}, u32[]{:S(2)}, u32[]{:S(2)}) async-start(bf16[8,96,512]{2,0,1:T(8,128)(2,1)} %pad_maximum_fusion.1), calls=%async_computation | async-start | bytes 1572864 | tf_op jit(solution)/shard_map/all_to_all | solution.py:218
  35.1 1.0 copy-start.2
  58.1 1.8 %copy-start.6 = (bf16[2,24,32,768]{3,2,1,0:T(8,128)(2,1)S(1)}, bf16[2,24,32,768]{3,2,1,0:T(8,128)(2,1)}, u32[]{:S(2)}) copy-start(bf16[2,24,32,768]{3,2,1,0:T(8,128)(2,1)} %get-tuple-element.5) | copy-start | bytes 7077892
  67.5 3.0 %collective-permute-start.4 = (f32[2,2,2,2,2,1,4,2,1024]{8,7,6,5,4,3,2,1,0:T(2,128)}, f32[2,2,2,2,2,1,4,2,1024]{8,7,6,5,4,3,2,1,0:T(2,128)}, u32[]{:S(2)}, u32[]{:S(2)}) collective-permute-start(f32[2,2,2,2,2,1,4,2,1024]{8,7,6,5,4,3,2,1,0:T(2,128)} %broadcast_select_fusion), channel_id=1, source_target_pairs={{0,1},{1,0},{2,3},{3,2},{4,5},{5,4},{6,7},{7,6},{8,9},{9,8},{10,11... | collective-permute-start | bytes 3145736 | tf_op jit(solution)/shard_map/ppermute | solution.py:59
  73.3 9.3 %collective-permute-start.5 = (f32[2,2,2,2,1,1,4,2,1024]{8,7,6,5,4,3,2,1,0:T(2,128)S(1)}, f32[2,2,2,2,1,1,4,2,1024]{8,7,6,5,4,3,2,1,0:T(2,128)S(1)}, u32[]{:S(2)}, u32[]{:S(2)}) collective-permute-start(f32[2,2,2,2,1,1,4,2,1024]{8,7,6,5,4,3,2,1,0:T(2,128)S(1)} %broadcast_select_fusion.1), channel_id=1, source_target_pairs={{0,2},{1,17},{2,0},{3,19},{4,6},{5,21},{6,4},{7,23},{8,10},{9,25},... | collective-permute-start | bytes 1572872 | tf_op jit(solution)/shard_map/ppermute | solution.py:59
  83.2 6.6 %collective-permute-start.6 = (f32[2,1,2,2,1,1,4,2,1024]{8,7,6,5,4,3,2,1,0:T(2,128)S(1)}, f32[2,1,2,2,1,1,4,2,1024]{8,7,6,5,4,3,2,1,0:T(2,128)S(1)}, u32[]{:S(2)}, u32[]{:S(2)}) collective-permute-start(f32[2,1,2,2,1,1,4,2,1024]{8,7,6,5,4,3,2,1,0:T(2,128)S(1)} %broadcast_select_fusion.2), channel_id=1, source_target_pairs={{0,16},{1,3},{2,18},{3,1},{4,20},{5,7},{6,22},{7,5},{8,24},{9,11},... | collective-permute-start | bytes 786440 | tf_op jit(solution)/shard_map/ppermute | solution.py:59
  84.8 11.2 %all-to-all-start.1 = ((bf16[32,24,256]{2,1,0:T(8,128)(2,1)}), bf16[32,24,256]{2,1,0:T(8,128)(2,1)S(1)}, u32[]{:S(2)}, u32[]{:S(2)}) async-start(bf16[32,24,256]{2,1,0:T(8,128)(2,1)} %copy.60), calls=%async_computation.1 | async-start | bytes 786432 | tf_op jit(solution)/shard_map/all_to_all | solution.py:252
  96.0 17.8 %all-to-all-start.2 = ((f32[8,4,2,1024]{3,2,1,0:T(2,128)}), f32[8,4,2,1024]{3,2,1,0:T(2,128)S(1)}, u32[]{:S(2)}, u32[]{:S(2)}) async-start(f32[8,4,2,1024]{3,2,1,0:T(2,128)} %bitcast.49), calls=%async_computation.2 | async-start | bytes 524288 | tf_op jit(solution)/shard_map/all_to_all | solution.py:279
  114.6 9.3 %all-to-all-start.3 = ((f32[4,4,2,1024]{3,1,2,0:T(4,128)}), f32[4,4,2,1024]{3,1,2,0:T(4,128)S(1)}, u32[]{:S(2)}, u32[]{:S(2)}) async-start(f32[4,4,2,1024]{3,1,2,0:T(4,128)} %broadcast_in_dim.74), calls=%async_computation.3 | async-start | bytes 262144 | tf_op jit(solution)/shard_map/all_to_all | solution.py:66
  118.0 15.0 %collective-permute-start.3 = (bf16[8,2,24,256]{3,0,2,1:T(8,128)(2,1)S(1)}, bf16[8,2,24,256]{3,0,2,1:T(8,128)(2,1)S(1)}, u32[]{:S(2)}, u32[]{:S(2)}) collective-permute-start(bf16[8,2,24,256]{3,0,2,1:T(8,128)(2,1)S(1)} %get-tuple-element.22), channel_id=1, source_target_pairs={{1,0},{2,1},{3,2},{4,3},{5,4},{6,5},{7,6},{8,7},{9,8},{10,9},{11,1... | collective-permute-start | bytes 589832 | tf_op jit(solution)/shard_map/ppermute | solution.py:90
  119.9 13.1 %collective-permute-start.2 = (bf16[8,2,24,256]{3,0,2,1:T(8,128)(2,1)S(1)}, bf16[8,2,24,256]{3,0,2,1:T(8,128)(2,1)S(1)}, u32[]{:S(2)}, u32[]{:S(2)}) collective-permute-start(bf16[8,2,24,256]{3,0,2,1:T(8,128)(2,1)S(1)} %get-tuple-element.21), channel_id=1, source_target_pairs={{0,1},{1,2},{2,3},{3,4},{4,5},{5,6},{6,7},{7,8},{8,9},{9,10},{10,1... | collective-permute-start | bytes 589832 | tf_op jit(solution)/shard_map/ppermute | solution.py:88
  125.7 15.8 %all-to-all-start.4 = ((f32[64,1,128]{2,1,0:T(1,128)}), f32[64,1,128]{2,1,0:T(1,128)S(1)}, u32[]{:S(2)}, u32[]{:S(2)}) async-start(f32[64,1,128]{2,1,0:T(1,128)} %broadcast_in_dim_broadcast_in_dim_broadcast_in_dim.2), calls=%async_computation.4 | async-start | bytes 65536 | tf_op jit(solution)/shard_map/all_to_all | solution.py:66

commit v10 on v7

--- a/solution.py
+++ b/solution.py
@@ -258,17 +258,17 @@
     rimmed_grad = with_halo(d_warped, (("tile", 1),), MAXOFF)
     d_feats = relocate(rimmed_grad, own_offsets, -1)
     norm_limit = math.sqrt(8.0 * channels * channels)
-    raw_all = jnp.concatenate([raw_qkv, raw_out], axis=-1)
+    raw_all = jnp.concatenate([raw_qkv[:, 0], raw_out[:, 0], raw_qkv[:, 1], raw_out[:, 1]], axis=-1)
     tiles = lax.axis_size("tile")
     share_rows = channels // tiles
-    pieces = raw_all.reshape(tiles, share_rows, 2, 4 * channels)
+    pieces = raw_all.reshape(tiles, share_rows, 2 * 4 * channels)
     share_all = halving_sum(pieces, "tile", tile_bit_order(tiles), tile_twins(tiles))
     share_all = gather_sum(share_all, "agent")
     square_sum = jnp.sum(share_all * share_all).reshape(1, 1)
     square_sum = gather_sum(jnp.broadcast_to(square_sum, (1, 128)), "tile")[0, 0]
     factor = norm_limit / jnp.maximum(jnp.sqrt(square_sum), norm_limit)
     scaled = share_all * factor
-    scaled = jnp.transpose(scaled, (1, 0, 2))
+    scaled = jnp.transpose(scaled.reshape(share_rows, 2, 4 * channels), (1, 0, 2))
     return (d_feats, scaled[..., : 3 * channels], scaled[..., 3 * channels :])
 
 

time: 144 us -> 149 us (1.035)
  local copies, waits for them, and re-layouts: 13.5 us -> 19.4 us
  other arithmetic: 12.1 us -> 8.85 us
  matrix products: 5.65 us -> 7.3 us
    unnamed x19 -> x24, local copies, waits for them, and re-layouts: 2.74 us -> 5.27 us
    dot_general x1, matrix products: 1.48 us -> 3.22 us  [body(): jnp.einsum('tgac,sgae->scte', feats_typed, d_split, preferred_element_typ...]
    slice x0 -> x2, local copies, waits for them, and re-layouts: none -> 1.72 us  [the longest x1 0.99 us: body(): raw_qkv[:, 1]]
    concatenate x1 -> x5, local copies, waits for them, and re-layouts: 2.92 us -> 4.55 us  [body(): jnp.concatenate([raw_qkv[:, 0], raw_out[:, 0], raw_qkv[:, 1], raw_out[:,...]
where the time goes in v10:
time: 149 us; the launch traced here: 146 us
  waiting for transfers between devices  52.4 us (35%)
  starting transfers between devices  37.6 us (25%)
  Pallas kernels  19.5 us (13%)
  local copies, waits for them, and re-layouts  19.4 us (13%)
  other arithmetic  8.85 us (6%)
  matrix products  7.3 us (5%)
    ppermute x6, waiting for transfers between devices, halving_sum(): x = keep + lax.ppermute(send, axis, pairs)  24 us
    pallas_call x1, Pallas kernels, cell_attention(): pl.pallas_call(functools.partial(attention_kernel, block_size), grid=(cel...  19.5 us
    all_to_all x2, starting transfers between devices, gather_sum(): held = lax.all_to_all(copies, axis, 0, 0, tiled=True)  11.1 us
    ppermute x2, starting transfers between devices, with_halo(): lax.ppermute(head, axis, [((i + 1) % count, i) for i in range(ends)])  9.1 us
    all_to_all x1, waiting for transfers between devices, body(): lax.all_to_all(jnp.concatenate([flat_feats, flat_grads], axis=-1), 'agent...  8.94 us
    all_to_all x2, waiting for transfers between devices, gather_sum(): held = lax.all_to_all(copies, axis, 0, 0, tiled=True)  7.55 us
    ppermute x2, waiting for transfers between devices, with_halo(): lax.ppermute(tail, axis, [(i, (i + 1) % count) for i in range(ends)])  5.93 us
    unnamed x24, local copies, waits for them, and re-layouts  5.27 us
  transfers between devices with their start and end apart: 14, of which 11 were waited for; matrix products, arithmetic and copies ran while one was open for 6% of the time, Pallas kernels for 0%

profile of v10, /device:TPU:2, one launch (start us, length us, event | category | flops | bytes accessed | tf_op | source)
XLA Modules:
  0.0 146.4 jit_solution(16830091690941578068)
XLA Ops:
  0.7 1.3 copy.56
  2.0 7.2 %collective-permute-start.1 = (bf16[8,2,24,256]{3,0,2,1:T(8,128)(2,1)S(1)}, bf16[8,2,24,256]{3,0,2,1:T(8,128)(2,1)S(1)}, u32[]{:S(2)}, u32[]{:S(2)}) collective-permute-start(bf16[8,2,24,256]{3,0,2,1:T(8,128)(2,1)S(1)} %get-tuple-element.31), channel_id=1, source_target_pairs={{1,0},{2,1},{3,2},{4,3},{5,4},{6,5},{7,6},{8,7},{9,8},{10,9},{11,1... | collective-permute-start | bytes 589832 | tf_op jit(solution)/shard_map/ppermute | solution.py:89
  9.2 1.9 %collective-permute-start = (bf16[8,2,24,256]{3,0,2,1:T(8,128)(2,1)S(1)}, bf16[8,2,24,256]{3,0,2,1:T(8,128)(2,1)S(1)}, u32[]{:S(2)}, u32[]{:S(2)}) collective-permute-start(bf16[8,2,24,256]{3,0,2,1:T(8,128)(2,1)S(1)} %get-tuple-element.30), channel_id=1, source_target_pairs={{0,1},{1,2},{2,3},{3,4},{4,5},{5,6},{6,7},{7,8},{8,9},{9,10},{10,1... | collective-permute-start | bytes 589832 | tf_op jit(solution)/shard_map/ppermute | solution.py:87
  11.1 0.2 copy.59
  11.5 0.9 collective-permute-done.1
  12.4 5.9 %collective-permute-done = bf16[8,2,24,256]{3,0,2,1:T(8,128)(2,1)S(1)} collective-permute-done((bf16[8,2,24,256]{3,0,2,1:T(8,128)(2,1)S(1)}, bf16[8,2,24,256]{3,0,2,1:T(8,128)(2,1)S(1)}, u32[]{:S(2)}, u32[]{:S(2)}) %collective-permute-start) | collective-permute-done | bytes 196640 | tf_op jit(solution)/shard_map/ppermute | solution.py:87
  18.4 1.7 %gather_fusion = bf16[8,4,24,256]{3,0,2,1:T(8,128)(2,1)S(1)} fusion(bf16[8,8,28,256]{3,0,2,1:T(8,128)(2,1)S(1)} %fusion.18, s32[8]{0:T(128)S(1)} %get-tuple-element.33), kind=kCustom, calls=%fused_computation | custom fusion | bytes 786560 | tf_op jit(solution)/shard_map/vmap()/gather | solution.py:104
  20.1 1.0 pad_maximum_fusion
  21.1 4.5 %all-to-all-start = ((bf16[8,96,512]{2,0,1:T(8,128)(2,1)}), bf16[8,96,512]{2,0,1:T(8,128)(2,1)S(1)}, u32[]{:S(2)}, u32[]{:S(2)}) async-start(bf16[8,96,512]{2,0,1:T(8,128)(2,1)} %pad_maximum_fusion), calls=%async_computation | async-start | bytes 1572864 | tf_op jit(solution)/shard_map/all_to_all | solution.py:217
  25.6 0.5 fusion.37.valid_ref
  26.1 8.9 %all-to-all-done = bf16[8,96,512]{2,0,1:T(8,128)(2,1)S(1)} async-done(((bf16[8,96,512]{2,0,1:T(8,128)(2,1)}), bf16[8,96,512]{2,0,1:T(8,128)(2,1)S(1)}, u32[]{:S(2)}, u32[]{:S(2)}) %all-to-all-start) | async-done | bytes 786464 | tf_op jit(solution)/shard_map/all_to_all | solution.py:217
  35.0 0.1 copy.82
  35.2 0.8 convert_bitcast_fusion
  36.0 0.3 copy-done.3
  36.3 0.4 fusion.12
  36.7 1.2 fusion.13.qkv_ref
  37.9 0.8 fusion.29.da_ref
  38.8 19.5 %shard_map.94 = (bf16[24,32,256]{2,1,0:T(8,128)(2,1)}, bf16[2,24,32,768]{3,2,1,0:T(8,128)(2,1)}) custom-call(f32[1,32]{1,0:T(1,128)} %fusion.37.valid_ref, bf16[24,32,768]{2,1,0:T(8,128)(2,1)} %fusion.13.qkv_ref, bf16[24,32,256]{2,1,0:T(8,128)(2,1)} %fusion.29.da_ref), custom_call_target="tpu_custom_call" | custom-call | flops 2415919104 | bytes 4325376 | tf_op jit(solution)/shard_map/pallas_call | solution.py:177
  58.3 3.2 %fusion.7 = f32[2,256,2,768]{3,1,2,0:T(8,128)S(1)} fusion(bf16[2,24,32,768]{3,2,1,0:T(8,128)(2,1)} %get-tuple-element.5, pred[2,32]{1,0:T(4,128)(4,1)S(1)} %pad_add_fusion, bf16[24,32,256]{2,1,0:T(8,128)(2,1)S(1)} %slice_bitcast_fusion.7), kind=kOutput, calls=%fused_computation.10 | convolution fusion | flops 1208352768 | bytes 5898304 | tf_op jit(solution)/shard_map/tgac,sgae->scte/dot_general | solution.py:254
  61.5 0.2 fusion.11
  61.7 1.0 fusion.93
  62.7 1.2 concatenate.32
  63.9 1.2 constant_dynamic-update-slice_fusion.3
  65.1 1.5 %convolution_bitcast_fusion = f32[256,2,256]{2,0,1:T(8,128)S(1)} fusion(pred[2,32]{1,0:T(4,128)(4,1)S(1)} %pad_add_fusion, bf16[24,32,256]{2,1,0:T(8,128)(2,1)S(1)} %copy-done.8, bf16[32,24,512]{2,0,1:T(8,128)(2,1)} %bitcast.417), kind=kOutput, calls=%fused_computation.17 | convolution fusion | flops 201719808 | bytes 1310784 | tf_op jit(solution)/shard_map/tgac,gae->cte/dot_general | solution.py:242
  66.6 0.7 fusion.94
  67.3 0.1 concatenate.33
  67.4 2.3 %concatenate.34 = f32[2,2,2,2,2,2,4,768]{7,6,5,4,3,2,1,0:T(4,128)} reshape(f32[256,1,768]{2,0,1:T(8,128)} %get-tuple-element.24) | data formatting | bytes 1572864 | tf_op jit(solution)/shard_map/concatenate | solution.py:261
  69.7 1.0 concatenate.35
  70.8 1.2 constant_dynamic-update-slice_fusion.1
  72.1 1.3 slice_select_fusion
  73.3 3.0 %collective-permute-done.4 = f32[2,2,2,2,2,1,4,2048]{7,6,5,4,3,2,1,0:T(4,128)} collective-permute-done((f32[2,2,2,2,2,1,4,2048]{7,6,5,4,3,2,1,0:T(4,128)}, f32[2,2,2,2,2,1,4,2048]{7,6,5,4,3,2,1,0:T(4,128)}, u32[]{:S(2)}, u32[]{:S(2)}) %collective-permute-start.4) | collective-permute-done | bytes 1048608 | tf_op jit(solution)/shard_map/ppermute | solution.py:58
  76.3 1.7 %select_add_fusion = f32[2,2,2,2,2,1,4,2048]{7,6,5,4,3,2,1,0:T(4,128)S(1)} fusion(f32[2,2,2,2,2,1,4,2048]{7,6,5,4,3,2,1,0:T(4,128)} %collective-permute-done.4, f32[2,2,2,2,2,2,4,2048]{7,6,5,4,3,2,1,0:T(4,128)S(1)} %constant_dynamic-update-slice_fusion, pred[]{:T(512)S(6)} %eq.48), kind=kLoop, calls=%fused_computation.22 | loop fusion | flops 524288 | bytes 4194305 | tf_op jit(solution)/shard_map/add | solution.py:58
  78.1 0.2 bitcast_select_fusion
  78.3 0.2 slice_select_fusion.1
  78.5 0.1 collective-permute-start.5
  78.6 9.1 %collective-permute-done.5 = f32[2,2,2,2,1,1,4,2048]{7,6,5,4,3,2,1,0:T(4,128)S(1)} collective-permute-done((f32[2,2,2,2,1,1,4,2048]{7,6,5,4,3,2,1,0:T(4,128)S(1)}, f32[2,2,2,2,1,1,4,2048]{7,6,5,4,3,2,1,0:T(4,128)S(1)}, u32[]{:S(2)}, u32[]{:S(2)}) %collective-permute-start.5) | collective-permute-done | bytes 524320 | tf_op jit(solution)/shard_map/ppermute | solution.py:58
  87.7 0.2 select_add_fusion.1
  88.0 0.1 collective-permute-start.6
  88.1 1.4 fusion.4
  89.6 4.9 %collective-permute-done.6 = f32[2,1,2,2,1,1,4,2048]{7,6,5,4,3,2,1,0:T(4,128)S(1)} collective-permute-done((f32[2,1,2,2,1,1,4,2048]{7,6,5,4,3,2,1,0:T(4,128)S(1)}, f32[2,1,2,2,1,1,4,2048]{7,6,5,4,3,2,1,0:T(4,128)S(1)}, u32[]{:S(2)}, u32[]{:S(2)}) %collective-permute-start.6) | collective-permute-done | bytes 262176 | tf_op jit(solution)/shard_map/ppermute | solution.py:58
  94.5 0.1 select_add_fusion.2
  94.6 0.3 collective-permute-start.7
  94.9 0.3 slice_add_fusion.1
  95.2 6.4 %collective-permute-done.7 = f32[2,1,2,1,1,1,4,2048]{7,6,5,4,3,2,1,0:T(4,128)S(1)} collective-permute-done((f32[2,1,2,1,1,1,4,2048]{7,6,5,4,3,2,1,0:T(4,128)S(1)}, f32[2,1,2,1,1,1,4,2048]{7,6,5,4,3,2,1,0:T(4,128)S(1)}, u32[]{:S(2)}, u32[]{:S(2)}) %collective-permute-start.7) | collective-permute-done | bytes 131104 | tf_op jit(solution)/shard_map/ppermute | solution.py:58
  101.7 2.5 %collective-permute-start.8 = (f32[1,1,2,1,1,1,4,2048]{7,6,5,4,3,2,1,0:T(4,128)S(1)}, f32[1,1,2,1,1,1,4,2048]{7,6,5,4,3,2,1,0:T(4,128)S(1)}, u32[]{:S(2)}, u32[]{:S(2)}) collective-permute-start(f32[1,1,2,1,1,1,4,2048]{7,6,5,4,3,2,1,0:T(4,128)S(1)} %slice_select_fusion.4), channel_id=1, source_target_pairs={{0,32},{1,5},{2,34},{3,7},{4,36},{5,1},{6,38},{7,3},{8,40},{9,13},... | collective-permute-start | bytes 196616 | tf_op jit(solution)/shard_map/ppermute | solution.py:58
  104.2 0.1 fusion.28
  104.3 1.0 copy.65
  105.3 3.5 %all-to-all-start.1 = ((bf16[32,24,256]{2,1,0:T(8,128)(2,1)}), bf16[32,24,256]{2,1,0:T(8,128)(2,1)S(1)}, u32[]{:S(2)}, u32[]{:S(2)}) async-start(bf16[32,24,256]{2,1,0:T(8,128)(2,1)} %copy.65), calls=%async_computation.1 | async-start | bytes 786432 | tf_op jit(solution)/shard_map/all_to_all | solution.py:251
  108.8 2.2 %collective-permute-start.9 = (f32[1,1,1,1,1,1,4,2048]{7,6,5,4,3,2,1,0:T(4,128)S(1)}, f32[1,1,1,1,1,1,4,2048]{7,6,5,4,3,2,1,0:T(4,128)S(1)}, u32[]{:S(2)}, u32[]{:S(2)}) collective-permute-start(f32[1,1,1,1,1,1,4,2048]{7,6,5,4,3,2,1,0:T(4,128)S(1)} %slice_select_fusion.5), channel_id=1, source_target_pairs={{0,8},{1,9},{2,10},{3,11},{4,12},{5,13},{6,14},{7,15},{8,0},{9,1},... | collective-permute-start | bytes 98312 | tf_op jit(solution)/shard_map/ppermute | solution.py:58
  111.0 5.1 %all-to-all-done.1 = bf16[32,24,256]{2,1,0:T(8,128)(2,1)S(1)} async-done(((bf16[32,24,256]{2,1,0:T(8,128)(2,1)}), bf16[32,24,256]{2,1,0:T(8,128)(2,1)S(1)}, u32[]{:S(2)}, u32[]{:S(2)}) %all-to-all-start.1) | async-done | bytes 393248 | tf_op jit(solution)/shard_map/all_to_all | solution.py:251
  116.2 0.6 collective-permute-done.9
  116.7 0.7 broadcast_in_dim.73
  117.4 4.7 %all-to-all-start.2 = ((f32[4,4,2048]{2,1,0:T(4,128)}), f32[4,4,2048]{2,1,0:T(4,128)S(1)}, u32[]{:S(2)}, u32[]{:S(2)}) async-start(f32[4,4,2048]{2,1,0:T(4,128)} %broadcast_in_dim.73), calls=%async_computation.2 | async-start | bytes 262144 | tf_op jit(solution)/shard_map/all_to_all | solution.py:65
  122.2 1.9 %collective-permute-start.3 = (bf16[8,2,24,256]{3,0,2,1:T(8,128)(2,1)S(1)}, bf16[8,2,24,256]{3,0,2,1:T(8,128)(2,1)S(1)}, u32[]{:S(2)}, u32[]{:S(2)}) collective-permute-start(bf16[8,2,24,256]{3,0,2,1:T(8,128)(2,1)S(1)} %get-tuple-element.29), channel_id=1, source_target_pairs={{1,0},{2,1},{3,2},{4,3},{5,4},{6,5},{7,6},{8,7},{9,8},{10,9},{11,1... | collective-permute-start | bytes 589832 | tf_op jit(solution)/shard_map/ppermute | solution.py:89
  124.1 2.4 %collective-permute-start.2 = (bf16[8,2,24,256]{3,0,2,1:T(8,128)(2,1)S(1)}, bf16[8,2,24,256]{3,0,2,1:T(8,128)(2,1)S(1)}, u32[]{:S(2)}, u32[]{:S(2)}) collective-permute-start(bf16[8,2,24,256]{3,0,2,1:T(8,128)(2,1)S(1)} %get-tuple-element.28), channel_id=1, source_target_pairs={{0,1},{1,2},{2,3},{3,4},{4,5},{5,6},{6,7},{7,8},{8,9},{9,10},{10,1... | collective-permute-start | bytes 589832 | tf_op jit(solution)/shard_map/ppermute | solution.py:87
  126.5 1.6 %all-to-all-done.2 = f32[4,4,2048]{2,1,0:T(4,128)S(1)} async-done(((f32[4,4,2048]{2,1,0:T(4,128)}), f32[4,4,2048]{2,1,0:T(4,128)S(1)}, u32[]{:S(2)}, u32[]{:S(2)}) %all-to-all-start.2) | async-done | bytes 131104 | tf_op jit(solution)/shard_map/all_to_all | solution.py:65
  128.1 0.6 multiply_reduce_fusion
  128.7 1.3 broadcast_in_dim_broadcast_in_dim_broadcast_in_dim.2
  130.0 6.3 %all-to-all-start.3 = ((f32[64,1,128]{2,1,0:T(1,128)}), f32[64,1,128]{2,1,0:T(1,128)S(1)}, u32[]{:S(2)}, u32[]{:S(2)}) async-start(f32[64,1,128]{2,1,0:T(1,128)} %broadcast_in_dim_broadcast_in_dim_broadcast_in_dim.2), calls=%async_computation.3 | async-start | bytes 65536 | tf_op jit(solution)/shard_map/all_to_all | solution.py:65
  136.5 1.7 %gather_fusion.1 = bf16[8,4,24,256]{3,0,2,1:T(8,128)(2,1)S(1)} fusion(bf16[8,8,28,256]{3,0,2,1:T(8,128)(2,1)S(1)} %select_maximum_fusion, s32[8]{0:T(128)S(1)} %get-tuple-element.32), kind=kCustom, calls=%fused_computation.1 | custom fusion | bytes 786560 | tf_op jit(solution)/shard_map/vmap()/gather | solution.py:104
  138.2 0.8 copy.68
  139.0 5.9 %all-to-all-done.3 = f32[64,1,128]{2,1,0:T(1,128)S(1)} async-done(((f32[64,1,128]{2,1,0:T(1,128)}), f32[64,1,128]{2,1,0:T(1,128)S(1)}, u32[]{:S(2)}, u32[]{:S(2)}) %all-to-all-start.3) | async-done | bytes 32800 | tf_op jit(solution)/shard_map/all_to_all | solution.py:65
  145.2 0.6 slice.532
  145.8 0.6 slice.533
  (42 shorter events, 0.9 us)
Async XLA Ops:
  0.6 34.5 %copy-start = (bf16[2,256,768]{2,1,0:T(8,128)(2,1)S(1)}, bf16[2,256,768]{2,1,0:T(8,128)(2,1)}, u32[]{:S(2)}) copy-start(bf16[2,256,768]{2,1,0:T(8,128)(2,1)} %param.11) | copy-start | bytes 2359300
  0.6 10.5 %copy-start.2 = (bf16[8,4,24,256]{3,2,1,0:T(8,128)(2,1)S(1)}, bf16[8,4,24,256]{3,2,1,0:T(8,128)(2,1)}, u32[]{:S(2)}) copy-start(bf16[8,4,24,256]{3,2,1,0:T(8,128)(2,1)} %param.13) | copy-start | bytes 1179652
  0.7 10.7 %copy-start.4 = (s32[32,2]{0,1:T(2,128)S(1)}, s32[32,2]{0,1:T(2,128)}, u32[]{:S(2)}) copy-start(s32[32,2]{0,1:T(2,128)} %param.10) | copy-start | bytes 772
  2.0 10.3 %collective-permute-start.1 = (bf16[8,2,24,256]{3,0,2,1:T(8,128)(2,1)S(1)}, bf16[8,2,24,256]{3,0,2,1:T(8,128)(2,1)S(1)}, u32[]{:S(2)}, u32[]{:S(2)}) collective-permute-start(bf16[8,2,24,256]{3,0,2,1:T(8,128)(2,1)S(1)} %get-tuple-element.31), channel_id=1, source_target_pairs={{1,0},{2,1},{3,2},{4,3},{5,4},{6,5},{7,6},{8,7},{9,8},{10,9},{11,1... | collective-permute-start | bytes 589832 | tf_op jit(solution)/shard_map/ppermute | solution.py:89
  9.2 9.1 %collective-permute-start = (bf16[8,2,24,256]{3,0,2,1:T(8,128)(2,1)S(1)}, bf16[8,2,24,256]{3,0,2,1:T(8,128)(2,1)S(1)}, u32[]{:S(2)}, u32[]{:S(2)}) collective-permute-start(bf16[8,2,24,256]{3,0,2,1:T(8,128)(2,1)S(1)} %get-tuple-element.30), channel_id=1, source_target_pairs={{0,1},{1,2},{2,3},{3,4},{4,5},{5,6},{6,7},{7,8},{8,9},{9,10},{10,1... | collective-permute-start | bytes 589832 | tf_op jit(solution)/shard_map/ppermute | solution.py:87
  20.1 5.4 %copy-start.5 = (s32[32]{0:T(128)S(1)}, s32[32]{0:T(128)}, u32[]{:S(2)}) copy-start(s32[32]{0:T(128)} %param.8) | copy-start | bytes 388
  20.1 5.5 %copy-start.6 = (s32[32]{0:T(128)S(1)}, s32[32]{0:T(128)}, u32[]{:S(2)}) copy-start(s32[32]{0:T(128)} %param.9) | copy-start | bytes 388
  21.1 14.0 %all-to-all-start = ((bf16[8,96,512]{2,0,1:T(8,128)(2,1)}), bf16[8,96,512]{2,0,1:T(8,128)(2,1)S(1)}, u32[]{:S(2)}, u32[]{:S(2)}) async-start(bf16[8,96,512]{2,0,1:T(8,128)(2,1)} %pad_maximum_fusion), calls=%async_computation | async-start | bytes 1572864 | tf_op jit(solution)/shard_map/all_to_all | solution.py:217
  35.1 0.9 copy-start.1
  35.1 1.2 copy-start.3
  62.7 2.4 %copy-start.8 = (bf16[24,32,256]{2,1,0:T(8,128)(2,1)S(1)}, bf16[24,32,256]{2,1,0:T(8,128)(2,1)}, u32[]{:S(2)}) copy-start(bf16[24,32,256]{2,1,0:T(8,128)(2,1)} %get-tuple-element.6) | copy-start | bytes 1179652
  73.3 3.0 %collective-permute-start.4 = (f32[2,2,2,2,2,1,4,2048]{7,6,5,4,3,2,1,0:T(4,128)}, f32[2,2,2,2,2,1,4,2048]{7,6,5,4,3,2,1,0:T(4,128)}, u32[]{:S(2)}, u32[]{:S(2)}) collective-permute-start(f32[2,2,2,2,2,1,4,2048]{7,6,5,4,3,2,1,0:T(4,128)} %slice_select_fusion), channel_id=1, source_target_pairs={{0,1},{1,0},{2,3},{3,2},{4,5},{5,4},{6,7},{7,6},{8,9},{9,8},{10,11... | collective-permute-start | bytes 3145736 | tf_op jit(solution)/shard_map/ppermute | solution.py:58
  78.5 9.3 %collective-permute-start.5 = (f32[2,2,2,2,1,1,4,2048]{7,6,5,4,3,2,1,0:T(4,128)S(1)}, f32[2,2,2,2,1,1,4,2048]{7,6,5,4,3,2,1,0:T(4,128)S(1)}, u32[]{:S(2)}, u32[]{:S(2)}) collective-permute-start(f32[2,2,2,2,1,1,4,2048]{7,6,5,4,3,2,1,0:T(4,128)S(1)} %slice_select_fusion.1), channel_id=1, source_target_pairs={{0,2},{1,17},{2,0},{3,19},{4,6},{5,21},{6,4},{7,23},{8,10},{9,25},... | collective-permute-start | bytes 1572872 | tf_op jit(solution)/shard_map/ppermute | solution.py:58
  78.6 9.5 %copy-start.7 = (bf16[2,24,32,768]{3,2,1,0:T(8,128)(2,1)S(1)}, bf16[2,24,32,768]{3,2,1,0:T(8,128)(2,1)}, u32[]{:S(2)}) copy-start(bf16[2,24,32,768]{3,2,1,0:T(8,128)(2,1)} %get-tuple-element.5) | copy-start | bytes 7077892
  88.0 6.5 %collective-permute-start.6 = (f32[2,1,2,2,1,1,4,2048]{7,6,5,4,3,2,1,0:T(4,128)S(1)}, f32[2,1,2,2,1,1,4,2048]{7,6,5,4,3,2,1,0:T(4,128)S(1)}, u32[]{:S(2)}, u32[]{:S(2)}) collective-permute-start(f32[2,1,2,2,1,1,4,2048]{7,6,5,4,3,2,1,0:T(4,128)S(1)} %slice_select_fusion.2), channel_id=1, source_target_pairs={{0,16},{1,3},{2,18},{3,1},{4,20},{5,7},{6,22},{7,5},{8,24},{9,11},... | collective-permute-start | bytes 786440 | tf_op jit(solution)/shard_map/ppermute | solution.py:58
  94.6 7.0 %collective-permute-start.7 = (f32[2,1,2,1,1,1,4,2048]{7,6,5,4,3,2,1,0:T(4,128)S(1)}, f32[2,1,2,1,1,1,4,2048]{7,6,5,4,3,2,1,0:T(4,128)S(1)}, u32[]{:S(2)}, u32[]{:S(2)}) collective-permute-start(f32[2,1,2,1,1,1,4,2048]{7,6,5,4,3,2,1,0:T(4,128)S(1)} %slice_select_fusion.3), channel_id=1, source_target_pairs={{0,4},{1,33},{2,6},{3,35},{4,0},{5,37},{6,2},{7,39},{8,12},{9,41},... | collective-permute-start | bytes 393224 | tf_op jit(solution)/shard_map/ppermute | solution.py:58
  101.7 7.1 %collective-permute-start.8 = (f32[1,1,2,1,1,1,4,2048]{7,6,5,4,3,2,1,0:T(4,128)S(1)}, f32[1,1,2,1,1,1,4,2048]{7,6,5,4,3,2,1,0:T(4,128)S(1)}, u32[]{:S(2)}, u32[]{:S(2)}) collective-permute-start(f32[1,1,2,1,1,1,4,2048]{7,6,5,4,3,2,1,0:T(4,128)S(1)} %slice_select_fusion.4), channel_id=1, source_target_pairs={{0,32},{1,5},{2,34},{3,7},{4,36},{5,1},{6,38},{7,3},{8,40},{9,13},... | collective-permute-start | bytes 196616 | tf_op jit(solution)/shard_map/ppermute | solution.py:58
  105.3 10.8 %all-to-all-start.1 = ((bf16[32,24,256]{2,1,0:T(8,128)(2,1)}), bf16[32,24,256]{2,1,0:T(8,128)(2,1)S(1)}, u32[]{:S(2)}, u32[]{:S(2)}) async-start(bf16[32,24,256]{2,1,0:T(8,128)(2,1)} %copy.65), calls=%async_computation.1 | async-start | bytes 786432 | tf_op jit(solution)/shard_map/all_to_all | solution.py:251
  108.8 7.9 %collective-permute-start.9 = (f32[1,1,1,1,1,1,4,2048]{7,6,5,4,3,2,1,0:T(4,128)S(1)}, f32[1,1,1,1,1,1,4,2048]{7,6,5,4,3,2,1,0:T(4,128)S(1)}, u32[]{:S(2)}, u32[]{:S(2)}) collective-permute-start(f32[1,1,1,1,1,1,4,2048]{7,6,5,4,3,2,1,0:T(4,128)S(1)} %slice_select_fusion.5), channel_id=1, source_target_pairs={{0,8},{1,9},{2,10},{3,11},{4,12},{5,13},{6,14},{7,15},{8,0},{9,1},... | collective-permute-start | bytes 98312 | tf_op jit(solution)/shard_map/ppermute | solution.py:58
  117.4 10.7 %all-to-all-start.2 = ((f32[4,4,2048]{2,1,0:T(4,128)}), f32[4,4,2048]{2,1,0:T(4,128)S(1)}, u32[]{:S(2)}, u32[]{:S(2)}) async-start(f32[4,4,2048]{2,1,0:T(4,128)} %broadcast_in_dim.73), calls=%async_computation.2 | async-start | bytes 262144 | tf_op jit(solution)/shard_map/all_to_all | solution.py:65
  122.2 14.2 %collective-permute-start.3 = (bf16[8,2,24,256]{3,0,2,1:T(8,128)(2,1)S(1)}, bf16[8,2,24,256]{3,0,2,1:T(8,128)(2,1)S(1)}, u32[]{:S(2)}, u32[]{:S(2)}) collective-permute-start(bf16[8,2,24,256]{3,0,2,1:T(8,128)(2,1)S(1)} %get-tuple-element.29), channel_id=1, source_target_pairs={{1,0},{2,1},{3,2},{4,3},{5,4},{6,5},{7,6},{8,7},{9,8},{10,9},{11,1... | collective-permute-start | bytes 589832 | tf_op jit(solution)/shard_map/ppermute | solution.py:89
  124.1 12.3 %collective-permute-start.2 = (bf16[8,2,24,256]{3,0,2,1:T(8,128)(2,1)S(1)}, bf16[8,2,24,256]{3,0,2,1:T(8,128)(2,1)S(1)}, u32[]{:S(2)}, u32[]{:S(2)}) collective-permute-start(bf16[8,2,24,256]{3,0,2,1:T(8,128)(2,1)S(1)} %get-tuple-element.28), channel_id=1, source_target_pairs={{0,1},{1,2},{2,3},{3,4},{4,5},{5,6},{6,7},{7,8},{8,9},{9,10},{10,1... | collective-permute-start | bytes 589832 | tf_op jit(solution)/shard_map/ppermute | solution.py:87
  130.0 14.9 %all-to-all-start.3 = ((f32[64,1,128]{2,1,0:T(1,128)}), f32[64,1,128]{2,1,0:T(1,128)S(1)}, u32[]{:S(2)}, u32[]{:S(2)}) async-start(f32[64,1,128]{2,1,0:T(1,128)} %broadcast_in_dim_broadcast_in_dim_broadcast_in_dim.2), calls=%async_computation.3 | async-start | bytes 65536 | tf_op jit(solution)/shard_map/all_to_all | solution.py:65
